TPU v7x, 32 devices: a whole 2x2x4 slice. The times are simulated.
32 devices in a mesh: row: 4 (over y, core), col: 8 (over z, x).
Axes of the slice: x: 2, y: 2, z: 4, core: 2. Of those that a mesh axis runs over, the one named last changes fastest.
Arguments:
- tokens: bfloat16 [1024, 16384], P('col', 'row'), may hold values from -6 to 6
- gate_weight: bfloat16 [16384, 26624], P('row', 'col'), may hold values from -0.046875 to 0.046875
- up_weight: bfloat16 [16384, 26624], P('row', 'col'), may hold values from -0.046875 to 0.046875
Outputs:
- hidden: bfloat16 [1024, 26624], P('row', 'col')
All inputs are finite; a program needn't handle non-finite values.
Results may differ from a plain program's by a relative error of at most 0.02.
Values may be sent and summed in bfloat16 or wider, within the bound.
No kernel may reach another device: no remote copies, remote signals or barrier semaphores. Data moves between devices by JAX's collectives and lax.ppermute only.
A program may use at most 192 MiB of HBM per device.

v0:
```python
import jax
import jax.numpy as jnp
from jax import lax
from jax.sharding import PartitionSpec as P


def on_device(tokens, gate_weight, up_weight):
    gathered = lax.all_gather(tokens, "col", axis=0, tiled=True)
    units = gate_weight.shape[1]
    gate_term = jnp.dot(gathered, gate_weight, preferred_element_type=jnp.float32)
    up_term = jnp.dot(gathered, up_weight, preferred_element_type=jnp.float32)
    summed = lax.psum_scatter(
        jnp.concatenate([gate_term, up_term], axis=1).astype(jnp.bfloat16),
        "row",
        scatter_dimension=0,
        tiled=True,
    ).astype(jnp.float32)
    gate = summed[:, :units]
    upper = summed[:, units:]
    return (jax.nn.silu(gate) * upper).astype(jnp.bfloat16)


def solution(mesh):
    placed = (P("col", "row"), P("row", "col"), P("row", "col"))
    return jax.shard_map(
        on_device, mesh=mesh, in_specs=placed, out_specs=P("row", "col"), check_vma=False
    )
```

profile of v0, /device:TPU:0, one launch (start us, length us, event | category | flops | bytes accessed | tf_op | source)
XLA Modules:
  0.0 333.6 jit_solution(17927107680310670530)
XLA Ops:
  6.5 0.0 all-gather.2.cloned.1.call-start
  6.5 0.7 all-gather.2.cloned.1.call-update
  7.3 0.0 reduce-scatter.2.cloned.1.call-start
  7.3 129.4 %all-gather.2.cloned.1.call-done = bf16[1024,4096]{1,0:T(8,128)(2,1)} async-done(((bf16[128,4096]{1,0:T(8,128)(2,1)}), bf16[1024,4096]{1,0:T(8,128)(2,1)}) %all-gather.2.cloned.1.call-update) | async-done | bytes 8388624 | tf_op jit(solution)/shard_map/all_gather | solution.py:8
  136.7 0.0 copy-start
  136.7 37.2 %convolution_convert_fusion = bf16[1024,3328]{1,0:T(8,128)(2,1)S(1)} fusion(bf16[1024,4096]{1,0:T(8,128)(2,1)} %all-gather.2.cloned.1.call-done, bf16[4096,3328]{1,0:T(8,128)(2,1)} %param.5), kind=kOutput, calls=%fused_computation.1 | convolution fusion | flops 27920695296 | bytes 42467328 | tf_op jit(solution)/shard_map/dot_general | solution.py:11
  173.9 0.0 copy-done
  173.9 33.8 %convolution_convert_fusion.1 = bf16[1024,3328]{1,0:T(8,128)(2,1)S(1)} fusion(bf16[1024,4096]{1,0:T(8,128)(2,1)S(1)} %copy-done, bf16[4096,3328]{1,0:T(8,128)(2,1)} %param.4), kind=kOutput, calls=%fused_computation.2 | convolution fusion | flops 27920695296 | bytes 42467328 | tf_op jit(solution)/shard_map/dot_general | solution.py:10
  207.7 9.0 %pad_maximum_fusion = bf16[1024,6656]{1,0:T(8,128)(2,1)} fusion(bf16[1024,3328]{1,0:T(8,128)(2,1)S(1)} %convolution_convert_fusion, bf16[1024,3328]{1,0:T(8,128)(2,1)S(1)} %convolution_convert_fusion.1), kind=kLoop, calls=%fused_computation | loop fusion | flops 27262976 | bytes 27262976 | tf_op jit(solution)/shard_map/concatenate | solution.py:13
  216.6 0.0 reduce-scatter.2.cloned.1.call-update
  216.6 105.1 %reduce-scatter.2.cloned.1.call-done = bf16[256,6656]{1,0:T(8,128)(2,1)} async-done(((bf16[1024,6656]{1,0:T(8,128)(2,1)}), bf16[256,6656]{1,0:T(8,128)(2,1)}) %reduce-scatter.2.cloned.1.call-update) | async-done | bytes 3407888 | tf_op jit(solution)/shard_map/reduce_scatter | solution.py:12
  321.8 2.7 convert_element_type.7
  324.5 2.2 fusion
Async XLA Ops:
  6.5 130.1 %all-gather.2.cloned.1.call-start = ((), (), s32[]{:S(2)}) async-start(), calls=%async_computation.1 | async-start | bytes 9437184 | tf_op jit(solution)/shard_map/all_gather | solution.py:8
  7.3 314.5 %reduce-scatter.2.cloned.1.call-start = ((), (), s32[]{:S(2)}) async-start(), calls=%async_computation.2 | async-start | bytes 17039360 | tf_op jit(solution)/shard_map/reduce_scatter | solution.py:12
  136.7 37.2 %copy-start = (bf16[1024,4096]{1,0:T(8,128)(2,1)S(1)}, bf16[1024,4096]{1,0:T(8,128)(2,1)}, u32[]{:S(2)}) copy-start(bf16[1024,4096]{1,0:T(8,128)(2,1)} %all-gather.2.cloned.1.call-done) | copy-start | bytes 25165828
Sparse Core Ops, SparseCore 0:
  9.5 127.1 all-gather.1
  216.8 104.9 reduce-scatter.1
where the time goes:
time: 334 us
  waiting for transfers between devices  235 us (70%)
  matrix products  70.9 us (21%)
  other arithmetic  13.9 us (4%)
  between operations  13.4 us (4%)
    all_gather x1, waiting for transfers between devices, on_device(): gathered = lax.all_gather(tokens, 'col', axis=0, tiled=True)  129 us
    reduce_scatter x1, waiting for transfers between devices, on_device(): lax.psum_scatter(jnp.concatenate([gate_term, up_term], axis=1).astype(jnp...  105 us
    dot_general x1, matrix products, on_device(): up_term = jnp.dot(gathered, up_weight, preferred_element_type=jnp.float32)  37.2 us
    dot_general x1, matrix products, on_device(): jnp.dot(gathered, gate_weight, preferred_element_type=jnp.float32)  33.8 us
    concatenate x1, other arithmetic, on_device(): jnp.concatenate([gate_term, up_term], axis=1).astype(jnp.bfloat16)  8.96 us
  transfers between devices with their start and end apart: 2, of which 2 were waited for; matrix products, arithmetic and copies ran while one was open for 0% of the time, Pallas kernels for 0%

commit v1 on v0

v1 whole, which is shorter than its diff:
```python
import jax
import jax.numpy as jnp
from jax import lax
from jax.sharding import PartitionSpec as P

CHUNKS = 4


def reduce_rows(part, n_row):
    r = lax.axis_index("row")
    cur = part
    d = 1
    while d < n_row:
        m = cur.shape[0] // (n_row // d)
        x4 = cur.reshape(n_row // (2 * d), 2, m, cur.shape[1])
        bit = (r // d) % 2
        keep = lax.dynamic_index_in_dim(x4, bit, axis=1, keepdims=False)
        send = lax.dynamic_index_in_dim(x4, 1 - bit, axis=1, keepdims=False)
        got = lax.ppermute(
            send.astype(jnp.bfloat16), "row", [(i, i ^ d) for i in range(n_row)]
        )
        cur = (keep.astype(jnp.float32) + got.astype(jnp.float32)).reshape(-1, cur.shape[1])
        d *= 2
    return cur


def make_on_device(n_row, n_col):
    def on_device(tokens, gate_weight, up_weight):
        local = tokens.shape[0]
        tc = local // CHUNKS
        group = n_col // n_row
        gates, ups = [], []
        for i in range(CHUNKS):
            piece = lax.all_gather(tokens[i * tc:(i + 1) * tc], "col", axis=0, tiled=True)
            g = jnp.dot(piece, gate_weight, preferred_element_type=jnp.float32).astype(jnp.bfloat16)
            u = jnp.dot(piece, up_weight, preferred_element_type=jnp.float32).astype(jnp.bfloat16)
            gates.append(reduce_rows(g, n_row))
            ups.append(reduce_rows(u, n_row))
        units = gate_weight.shape[1]

        def assemble(parts):
            x = jnp.stack(parts).reshape(CHUNKS, group, tc, units)
            return x.transpose(1, 0, 2, 3).reshape(group * CHUNKS * tc, units)

        gate = assemble(gates)
        up = assemble(ups)
        return (jax.nn.silu(gate) * up).astype(jnp.bfloat16)

    return on_device


def solution(mesh):
    placed = (P("col", "row"), P("row", "col"), P("row", "col"))
    fn = make_on_device(mesh.shape["row"], mesh.shape["col"])
    return jax.shard_map(
        fn, mesh=mesh, in_specs=placed, out_specs=P("row", "col"), check_vma=False
    )
```

time: 334 us -> 332 us (level)
  waiting for transfers between devices: 235 us -> 163 us
  matrix products: 70.9 us -> 120 us
  local copies, waits for them, and re-layouts: 0.01 us -> 13.4 us
  starting transfers between devices: 0.04 us -> 12 us
    reduce_scatter x1 -> x0, waiting for transfers between devices: 105 us -> none  [on_device(): lax.psum_scatter(jnp.concatenate([gate_term, up_term], axis=1).astype(jnp...]
    ppermute x0 -> x16, waiting for transfers between devices: none -> 60.7 us  [reduce_rows(): lax.ppermute(send.astype(jnp.bfloat16), 'row', [(i, i ^ d) for i in range...]
    dot_general x2 -> x8, matrix products: 70.9 us -> 120 us  [the longest x4 64.4 us: on_device(): jnp.dot(piece, up_weight, preferred_element_type=jnp.float32)]
    all_gather x1 -> x4, waiting for transfers between devices: 129 us -> 100 us  [on_device(): lax.all_gather(tokens[i * tc:(i + 1) * tc], 'col', axis=0, tiled=True)]
    ppermute x0 -> x16, starting transfers between devices: none -> 11.8 us  [reduce_rows(): lax.ppermute(send.astype(jnp.bfloat16), 'row', [(i, i ^ d) for i in range...]
    concatenate x1 -> x0, other arithmetic: 8.96 us -> none  [on_device(): jnp.concatenate([gate_term, up_term], axis=1).astype(jnp.bfloat16)]
    add x0 -> x16, other arithmetic: none -> 7.96 us  [reduce_rows(): keep.astype(jnp.float32) + got.astype(jnp.float32)]
    squeeze x0 -> x8, local copies, waits for them, and re-layouts: none -> 6.22 us  [reduce_rows(): send = lax.dynamic_index_in_dim(x4, 1 - bit, axis=1, keepdims=False)]
  transfers between devices with their start and end apart: 2 -> 20, of which waited for: 2 -> 12; matrix products, arithmetic and copies ran while one was open for 0% -> 41% of each run, Pallas kernels for 0% -> 0%
where the time goes in v1:
time: 332 us
  waiting for transfers between devices  163 us (49%)
  matrix products  120 us (36%)
  between operations  13.6 us (4%)
  local copies, waits for them, and re-layouts  13.4 us (4%)
  starting transfers between devices  12 us (4%)
  other arithmetic  10.7 us (3%)
    all_gather x4, waiting for transfers between devices, on_device(): lax.all_gather(tokens[i * tc:(i + 1) * tc], 'col', axis=0, tiled=True)  100 us
    dot_general x4, matrix products, on_device(): jnp.dot(piece, up_weight, preferred_element_type=jnp.float32)  64.4 us
    ppermute x16, waiting for transfers between devices, reduce_rows(): lax.ppermute(send.astype(jnp.bfloat16), 'row', [(i, i ^ d) for i in range...  60.7 us
    dot_general x4, matrix products, on_device(): jnp.dot(piece, gate_weight, preferred_element_type=jnp.float32)  55.2 us
    ppermute x16, starting transfers between devices, reduce_rows(): lax.ppermute(send.astype(jnp.bfloat16), 'row', [(i, i ^ d) for i in range...  11.8 us
    add x16, other arithmetic, reduce_rows(): keep.astype(jnp.float32) + got.astype(jnp.float32)  7.96 us
  transfers between devices with their start and end apart: 20, of which 12 were waited for; matrix products, arithmetic and copies ran while one was open for 41% of the time, Pallas kernels for 0%

profile of v1, /device:TPU:0, one launch (start us, length us, event | category | flops | bytes accessed | tf_op | source)
XLA Modules:
  0.0 332.2 jit_solution(17534015869885583482)
XLA Ops:
  6.5 2.2 fusion.4
  10.8 50.5 %all-gather.9.cloned.1.call-done = bf16[256,4096]{1,0:T(8,128)(2,1)} async-done(((bf16[32,4096]{1,0:T(8,128)(2,1)}), bf16[256,4096]{1,0:T(8,128)(2,1)}) %all-gather.9.cloned.1.call-update) | async-done | bytes 2097168 | tf_op jit(solution)/shard_map/all_gather | solution.py:34
  61.3 17.3 %convolution_convert_fusion.1 = bf16[256,3328]{1,0:T(8,128)(2,1)S(1)} fusion(bf16[256,4096]{1,0:T(8,128)(2,1)} %all-gather.9.cloned.1.call-done, bf16[4096,3328]{1,0:T(8,128)(2,1)} %param.5), kind=kOutput, calls=%fused_computation.1 | convolution fusion | flops 6980173824 | bytes 31064064 | tf_op jit(solution)/shard_map/dot_general | solution.py:36
  79.7 12.7 %convolution_convert_fusion.5 = bf16[256,3328]{1,0:T(8,128)(2,1)S(1)} fusion(bf16[256,4096]{1,0:T(8,128)(2,1)S(1)} %copy-done.12, bf16[4096,3328]{1,0:T(8,128)(2,1)} %param.4), kind=kOutput, calls=%fused_computation.5 | convolution fusion | flops 6980173824 | bytes 31064064 | tf_op jit(solution)/shard_map/dot_general | solution.py:35
  95.0 16.0 %all-gather.11.cloned.1.call-done = bf16[256,4096]{1,0:T(8,128)(2,1)} async-done(((bf16[32,4096]{1,0:T(8,128)(2,1)}), bf16[256,4096]{1,0:T(8,128)(2,1)}) %all-gather.11.cloned.1.call-update) | async-done | bytes 2097168 | tf_op jit(solution)/shard_map/all_gather | solution.py:34
  111.1 17.2 %convolution_convert_fusion = bf16[256,3328]{1,0:T(8,128)(2,1)S(1)} fusion(bf16[256,4096]{1,0:T(8,128)(2,1)} %all-gather.11.cloned.1.call-done, bf16[4096,3328]{1,0:T(8,128)(2,1)} %param.5), kind=kOutput, calls=%fused_computation | convolution fusion | flops 6980173824 | bytes 31064064 | tf_op jit(solution)/shard_map/dot_general | solution.py:36
  129.3 12.7 %convolution_convert_fusion.4 = bf16[256,3328]{1,0:T(8,128)(2,1)S(1)} fusion(bf16[256,4096]{1,0:T(8,128)(2,1)S(1)} %copy-done.11, bf16[4096,3328]{1,0:T(8,128)(2,1)} %param.4), kind=kOutput, calls=%fused_computation.4 | convolution fusion | flops 6980173824 | bytes 31064064 | tf_op jit(solution)/shard_map/dot_general | solution.py:35
  144.6 16.2 %all-gather.7.cloned.1.call-done = bf16[256,4096]{1,0:T(8,128)(2,1)} async-done(((bf16[32,4096]{1,0:T(8,128)(2,1)}), bf16[256,4096]{1,0:T(8,128)(2,1)}) %all-gather.7.cloned.1.call-update) | async-done | bytes 2097168 | tf_op jit(solution)/shard_map/all_gather | solution.py:34
  160.9 17.3 %convolution_convert_fusion.6 = bf16[256,3328]{1,0:T(8,128)(2,1)S(1)} fusion(bf16[256,4096]{1,0:T(8,128)(2,1)} %all-gather.7.cloned.1.call-done, bf16[4096,3328]{1,0:T(8,128)(2,1)} %param.4), kind=kOutput, calls=%fused_computation.6 | convolution fusion | flops 6980173824 | bytes 31064064 | tf_op jit(solution)/shard_map/dot_general | solution.py:35
  179.2 12.7 %convolution_convert_fusion.2 = bf16[256,3328]{1,0:T(8,128)(2,1)S(1)} fusion(bf16[256,4096]{1,0:T(8,128)(2,1)S(1)} %copy-done.9, bf16[4096,3328]{1,0:T(8,128)(2,1)} %param.5), kind=kOutput, calls=%fused_computation.2 | convolution fusion | flops 6980173824 | bytes 31064064 | tf_op jit(solution)/shard_map/dot_general | solution.py:36
  193.0 17.5 %all-gather.5.cloned.1.call-done = bf16[256,4096]{1,0:T(8,128)(2,1)} async-done(((bf16[32,4096]{1,0:T(8,128)(2,1)}), bf16[256,4096]{1,0:T(8,128)(2,1)}) %all-gather.5.cloned.1.call-update) | async-done | bytes 2097168 | tf_op jit(solution)/shard_map/all_gather | solution.py:34
  210.5 17.2 %convolution_convert_fusion.3 = bf16[256,3328]{1,0:T(8,128)(2,1)S(1)} fusion(bf16[256,4096]{1,0:T(8,128)(2,1)} %all-gather.5.cloned.1.call-done, bf16[4096,3328]{1,0:T(8,128)(2,1)} %param.5), kind=kOutput, calls=%fused_computation.3 | convolution fusion | flops 6980173824 | bytes 31064064 | tf_op jit(solution)/shard_map/dot_general | solution.py:36
  227.8 12.6 %convolution_convert_fusion.7 = bf16[256,3328]{1,0:T(8,128)(2,1)S(1)} fusion(bf16[256,4096]{1,0:T(8,128)(2,1)S(1)} %copy-done.10, bf16[4096,3328]{1,0:T(8,128)(2,1)} %param.4), kind=kOutput, calls=%fused_computation.7 | convolution fusion | flops 6980173824 | bytes 31064064 | tf_op jit(solution)/shard_map/dot_general | solution.py:35
  247.0 1.5 collective-permute-start.5
  252.0 1.5 collective-permute-start.7
  256.5 3.3 collective-permute-done.5
  261.3 7.6 %collective-permute-done.13 = bf16[1,64,3328]{2,1,0:T(8,128)(2,1)S(1)} collective-permute-done((bf16[1,64,3328]{2,1,0:T(8,128)(2,1)S(1)}, bf16[1,64,3328]{2,1,0:T(8,128)(2,1)S(1)}, u32[]{:S(2)}, u32[]{:S(2)}) %collective-permute-start.13) | collective-permute-done | bytes 426016 | tf_op jit(solution)/shard_map/ppermute | solution.py:19
  270.4 7.6 %collective-permute-done.7 = bf16[1,64,3328]{2,1,0:T(8,128)(2,1)S(1)} collective-permute-done((bf16[1,64,3328]{2,1,0:T(8,128)(2,1)S(1)}, bf16[1,64,3328]{2,1,0:T(8,128)(2,1)S(1)}, u32[]{:S(2)}, u32[]{:S(2)}) %collective-permute-start.7) | collective-permute-done | bytes 426016 | tf_op jit(solution)/shard_map/ppermute | solution.py:19
  279.6 7.6 %collective-permute-done.15 = bf16[1,64,3328]{2,1,0:T(8,128)(2,1)S(1)} collective-permute-done((bf16[1,64,3328]{2,1,0:T(8,128)(2,1)S(1)}, bf16[1,64,3328]{2,1,0:T(8,128)(2,1)S(1)}, u32[]{:S(2)}, u32[]{:S(2)}) %collective-permute-start.15) | collective-permute-done | bytes 426016 | tf_op jit(solution)/shard_map/ppermute | solution.py:19
  287.2 9.0 %collective-permute-done.3 = bf16[1,64,3328]{2,1,0:T(8,128)(2,1)S(1)} collective-permute-done((bf16[1,64,3328]{2,1,0:T(8,128)(2,1)S(1)}, bf16[1,64,3328]{2,1,0:T(8,128)(2,1)S(1)}, u32[]{:S(2)}, u32[]{:S(2)}) %collective-permute-start.3) | collective-permute-done | bytes 426016 | tf_op jit(solution)/shard_map/ppermute | solution.py:19
  296.4 9.0 %collective-permute-done.11 = bf16[1,64,3328]{2,1,0:T(8,128)(2,1)S(1)} collective-permute-done((bf16[1,64,3328]{2,1,0:T(8,128)(2,1)S(1)}, bf16[1,64,3328]{2,1,0:T(8,128)(2,1)S(1)}, u32[]{:S(2)}, u32[]{:S(2)}) %collective-permute-start.11) | collective-permute-done | bytes 426016 | tf_op jit(solution)/shard_map/ppermute | solution.py:19
  305.5 9.0 %collective-permute-done.1 = bf16[1,64,3328]{2,1,0:T(8,128)(2,1)S(1)} collective-permute-done((bf16[1,64,3328]{2,1,0:T(8,128)(2,1)S(1)}, bf16[1,64,3328]{2,1,0:T(8,128)(2,1)S(1)}, u32[]{:S(2)}, u32[]{:S(2)}) %collective-permute-start.1) | collective-permute-done | bytes 426016 | tf_op jit(solution)/shard_map/ppermute | solution.py:19
  315.2 7.6 %collective-permute-done.9 = bf16[1,64,3328]{2,1,0:T(8,128)(2,1)S(1)} collective-permute-done((bf16[1,64,3328]{2,1,0:T(8,128)(2,1)S(1)}, bf16[1,64,3328]{2,1,0:T(8,128)(2,1)S(1)}, u32[]{:S(2)}, u32[]{:S(2)}) %collective-permute-start.9) | collective-permute-done | bytes 426016 | tf_op jit(solution)/shard_map/ppermute | solution.py:19
  323.5 2.2 fusion
  (92 shorter events, 30.5 us)
Async XLA Ops:
  6.5 54.8 %all-gather.9.cloned.1.call-start = ((), (), s32[]{:S(2)}) async-start(), calls=%async_computation.2 | async-start | bytes 2359296 | tf_op jit(solution)/shard_map/all_gather | solution.py:34
  8.7 102.4 %all-gather.11.cloned.1.call-start = ((), (), s32[]{:S(2)}) async-start(), calls=%async_computation.3 | async-start | bytes 2359296 | tf_op jit(solution)/shard_map/all_gather | solution.py:34
  9.5 151.4 %all-gather.7.cloned.1.call-start = ((), (), s32[]{:S(2)}) async-start(), calls=%async_computation.1 | async-start | bytes 2359296 | tf_op jit(solution)/shard_map/all_gather | solution.py:34
  10.2 200.3 %all-gather.5.cloned.1.call-start = ((), (), s32[]{:S(2)}) async-start(), calls=%async_computation | async-start | bytes 2359296 | tf_op jit(solution)/shard_map/all_gather | solution.py:34
  61.3 18.4 %copy-start.12 = (bf16[256,4096]{1,0:T(8,128)(2,1)S(1)}, bf16[256,4096]{1,0:T(8,128)(2,1)}, u32[]{:S(2)}) copy-start(bf16[256,4096]{1,0:T(8,128)(2,1)} %all-gather.9.cloned.1.call-done) | copy-start | bytes 6291460
  94.5 146.1 %collective-permute-start.4 = (bf16[2,64,3328]{2,1,0:T(8,128)(2,1)}, bf16[2,64,3328]{2,1,0:T(8,128)(2,1)}, u32[]{:S(2)}, u32[]{:S(2)}) collective-permute-start(bf16[2,64,3328]{2,1,0:T(8,128)(2,1)} %dynamic-slice_bitcast_fusion.5), channel_id=1, source_target_pairs={{0,8},{8,0},{16,24},{24,16},{1,9},{9,1},{17,25},{25,17},{2,10},{10... | collective-permute-start | bytes 2555912 | tf_op jit(solution)/shard_map/ppermute | solution.py:19
  94.5 149.0 %collective-permute-start.12 = (bf16[2,64,3328]{2,1,0:T(8,128)(2,1)}, bf16[2,64,3328]{2,1,0:T(8,128)(2,1)}, u32[]{:S(2)}, u32[]{:S(2)}) collective-permute-start(bf16[2,64,3328]{2,1,0:T(8,128)(2,1)} %dynamic-slice_bitcast_fusion.1), channel_id=1, source_target_pairs={{0,8},{8,0},{16,24},{24,16},{1,9},{9,1},{17,25},{25,17},{2,10},{10... | collective-permute-start | bytes 2555912 | tf_op jit(solution)/shard_map/ppermute | solution.py:19
  111.1 18.2 %copy-start.11 = (bf16[256,4096]{1,0:T(8,128)(2,1)S(1)}, bf16[256,4096]{1,0:T(8,128)(2,1)}, u32[]{:S(2)}) copy-start(bf16[256,4096]{1,0:T(8,128)(2,1)} %all-gather.11.cloned.1.call-done) | copy-start | bytes 6291460
  144.1 100.9 %collective-permute-start.6 = (bf16[2,64,3328]{2,1,0:T(8,128)(2,1)}, bf16[2,64,3328]{2,1,0:T(8,128)(2,1)}, u32[]{:S(2)}, u32[]{:S(2)}) collective-permute-start(bf16[2,64,3328]{2,1,0:T(8,128)(2,1)} %dynamic-slice_bitcast_fusion.4), channel_id=1, source_target_pairs={{0,8},{8,0},{16,24},{24,16},{1,9},{9,1},{17,25},{25,17},{2,10},{10... | collective-permute-start | bytes 2555912 | tf_op jit(solution)/shard_map/ppermute | solution.py:19
  144.1 102.9 %collective-permute-start.14 = (bf16[2,64,3328]{2,1,0:T(8,128)(2,1)}, bf16[2,64,3328]{2,1,0:T(8,128)(2,1)}, u32[]{:S(2)}, u32[]{:S(2)}) collective-permute-start(bf16[2,64,3328]{2,1,0:T(8,128)(2,1)} %dynamic-slice_bitcast_fusion), channel_id=1, source_target_pairs={{0,8},{8,0},{16,24},{24,16},{1,9},{9,1},{17,25},{25,17},{2,10},{10... | collective-permute-start | bytes 2555912 | tf_op jit(solution)/shard_map/ppermute | solution.py:19
  160.9 18.4 %copy-start.9 = (bf16[256,4096]{1,0:T(8,128)(2,1)S(1)}, bf16[256,4096]{1,0:T(8,128)(2,1)}, u32[]{:S(2)}) copy-start(bf16[256,4096]{1,0:T(8,128)(2,1)} %all-gather.7.cloned.1.call-done) | copy-start | bytes 6291460
  179.2 70.6 %collective-permute-start.2 = (bf16[2,64,3328]{2,1,0:T(8,128)(2,1)}, bf16[2,64,3328]{2,1,0:T(8,128)(2,1)}, u32[]{:S(2)}, u32[]{:S(2)}) collective-permute-start(bf16[2,64,3328]{2,1,0:T(8,128)(2,1)} %dynamic-slice_bitcast_fusion.6), channel_id=1, source_target_pairs={{0,8},{8,0},{16,24},{24,16},{1,9},{9,1},{17,25},{25,17},{2,10},{10... | collective-permute-start | bytes 2555912 | tf_op jit(solution)/shard_map/ppermute | solution.py:19
  210.5 17.3 %copy-start.10 = (bf16[256,4096]{1,0:T(8,128)(2,1)S(1)}, bf16[256,4096]{1,0:T(8,128)(2,1)}, u32[]{:S(2)}) copy-start(bf16[256,4096]{1,0:T(8,128)(2,1)} %all-gather.5.cloned.1.call-done) | copy-start | bytes 6291460
  241.6 10.4 %collective-permute-start.10 = (bf16[2,64,3328]{2,1,0:T(8,128)(2,1)S(1)}, bf16[2,64,3328]{2,1,0:T(8,128)(2,1)S(1)}, u32[]{:S(2)}, u32[]{:S(2)}) collective-permute-start(bf16[2,64,3328]{2,1,0:T(8,128)(2,1)S(1)} %copy-done.8), channel_id=1, source_target_pairs={{0,8},{8,0},{16,24},{24,16},{1,9},{9,1},{17,25},{25,17},{2,10},{10... | collective-permute-start | bytes 2555912 | tf_op jit(solution)/shard_map/ppermute | solution.py:19
  243.5 10.2 %collective-permute-start = (bf16[2,64,3328]{2,1,0:T(8,128)(2,1)S(1)}, bf16[2,64,3328]{2,1,0:T(8,128)(2,1)S(1)}, u32[]{:S(2)}, u32[]{:S(2)}) collective-permute-start(bf16[2,64,3328]{2,1,0:T(8,128)(2,1)S(1)} %dynamic-slice_bitcast_fusion.7), channel_id=1, source_target_pairs={{0,8},{8,0},{16,24},{24,16},{1,9},{9,1},{17,25},{25,17},{2,10},{10... | collective-permute-start | bytes 2555912 | tf_op jit(solution)/shard_map/ppermute | solution.py:19
  245.1 9.6 %collective-permute-start.8 = (bf16[2,64,3328]{2,1,0:T(8,128)(2,1)S(1)}, bf16[2,64,3328]{2,1,0:T(8,128)(2,1)S(1)}, u32[]{:S(2)}, u32[]{:S(2)}) collective-permute-start(bf16[2,64,3328]{2,1,0:T(8,128)(2,1)S(1)} %dynamic-slice_bitcast_fusion.3), channel_id=1, source_target_pairs={{0,8},{8,0},{16,24},{24,16},{1,9},{9,1},{17,25},{25,17},{2,10},{10... | collective-permute-start | bytes 2555912 | tf_op jit(solution)/shard_map/ppermute | solution.py:19
  247.0 12.8 %collective-permute-start.5 = (bf16[1,64,3328]{2,1,0:T(8,128)(2,1)S(1)}, bf16[1,64,3328]{2,1,0:T(8,128)(2,1)S(1)}, u32[]{:S(2)}, u32[]{:S(2)}) collective-permute-start(bf16[1,64,3328]{2,1,0:T(8,128)(2,1)S(1)} %dynamic-slice_convert_fusion.5), channel_id=1, source_target_pairs={{0,16},{8,24},{16,0},{24,8},{1,17},{9,25},{17,1},{25,9},{2,18},{10... | collective-permute-start | bytes 1277960 | tf_op jit(solution)/shard_map/ppermute | solution.py:19
  249.9 19.0 %collective-permute-start.13 = (bf16[1,64,3328]{2,1,0:T(8,128)(2,1)S(1)}, bf16[1,64,3328]{2,1,0:T(8,128)(2,1)S(1)}, u32[]{:S(2)}, u32[]{:S(2)}) collective-permute-start(bf16[1,64,3328]{2,1,0:T(8,128)(2,1)S(1)} %dynamic-slice_convert_fusion.1), channel_id=1, source_target_pairs={{0,16},{8,24},{16,0},{24,8},{1,17},{9,25},{17,1},{25,9},{2,18},{10... | collective-permute-start | bytes 1277960 | tf_op jit(solution)/shard_map/ppermute | solution.py:19
  252.0 26.0 %collective-permute-start.7 = (bf16[1,64,3328]{2,1,0:T(8,128)(2,1)S(1)}, bf16[1,64,3328]{2,1,0:T(8,128)(2,1)S(1)}, u32[]{:S(2)}, u32[]{:S(2)}) collective-permute-start(bf16[1,64,3328]{2,1,0:T(8,128)(2,1)S(1)} %dynamic-slice_convert_fusion.4), channel_id=1, source_target_pairs={{0,16},{8,24},{16,0},{24,8},{1,17},{9,25},{17,1},{25,9},{2,18},{10... | collective-permute-start | bytes 1277960 | tf_op jit(solution)/shard_map/ppermute | solution.py:19
  253.7 33.4 %collective-permute-start.15 = (bf16[1,64,3328]{2,1,0:T(8,128)(2,1)S(1)}, bf16[1,64,3328]{2,1,0:T(8,128)(2,1)S(1)}, u32[]{:S(2)}, u32[]{:S(2)}) collective-permute-start(bf16[1,64,3328]{2,1,0:T(8,128)(2,1)S(1)} %dynamic-slice_convert_fusion), channel_id=1, source_target_pairs={{0,16},{8,24},{16,0},{24,8},{1,17},{9,25},{17,1},{25,9},{2,18},{10... | collective-permute-start | bytes 1277960 | tf_op jit(solution)/shard_map/ppermute | solution.py:19
  254.7 41.6 %collective-permute-start.3 = (bf16[1,64,3328]{2,1,0:T(8,128)(2,1)S(1)}, bf16[1,64,3328]{2,1,0:T(8,128)(2,1)S(1)}, u32[]{:S(2)}, u32[]{:S(2)}) collective-permute-start(bf16[1,64,3328]{2,1,0:T(8,128)(2,1)S(1)} %dynamic-slice_convert_fusion.6), channel_id=1, source_target_pairs={{0,16},{8,24},{16,0},{24,8},{1,17},{9,25},{17,1},{25,9},{2,18},{10... | collective-permute-start | bytes 1277960 | tf_op jit(solution)/shard_map/ppermute | solution.py:19
  259.8 45.6 %collective-permute-start.11 = (bf16[1,64,3328]{2,1,0:T(8,128)(2,1)S(1)}, bf16[1,64,3328]{2,1,0:T(8,128)(2,1)S(1)}, u32[]{:S(2)}, u32[]{:S(2)}) collective-permute-start(bf16[1,64,3328]{2,1,0:T(8,128)(2,1)S(1)} %dynamic-slice_convert_fusion.2), channel_id=1, source_target_pairs={{0,16},{8,24},{16,0},{24,8},{1,17},{9,25},{17,1},{25,9},{2,18},{10... | collective-permute-start | bytes 1277960 | tf_op jit(solution)/shard_map/ppermute | solution.py:19
  268.9 45.6 %collective-permute-start.1 = (bf16[1,64,3328]{2,1,0:T(8,128)(2,1)S(1)}, bf16[1,64,3328]{2,1,0:T(8,128)(2,1)S(1)}, u32[]{:S(2)}, u32[]{:S(2)}) collective-permute-start(bf16[1,64,3328]{2,1,0:T(8,128)(2,1)S(1)} %dynamic-slice_convert_fusion.7), channel_id=1, source_target_pairs={{0,16},{8,24},{16,0},{24,8},{1,17},{9,25},{17,1},{25,9},{2,18},{10... | collective-permute-start | bytes 1277960 | tf_op jit(solution)/shard_map/ppermute | solution.py:19
  278.0 44.8 %collective-permute-start.9 = (bf16[1,64,3328]{2,1,0:T(8,128)(2,1)S(1)}, bf16[1,64,3328]{2,1,0:T(8,128)(2,1)S(1)}, u32[]{:S(2)}, u32[]{:S(2)}) collective-permute-start(bf16[1,64,3328]{2,1,0:T(8,128)(2,1)S(1)} %dynamic-slice_convert_fusion.3), channel_id=1, source_target_pairs={{0,16},{8,24},{16,0},{24,8},{1,17},{9,25},{17,1},{25,9},{2,18},{10... | collective-permute-start | bytes 1277960 | tf_op jit(solution)/shard_map/ppermute | solution.py:19
  (9 other events, 41.5 us)
Sparse Core Ops, SparseCore 0:
  9.5 51.7 all-gather.8
  63.4 47.6 all-gather.10
  113.2 47.5 all-gather.6
  162.8 47.6 all-gather.4

commit v2 on v0

v2 whole, which is shorter than its diff:
```python
import jax
import jax.numpy as jnp
import numpy as np
from jax import lax
from jax.sharding import PartitionSpec as P

HALVES = 2
SPLIT_UNITS = 2


def ring_order(mesh):
    col = mesh.devices[0]
    n = len(col)
    try:
        zs = sorted({d.coords[2] for d in col})
        xs = sorted({d.coords[0] for d in col})
        at = {(zs.index(d.coords[2]), xs.index(d.coords[0])): i for i, d in enumerate(col)}
    except Exception:
        return list(range(n))
    a, b = len(zs), len(xs)
    if a * b != n or len(at) != n or a % 2 or b < 2:
        return list(range(n))
    cells = [(z, 0) for z in range(a)]
    for k, z in enumerate(range(a - 1, -1, -1)):
        span = range(1, b) if k % 2 == 0 else range(b - 1, 0, -1)
        cells += [(z, x) for x in span]
    return [at[c] for c in cells]


class Ring:
    def __init__(self, order):
        self.order = order
        n = len(order)
        self.n = n
        pos = np.zeros(n, np.int32)
        for q, c in enumerate(order):
            pos[c] = q
        self.pos = pos
        self.fwd_pairs = [(order[q], order[(q + 1) % n]) for q in range(n)]
        self.bwd_pairs = [(order[q], order[(q - 1) % n]) for q in range(n)]
        self.steps = n // 2
        self.back_steps = n - 1 - n // 2

    def init(self, x):
        n = self.n
        c = lax.axis_index("col")
        buf = jnp.zeros((n,) + x.shape, x.dtype)
        buf = lax.dynamic_update_slice(buf, x[None], (c, 0, 0))
        return {"buf": buf, "f": x, "b": x}

    def step(self, st, s):
        n = self.n
        c = lax.axis_index("col")
        p = jnp.asarray(self.pos)[c]
        order_t = jnp.asarray(np.array(self.order, np.int32))
        buf = st["buf"]
        f = lax.ppermute(st["f"], "col", self.fwd_pairs)
        buf = lax.dynamic_update_slice(buf, f[None], (order_t[(p - s) % n], 0, 0))
        b = st["b"]
        if s <= self.back_steps:
            b = lax.ppermute(b, "col", self.bwd_pairs)
            buf = lax.dynamic_update_slice(buf, b[None], (order_t[(p + s) % n], 0, 0))
        return {"buf": buf, "f": f, "b": b}

    def result(self, st):
        buf = st["buf"]
        return buf.reshape((-1,) + buf.shape[2:])


def reduce_level(cur, d, n_row):
    r = lax.axis_index("row")
    m = cur.shape[0] // (n_row // d)
    x4 = cur.reshape(n_row // (2 * d), 2, m, cur.shape[1])
    bit = (r // d) % 2
    keep = lax.dynamic_index_in_dim(x4, bit, axis=1, keepdims=False)
    send = lax.dynamic_index_in_dim(x4, 1 - bit, axis=1, keepdims=False)
    got = lax.ppermute(send.astype(jnp.bfloat16), "row", [(i, i ^ d) for i in range(n_row)])
    return (keep.astype(jnp.float32) + got.astype(jnp.float32)).reshape(-1, cur.shape[1])


def make_on_device(n_row, n_col, order):
    ring = Ring(order)
    levels = []
    d = 1
    while d < n_row:
        levels.append(d)
        d *= 2

    def on_device(tokens, gate_weight, up_weight):
        local = tokens.shape[0]
        tc = local // HALVES
        group = n_col // n_row
        units = gate_weight.shape[1]
        us = units // SPLIT_UNITS

        st = ring.init(tokens[:tc])
        for s in range(1, ring.steps + 1):
            st = ring.step(st, s)
        piece = ring.result(st)

        tiles = []
        for h in range(HALVES):
            for w in range(2):
                for j in range(SPLIT_UNITS):
                    tiles.append((h, w, j))

        jobs = []
        done = {}
        nxt = None
        t = 0
        while t < len(tiles) or jobs:
            carry = {}
            for job in jobs:
                job[2] = reduce_level(job[2], levels[job[1]], n_row)
                job[1] += 1
            if t < len(tiles):
                h, w, j = tiles[t]
                first_of_share = t % (2 * SPLIT_UNITS) == 0
                if first_of_share and h + 1 < HALVES:
                    nxt = {"st": ring.init(tokens[(h + 1) * tc:(h + 2) * tc]), "s": 1}
                if nxt is not None and nxt["s"] <= ring.steps:
                    nxt["st"] = ring.step(nxt["st"], nxt["s"])
                    nxt["s"] += 1
                weight = gate_weight if w == 0 else up_weight
                out = jnp.dot(
                    piece, weight[:, j * us:(j + 1) * us], preferred_element_type=jnp.float32
                ).astype(jnp.bfloat16)
                new_job = [t, 0, out]
            else:
                new_job = None
            finished = [jb for jb in jobs if jb[1] == len(levels)]
            jobs = [jb for jb in jobs if jb[1] < len(levels)]
            for jb in finished:
                done[jb[0]] = jb[2]
            if new_job is not None:
                if levels:
                    jobs.append(new_job)
                else:
                    done[new_job[0]] = new_job[2].astype(jnp.float32)
            carry["piece"] = piece
            carry["jobs"] = [jb[2] for jb in jobs]
            carry["nxt"] = nxt["st"] if nxt is not None else None
            carry["done"] = done
            carry = lax.optimization_barrier(carry)
            piece = carry["piece"]
            for jb, a in zip(jobs, carry["jobs"]):
                jb[2] = a
            if nxt is not None:
                nxt["st"] = carry["nxt"]
            done = carry["done"]
            t += 1
            if t < len(tiles) and t % (2 * SPLIT_UNITS) == 0 and nxt is not None:
                while nxt["s"] <= ring.steps:
                    nxt["st"] = ring.step(nxt["st"], nxt["s"])
                    nxt["s"] += 1
                piece = ring.result(nxt["st"])
                nxt = None

        def assemble(w):
            parts = []
            for h in range(HALVES):
                base = (h * 2 + w) * SPLIT_UNITS
                parts.append(jnp.concatenate([done[base + j] for j in range(SPLIT_UNITS)], axis=1))
            x = jnp.stack(parts).reshape(HALVES, group, tc, units)
            return x.transpose(1, 0, 2, 3).reshape(group * HALVES * tc, units)

        gate = assemble(0)
        up = assemble(1)
        return (jax.nn.silu(gate) * up).astype(jnp.bfloat16)

    return on_device


def solution(mesh):
    placed = (P("col", "row"), P("row", "col"), P("row", "col"))
    fn = make_on_device(mesh.shape["row"], mesh.shape["col"], ring_order(mesh))
    return jax.shard_map(
        fn, mesh=mesh, in_specs=placed, out_specs=P("row", "col"), check_vma=False
    )
```

time: 334 us -> 204 us (0.61)
  waiting for transfers between devices: 235 us -> 47.7 us
  starting transfers between devices: 0.04 us -> 25.6 us
  matrix products: 70.9 us -> 91.3 us
  local copies, waits for them, and re-layouts: 0.01 us -> 16.1 us
  other arithmetic: 13.9 us -> 5.23 us
  between operations: 13.4 us -> 17.9 us
    all_gather x1 -> x0, waiting for transfers between devices: 129 us -> none  [on_device(): gathered = lax.all_gather(tokens, 'col', axis=0, tiled=True)]
    reduce_scatter x1 -> x0, waiting for transfers between devices: 105 us -> none  [on_device(): lax.psum_scatter(jnp.concatenate([gate_term, up_term], axis=1).astype(jnp...]
    ppermute x0 -> x30, waiting for transfers between devices: none -> 47.7 us  [the longest x8 26.7 us: step(): f = lax.ppermute(st['f'], 'col', self.fwd_pairs)]
    ppermute x0 -> x30, starting transfers between devices: none -> 25.6 us  [the longest x8 12.4 us: step(): f = lax.ppermute(st['f'], 'col', self.fwd_pairs)]
    dot_general x2 -> x8, matrix products: 70.9 us -> 91.3 us  [on_device(): jnp.dot(piece, weight[:, j * us:(j + 1) * us], preferred_element_type=jnp...]
    concatenate x1 -> x2, other arithmetic: 8.96 us -> 0.46 us  [assemble(): jnp.concatenate([done[base + j] for j in range(SPLIT_UNITS)], axis=1)]
    dynamic_update_slice x0 -> x16, local copies, waits for them, and re-layouts: none -> 6.95 us  [the longest x8 3.46 us: step(): buf = lax.dynamic_update_slice(buf, f[None], (order_t[(p - s) % n], 0, 0))]
  transfers between devices with their start and end apart: 2 -> 30, of which waited for: 2 -> 8; matrix products, arithmetic and copies ran while one was open for 0% -> 45% of each run, Pallas kernels for 0% -> 0%
where the time goes in v2:
time: 204 us
  matrix products  91.3 us (45%)
  waiting for transfers between devices  47.7 us (23%)
  starting transfers between devices  25.6 us (13%)
  between operations  17.9 us (9%)
  local copies, waits for them, and re-layouts  16.1 us (8%)
  other arithmetic  5.23 us (3%)
    dot_general x8, matrix products, on_device(): jnp.dot(piece, weight[:, j * us:(j + 1) * us], preferred_element_type=jnp...  91.3 us
    ppermute x8, waiting for transfers between devices, step(): f = lax.ppermute(st['f'], 'col', self.fwd_pairs)  26.7 us
    ppermute x16, waiting for transfers between devices, reduce_level(): lax.ppermute(send.astype(jnp.bfloat16), 'row', [(i, i ^ d) for i in range...  20.9 us
    ppermute x8, starting transfers between devices, step(): f = lax.ppermute(st['f'], 'col', self.fwd_pairs)  12.4 us
    ppermute x16, starting transfers between devices, reduce_level(): lax.ppermute(send.astype(jnp.bfloat16), 'row', [(i, i ^ d) for i in range...  9.95 us
  transfers between devices with their start and end apart: 30, of which 8 were waited for; matrix products, arithmetic and copies ran while one was open for 45% of the time, Pallas kernels for 0%

profile of v2, /device:TPU:0, one launch (start us, length us, event | category | flops | bytes accessed | tf_op | source)
XLA Modules:
  0.0 203.9 jit_solution(18152033890115619305)
XLA Ops:
  0.0 2.4 %fusion.60 = (bf16[64,4096]{1,0:T(8,128)(2,1)}, bf16[64,4096]{1,0:T(8,128)(2,1)}) fusion(bf16[128,4096]{1,0:T(8,128)(2,1)} %param.12), kind=kLoop, calls=%fused_computation.101 | loop fusion | bytes 2097152 | tf_op jit(solution)/shard_map/slice | solution.py:120
  2.4 3.1 %collective-permute-start.8 = (bf16[64,4096]{1,0:T(8,128)(2,1)}, bf16[64,4096]{1,0:T(8,128)(2,1)S(1)}, u32[]{:S(2)}, u32[]{:S(2)}) collective-permute-start(bf16[64,4096]{1,0:T(8,128)(2,1)} %get-tuple-element.139), channel_id=1, source_target_pairs={{0,2},{2,4},{4,6},{6,7},{7,5},{5,3},{3,1},{1,0},{8,10},{10,12},{12... | collective-permute-start | bytes 1572872 | tf_op jit(solution)/shard_map/ppermute | solution.py:57
  5.4 2.0 collective-permute-start
  13.1 1.6 fusion.61
  23.4 2.5 %broadcast.16.clone = bf16[8,64,4096]{2,1,0:T(8,128)(2,1)} broadcast(bf16[]{:T(256)} %constant.232.clone.1), dimensions={} | broadcast | bytes 4194306 | tf_op jit(solution)/shard_map/broadcast.3
  31.6 2.1 %collective-permute-start.2 = (bf16[64,4096]{1,0:T(8,128)(2,1)S(1)}, bf16[64,4096]{1,0:T(8,128)(2,1)S(1)}, u32[]{:S(2)}, u32[]{:S(2)}) collective-permute-start(bf16[64,4096]{1,0:T(8,128)(2,1)S(1)} %collective-permute-done), channel_id=1, source_target_pairs={{0,2},{2,4},{4,6},{6,7},{7,5},{5,3},{3,1},{1,0},{8,10},{10,12},{12... | collective-permute-start | bytes 1572872 | tf_op jit(solution)/shard_map/ppermute | solution.py:57
  35.4 9.0 %collective-permute-done.2 = bf16[64,4096]{1,0:T(8,128)(2,1)S(1)} collective-permute-done((bf16[64,4096]{1,0:T(8,128)(2,1)S(1)}, bf16[64,4096]{1,0:T(8,128)(2,1)S(1)}, u32[]{:S(2)}, u32[]{:S(2)}) %collective-permute-start.2) | collective-permute-done | bytes 524320 | tf_op jit(solution)/shard_map/ppermute | solution.py:57
  44.5 1.7 collective-permute-start.4
  48.1 8.4 %collective-permute-done.4 = bf16[64,4096]{1,0:T(8,128)(2,1)S(1)} collective-permute-done((bf16[64,4096]{1,0:T(8,128)(2,1)S(1)}, bf16[64,4096]{1,0:T(8,128)(2,1)S(1)}, u32[]{:S(2)}, u32[]{:S(2)}) %collective-permute-start.4) | collective-permute-done | bytes 524320 | tf_op jit(solution)/shard_map/ppermute | solution.py:57
  56.5 1.7 collective-permute-start.6
  60.0 7.7 %collective-permute-done.6 = bf16[64,4096]{1,0:T(8,128)(2,1)S(1)} collective-permute-done((bf16[64,4096]{1,0:T(8,128)(2,1)S(1)}, bf16[64,4096]{1,0:T(8,128)(2,1)S(1)}, u32[]{:S(2)}, u32[]{:S(2)}) %collective-permute-start.6) | collective-permute-done | bytes 524320 | tf_op jit(solution)/shard_map/ppermute | solution.py:57
  68.5 11.7 %fusion.20 = bf16[512,1664]{1,0:T(8,128)(2,1)S(1)} fusion(bf16[512,4096]{1,0:T(8,128)(2,1)} %bitcast.22, bf16[4096,3328]{1,0:T(8,128)(2,1)} %param.13), kind=kOutput, calls=%fused_computation.25 | convolution fusion | flops 6980173824 | bytes 19529728 | tf_op jit(solution)/shard_map/dot_general | solution.py:125
  82.4 11.7 %fusion.26 = bf16[512,1664]{1,0:T(8,128)(2,1)S(1)} fusion(bf16[512,4096]{1,0:T(8,128)(2,1)} %bitcast.22, bf16[4096,3328]{1,0:T(8,128)(2,1)} %param.13), kind=kOutput, calls=%fused_computation.27 | convolution fusion | flops 6980173824 | bytes 19529728 | tf_op jit(solution)/shard_map/dot_general | solution.py:125
  94.4 1.5 collective-permute-start.12
  95.9 1.5 collective-permute-start.14
  98.1 11.7 %fusion.32 = bf16[512,1664]{1,0:T(8,128)(2,1)S(1)} fusion(bf16[512,4096]{1,0:T(8,128)(2,1)} %bitcast.22, bf16[4096,3328]{1,0:T(8,128)(2,1)} %param.14), kind=kOutput, calls=%fused_computation.29 | convolution fusion | flops 6980173824 | bytes 19529728 | tf_op jit(solution)/shard_map/dot_general | solution.py:125
  112.9 11.7 %fusion.38 = bf16[512,1664]{1,0:T(8,128)(2,1)S(1)} fusion(bf16[512,4096]{1,0:T(8,128)(2,1)} %bitcast.22, bf16[4096,3328]{1,0:T(8,128)(2,1)} %param.14), kind=kOutput, calls=%fused_computation.31 | convolution fusion | flops 6980173824 | bytes 19529728 | tf_op jit(solution)/shard_map/dot_general | solution.py:125
  126.9 11.1 %fusion.23 = bf16[512,1664]{1,0:T(8,128)(2,1)S(1)} fusion(bf16[512,4096]{1,0:T(8,128)(2,1)S(1)} %bitcast.229, bf16[4096,3328]{1,0:T(8,128)(2,1)} %param.13), kind=kOutput, calls=%fused_computation.26 | convolution fusion | flops 6980173824 | bytes 19529728 | tf_op jit(solution)/shard_map/dot_general | solution.py:125
  139.4 11.1 %fusion.29 = bf16[512,1664]{1,0:T(8,128)(2,1)S(1)} fusion(bf16[512,4096]{1,0:T(8,128)(2,1)S(1)} %bitcast.230, bf16[4096,3328]{1,0:T(8,128)(2,1)} %param.13), kind=kOutput, calls=%fused_computation.28 | convolution fusion | flops 6980173824 | bytes 19529728 | tf_op jit(solution)/shard_map/dot_general | solution.py:125
  152.4 11.3 %fusion.35 = bf16[512,1664]{1,0:T(8,128)(2,1)S(1)} fusion(bf16[512,4096]{1,0:T(8,128)(2,1)S(1)} %bitcast.231, bf16[4096,3328]{1,0:T(8,128)(2,1)} %param.14), kind=kOutput, calls=%fused_computation.30 | convolution fusion | flops 6980173824 | bytes 19529728 | tf_op jit(solution)/shard_map/dot_general | solution.py:125
  165.0 11.1 %fusion.41 = bf16[512,1664]{1,0:T(8,128)(2,1)S(1)} fusion(bf16[512,4096]{1,0:T(8,128)(2,1)S(1)} %bitcast.232, bf16[4096,3328]{1,0:T(8,128)(2,1)} %param.14), kind=kOutput, calls=%fused_computation.32 | convolution fusion | flops 6980173824 | bytes 19529728 | tf_op jit(solution)/shard_map/dot_general | solution.py:125
  178.2 10.6 %collective-permute-done.27 = bf16[1,128,1664]{2,1,0:T(8,128)(2,1)S(1)} collective-permute-done((bf16[1,128,1664]{2,1,0:T(8,128)(2,1)S(1)}, bf16[1,128,1664]{2,1,0:T(8,128)(2,1)S(1)}, u32[]{:S(2)}, u32[]{:S(2)}) %collective-permute-start.27) | collective-permute-done | bytes 426016 | tf_op jit(solution)/shard_map/ppermute | solution.py:77
  190.5 10.1 %collective-permute-done.29 = bf16[1,128,1664]{2,1,0:T(8,128)(2,1)S(1)} collective-permute-done((bf16[1,128,1664]{2,1,0:T(8,128)(2,1)S(1)}, bf16[1,128,1664]{2,1,0:T(8,128)(2,1)S(1)}, u32[]{:S(2)}, u32[]{:S(2)}) %collective-permute-start.29) | collective-permute-done | bytes 426016 | tf_op jit(solution)/shard_map/ppermute | solution.py:77
  201.7 2.2 %fusion.16 = bf16[256,3328]{1,0:T(8,128)(2,1)} fusion(f32[2,2,64,3328]{3,2,0,1:T(8,128)S(1)} %pad_maximum_fusion.1, f32[2,2,64,3328]{3,2,0,1:T(8,128)S(1)} %pad_maximum_fusion), kind=kLoop, calls=%fused_computation.19 | loop fusion | flops 5111808 | bytes 8519680 | tf_op jit(solution)/shard_map/convert_element_type | solution.py:169
  (104 shorter events, 26.6 us)
Async XLA Ops:
  2.4 33.0 %collective-permute-start.8 = (bf16[64,4096]{1,0:T(8,128)(2,1)}, bf16[64,4096]{1,0:T(8,128)(2,1)S(1)}, u32[]{:S(2)}, u32[]{:S(2)}) collective-permute-start(bf16[64,4096]{1,0:T(8,128)(2,1)} %get-tuple-element.139), channel_id=1, source_target_pairs={{0,2},{2,4},{4,6},{6,7},{7,5},{5,3},{3,1},{1,0},{8,10},{10,12},{12... | collective-permute-start | bytes 1572872 | tf_op jit(solution)/shard_map/ppermute | solution.py:57
  5.4 29.9 %collective-permute-start.7 = (bf16[64,4096]{1,0:T(8,128)(2,1)}, bf16[64,4096]{1,0:T(8,128)(2,1)S(1)}, u32[]{:S(2)}, u32[]{:S(2)}) collective-permute-start(bf16[64,4096]{1,0:T(8,128)(2,1)} %get-tuple-element.139), channel_id=1, source_target_pairs={{0,1},{2,0},{4,2},{6,4},{7,6},{5,7},{3,5},{1,3},{8,9},{10,8},{12,1... | collective-permute-start | bytes 1572872 | tf_op jit(solution)/shard_map/ppermute | solution.py:61
  5.4 26.1 %collective-permute-start = (bf16[64,4096]{1,0:T(8,128)(2,1)}, bf16[64,4096]{1,0:T(8,128)(2,1)S(1)}, u32[]{:S(2)}, u32[]{:S(2)}) collective-permute-start(bf16[64,4096]{1,0:T(8,128)(2,1)} %get-tuple-element.140), channel_id=1, source_target_pairs={{0,2},{2,4},{4,6},{6,7},{7,5},{5,3},{3,1},{1,0},{8,10},{10,12},{12... | collective-permute-start | bytes 1572872 | tf_op jit(solution)/shard_map/ppermute | solution.py:57
  7.5 26.2 %collective-permute-start.1 = (bf16[64,4096]{1,0:T(8,128)(2,1)}, bf16[64,4096]{1,0:T(8,128)(2,1)S(1)}, u32[]{:S(2)}, u32[]{:S(2)}) collective-permute-start(bf16[64,4096]{1,0:T(8,128)(2,1)} %get-tuple-element.140), channel_id=1, source_target_pairs={{0,1},{2,0},{4,2},{6,4},{7,6},{5,7},{3,5},{1,3},{8,9},{10,8},{12,1... | collective-permute-start | bytes 1572872 | tf_op jit(solution)/shard_map/ppermute | solution.py:61
  31.6 12.9 %collective-permute-start.2 = (bf16[64,4096]{1,0:T(8,128)(2,1)S(1)}, bf16[64,4096]{1,0:T(8,128)(2,1)S(1)}, u32[]{:S(2)}, u32[]{:S(2)}) collective-permute-start(bf16[64,4096]{1,0:T(8,128)(2,1)S(1)} %collective-permute-done), channel_id=1, source_target_pairs={{0,2},{2,4},{4,6},{6,7},{7,5},{5,3},{3,1},{1,0},{8,10},{10,12},{12... | collective-permute-start | bytes 1572872 | tf_op jit(solution)/shard_map/ppermute | solution.py:57
  33.7 12.5 %collective-permute-start.3 = (bf16[64,4096]{1,0:T(8,128)(2,1)S(1)}, bf16[64,4096]{1,0:T(8,128)(2,1)S(1)}, u32[]{:S(2)}, u32[]{:S(2)}) collective-permute-start(bf16[64,4096]{1,0:T(8,128)(2,1)S(1)} %collective-permute-done.1), channel_id=1, source_target_pairs={{0,1},{2,0},{4,2},{6,4},{7,6},{5,7},{3,5},{1,3},{8,9},{10,8},{12,1... | collective-permute-start | bytes 1572872 | tf_op jit(solution)/shard_map/ppermute | solution.py:61
  44.5 12.1 %collective-permute-start.4 = (bf16[64,4096]{1,0:T(8,128)(2,1)S(1)}, bf16[64,4096]{1,0:T(8,128)(2,1)S(1)}, u32[]{:S(2)}, u32[]{:S(2)}) collective-permute-start(bf16[64,4096]{1,0:T(8,128)(2,1)S(1)} %collective-permute-done.2), channel_id=1, source_target_pairs={{0,2},{2,4},{4,6},{6,7},{7,5},{5,3},{3,1},{1,0},{8,10},{10,12},{12... | collective-permute-start | bytes 1572872 | tf_op jit(solution)/shard_map/ppermute | solution.py:57
  46.2 12.9 %collective-permute-start.5 = (bf16[64,4096]{1,0:T(8,128)(2,1)S(1)}, bf16[64,4096]{1,0:T(8,128)(2,1)S(1)}, u32[]{:S(2)}, u32[]{:S(2)}) collective-permute-start(bf16[64,4096]{1,0:T(8,128)(2,1)S(1)} %collective-permute-done.3), channel_id=1, source_target_pairs={{0,1},{2,0},{4,2},{6,4},{7,6},{5,7},{3,5},{1,3},{8,9},{10,8},{12,1... | collective-permute-start | bytes 1572872 | tf_op jit(solution)/shard_map/ppermute | solution.py:61
  80.2 14.0 %collective-permute-start.10 = (bf16[64,4096]{1,0:T(8,128)(2,1)S(1)}, bf16[64,4096]{1,0:T(8,128)(2,1)S(1)}, u32[]{:S(2)}, u32[]{:S(2)}) collective-permute-start(bf16[64,4096]{1,0:T(8,128)(2,1)S(1)} %collective-permute-done.7), channel_id=1, source_target_pairs={{0,1},{2,0},{4,2},{6,4},{7,6},{5,7},{3,5},{1,3},{8,9},{10,8},{12,1... | collective-permute-start | bytes 1572872 | tf_op jit(solution)/shard_map/ppermute | solution.py:61
  81.6 12.5 %collective-permute-start.11 = (bf16[64,4096]{1,0:T(8,128)(2,1)S(1)}, bf16[64,4096]{1,0:T(8,128)(2,1)S(1)}, u32[]{:S(2)}, u32[]{:S(2)}) collective-permute-start(bf16[64,4096]{1,0:T(8,128)(2,1)S(1)} %collective-permute-done.8), channel_id=1, source_target_pairs={{0,2},{2,4},{4,6},{6,7},{7,5},{5,3},{3,1},{1,0},{8,10},{10,12},{12... | collective-permute-start | bytes 1572872 | tf_op jit(solution)/shard_map/ppermute | solution.py:57
  82.3 11.9 %collective-permute-start.9 = (bf16[2,128,1664]{2,1,0:T(8,128)(2,1)S(1)}, bf16[2,128,1664]{2,1,0:T(8,128)(2,1)S(1)}, u32[]{:S(2)}, u32[]{:S(2)}) collective-permute-start(bf16[2,128,1664]{2,1,0:T(8,128)(2,1)S(1)} %dynamic-slice_bitcast_fusion.7), channel_id=1, source_target_pairs={{0,8},{8,0},{16,24},{24,16},{1,9},{9,1},{17,25},{25,17},{2,10},{10... | collective-permute-start | bytes 2555912 | tf_op jit(solution)/shard_map/ppermute | solution.py:77
  94.4 15.3 %collective-permute-start.12 = (bf16[1,128,1664]{2,1,0:T(8,128)(2,1)S(1)}, bf16[1,128,1664]{2,1,0:T(8,128)(2,1)S(1)}, u32[]{:S(2)}, u32[]{:S(2)}) collective-permute-start(bf16[1,128,1664]{2,1,0:T(8,128)(2,1)S(1)} %fusion.52), channel_id=1, source_target_pairs={{0,16},{8,24},{16,0},{24,8},{1,17},{9,25},{17,1},{25,9},{2,18},{10... | collective-permute-start | bytes 1277960 | tf_op jit(solution)/shard_map/ppermute | solution.py:77
  95.9 15.3 %collective-permute-start.14 = (bf16[64,4096]{1,0:T(8,128)(2,1)S(1)}, bf16[64,4096]{1,0:T(8,128)(2,1)S(1)}, u32[]{:S(2)}, u32[]{:S(2)}) collective-permute-start(bf16[64,4096]{1,0:T(8,128)(2,1)S(1)} %collective-permute-done.10), channel_id=1, source_target_pairs={{0,1},{2,0},{4,2},{6,4},{7,6},{5,7},{3,5},{1,3},{8,9},{10,8},{12,1... | collective-permute-start | bytes 1572872 | tf_op jit(solution)/shard_map/ppermute | solution.py:61
  97.4 13.8 %collective-permute-start.15 = (bf16[64,4096]{1,0:T(8,128)(2,1)S(1)}, bf16[64,4096]{1,0:T(8,128)(2,1)S(1)}, u32[]{:S(2)}, u32[]{:S(2)}) collective-permute-start(bf16[64,4096]{1,0:T(8,128)(2,1)S(1)} %collective-permute-done.11), channel_id=1, source_target_pairs={{0,2},{2,4},{4,6},{6,7},{7,5},{5,3},{3,1},{1,0},{8,10},{10,12},{12... | collective-permute-start | bytes 1572872 | tf_op jit(solution)/shard_map/ppermute | solution.py:57
  98.0 13.3 %collective-permute-start.13 = (bf16[2,128,1664]{2,1,0:T(8,128)(2,1)S(1)}, bf16[2,128,1664]{2,1,0:T(8,128)(2,1)S(1)}, u32[]{:S(2)}, u32[]{:S(2)}) collective-permute-start(bf16[2,128,1664]{2,1,0:T(8,128)(2,1)S(1)} %dynamic-slice_bitcast_fusion.6), channel_id=1, source_target_pairs={{0,8},{8,0},{16,24},{24,16},{1,9},{9,1},{17,25},{25,17},{2,10},{10... | collective-permute-start | bytes 2555912 | tf_op jit(solution)/shard_map/ppermute | solution.py:77
  111.5 13.0 %collective-permute-start.16 = (bf16[1,128,1664]{2,1,0:T(8,128)(2,1)S(1)}, bf16[1,128,1664]{2,1,0:T(8,128)(2,1)S(1)}, u32[]{:S(2)}, u32[]{:S(2)}) collective-permute-start(bf16[1,128,1664]{2,1,0:T(8,128)(2,1)S(1)} %fusion.53), channel_id=1, source_target_pairs={{0,16},{8,24},{16,0},{24,8},{1,17},{9,25},{17,1},{25,9},{2,18},{10... | collective-permute-start | bytes 1277960 | tf_op jit(solution)/shard_map/ppermute | solution.py:77
  112.1 12.9 %collective-permute-start.18 = (bf16[64,4096]{1,0:T(8,128)(2,1)S(1)}, bf16[64,4096]{1,0:T(8,128)(2,1)S(1)}, u32[]{:S(2)}, u32[]{:S(2)}) collective-permute-start(bf16[64,4096]{1,0:T(8,128)(2,1)S(1)} %collective-permute-done.15), channel_id=1, source_target_pairs={{0,2},{2,4},{4,6},{6,7},{7,5},{5,3},{3,1},{1,0},{8,10},{10,12},{12... | collective-permute-start | bytes 1572872 | tf_op jit(solution)/shard_map/ppermute | solution.py:57
  112.8 12.2 %collective-permute-start.17 = (bf16[2,128,1664]{2,1,0:T(8,128)(2,1)S(1)}, bf16[2,128,1664]{2,1,0:T(8,128)(2,1)S(1)}, u32[]{:S(2)}, u32[]{:S(2)}) collective-permute-start(bf16[2,128,1664]{2,1,0:T(8,128)(2,1)S(1)} %dynamic-slice_bitcast_fusion.5), channel_id=1, source_target_pairs={{0,8},{8,0},{16,24},{24,16},{1,9},{9,1},{17,25},{25,17},{2,10},{10... | collective-permute-start | bytes 2555912 | tf_op jit(solution)/shard_map/ppermute | solution.py:77
  125.3 12.7 %collective-permute-start.19 = (bf16[1,128,1664]{2,1,0:T(8,128)(2,1)S(1)}, bf16[1,128,1664]{2,1,0:T(8,128)(2,1)S(1)}, u32[]{:S(2)}, u32[]{:S(2)}) collective-permute-start(bf16[1,128,1664]{2,1,0:T(8,128)(2,1)S(1)} %fusion.54), channel_id=1, source_target_pairs={{0,16},{8,24},{16,0},{24,8},{1,17},{9,25},{17,1},{25,9},{2,18},{10... | collective-permute-start | bytes 1277960 | tf_op jit(solution)/shard_map/ppermute | solution.py:77
  138.3 12.3 %collective-permute-start.21 = (bf16[1,128,1664]{2,1,0:T(8,128)(2,1)S(1)}, bf16[1,128,1664]{2,1,0:T(8,128)(2,1)S(1)}, u32[]{:S(2)}, u32[]{:S(2)}) collective-permute-start(bf16[1,128,1664]{2,1,0:T(8,128)(2,1)S(1)} %fusion.55), channel_id=1, source_target_pairs={{0,16},{8,24},{16,0},{24,8},{1,17},{9,25},{17,1},{25,9},{2,18},{10... | collective-permute-start | bytes 1277960 | tf_op jit(solution)/shard_map/ppermute | solution.py:77
  139.1 11.5 %collective-permute-start.22 = (bf16[2,128,1664]{2,1,0:T(8,128)(2,1)S(1)}, bf16[2,128,1664]{2,1,0:T(8,128)(2,1)S(1)}, u32[]{:S(2)}, u32[]{:S(2)}) collective-permute-start(bf16[2,128,1664]{2,1,0:T(8,128)(2,1)S(1)} %dynamic-slice_bitcast_fusion.3), channel_id=1, source_target_pairs={{0,8},{8,0},{16,24},{24,16},{1,9},{9,1},{17,25},{25,17},{2,10},{10... | collective-permute-start | bytes 2555912 | tf_op jit(solution)/shard_map/ppermute | solution.py:77
  150.9 12.8 %collective-permute-start.23 = (bf16[1,128,1664]{2,1,0:T(8,128)(2,1)S(1)}, bf16[1,128,1664]{2,1,0:T(8,128)(2,1)S(1)}, u32[]{:S(2)}, u32[]{:S(2)}) collective-permute-start(bf16[1,128,1664]{2,1,0:T(8,128)(2,1)S(1)} %fusion.56), channel_id=1, source_target_pairs={{0,16},{8,24},{16,0},{24,8},{1,17},{9,25},{17,1},{25,9},{2,18},{10... | collective-permute-start | bytes 1277960 | tf_op jit(solution)/shard_map/ppermute | solution.py:77
  164.1 12.1 %collective-permute-start.25 = (bf16[1,128,1664]{2,1,0:T(8,128)(2,1)S(1)}, bf16[1,128,1664]{2,1,0:T(8,128)(2,1)S(1)}, u32[]{:S(2)}, u32[]{:S(2)}) collective-permute-start(bf16[1,128,1664]{2,1,0:T(8,128)(2,1)S(1)} %fusion.57), channel_id=1, source_target_pairs={{0,16},{8,24},{16,0},{24,8},{1,17},{9,25},{17,1},{25,9},{2,18},{10... | collective-permute-start | bytes 1277960 | tf_op jit(solution)/shard_map/ppermute | solution.py:77
  176.5 12.3 %collective-permute-start.27 = (bf16[1,128,1664]{2,1,0:T(8,128)(2,1)S(1)}, bf16[1,128,1664]{2,1,0:T(8,128)(2,1)S(1)}, u32[]{:S(2)}, u32[]{:S(2)}) collective-permute-start(bf16[1,128,1664]{2,1,0:T(8,128)(2,1)S(1)} %fusion.58), channel_id=1, source_target_pairs={{0,16},{8,24},{16,0},{24,8},{1,17},{9,25},{17,1},{25,9},{2,18},{10... | collective-permute-start | bytes 1277960 | tf_op jit(solution)/shard_map/ppermute | solution.py:77
  (7 other events, 93.4 us)

commit v3 on v2

--- a/solution.py
+++ b/solution.py
@@ -78,6 +78,17 @@
     return (keep.astype(jnp.float32) + got.astype(jnp.float32)).reshape(-1, cur.shape[1])
 
 
+def reduce_direct(cur, n_row):
+    r = lax.axis_index("row")
+    x = cur.reshape(n_row, cur.shape[0] // n_row, cur.shape[1])
+    total = lax.dynamic_index_in_dim(x, r, axis=0, keepdims=False).astype(jnp.float32)
+    for d in range(1, n_row):
+        send = lax.dynamic_index_in_dim(x, r ^ d, axis=0, keepdims=False)
+        got = lax.ppermute(send.astype(jnp.bfloat16), "row", [(i, i ^ d) for i in range(n_row)])
+        total = total + got.astype(jnp.float32)
+    return total
+
+
 def make_on_device(n_row, n_col, order):
     ring = Ring(order)
     levels = []
@@ -97,6 +108,7 @@
         for s in range(1, ring.steps + 1):
             st = ring.step(st, s)
         piece = ring.result(st)
+        piece, tokens = lax.optimization_barrier((piece, tokens))
 
         tiles = []
         for h in range(HALVES):
@@ -111,8 +123,12 @@
         while t < len(tiles) or jobs:
             carry = {}
             for job in jobs:
-                job[2] = reduce_level(job[2], levels[job[1]], n_row)
-                job[1] += 1
+                if job[0] == len(tiles) - 1:
+                    job[2] = reduce_direct(job[2], n_row)
+                    job[1] = len(levels)
+                else:
+                    job[2] = reduce_level(job[2], levels[job[1]], n_row)
+                    job[1] += 1
             if t < len(tiles):
                 h, w, j = tiles[t]
                 first_of_share = t % (2 * SPLIT_UNITS) == 0

time: 204 us -> 215 us (1.054)
  waiting for transfers between devices: 47.7 us -> 59.5 us
  local copies, waits for them, and re-layouts: 16.1 us -> 9.86 us
  other arithmetic: 5.23 us -> 10.8 us
    ppermute x0 -> x3, waiting for transfers between devices: none -> 16.6 us  [reduce_direct(): lax.ppermute(send.astype(jnp.bfloat16), 'row', [(i, i ^ d) for i in range...]
    ppermute x16 -> x14, waiting for transfers between devices: 20.9 us -> 8.39 us  [reduce_level(): lax.ppermute(send.astype(jnp.bfloat16), 'row', [(i, i ^ d) for i in range...]
    ppermute x8, waiting for transfers between devices: 26.7 us -> 34.6 us  [step(): f = lax.ppermute(st['f'], 'col', self.fwd_pairs)]
    reshape x8 -> x7, other arithmetic: 0.65 us -> 5.19 us  [reduce_level(): (keep.astype(jnp.float32) + got.astype(jnp.float32)).reshape(-1, cur.shap...]
    dynamic_update_slice x8, local copies, waits for them, and re-layouts: 3.46 us -> 0.31 us  [step(): buf = lax.dynamic_update_slice(buf, f[None], (order_t[(p - s) % n], 0, 0))]
    dynamic_update_slice x6, local copies, waits for them, and re-layouts: 2.62 us -> 0.25 us  [step(): buf = lax.dynamic_update_slice(buf, b[None], (order_t[(p + s) % n], 0, 0))]
    slice x1, local copies, waits for them, and re-layouts: 2.37 us -> 0.04 us  [on_device(): nxt = {'st': ring.init(tokens[(h + 1) * tc:(h + 2) * tc]), 's': 1}]
    ppermute x0 -> x3, starting transfers between devices: none -> 2.21 us  [reduce_direct(): lax.ppermute(send.astype(jnp.bfloat16), 'row', [(i, i ^ d) for i in range...]
  transfers between devices with their start and end apart: 30 -> 31, of which waited for: 8 -> 9; matrix products, arithmetic and copies ran while one was open for 45% -> 47% of each run, Pallas kernels for 0% -> 0%
where the time goes in v3:
time: 215 us
  matrix products  90.1 us (42%)
  waiting for transfers between devices  59.5 us (28%)
  starting transfers between devices  26 us (12%)
  between operations  18.3 us (9%)
  other arithmetic  10.8 us (5%)
  local copies, waits for them, and re-layouts  9.86 us (5%)
    dot_general x8, matrix products, on_device(): jnp.dot(piece, weight[:, j * us:(j + 1) * us], preferred_element_type=jnp...  90.1 us
    ppermute x8, waiting for transfers between devices, step(): f = lax.ppermute(st['f'], 'col', self.fwd_pairs)  34.6 us
    ppermute x3, waiting for transfers between devices, reduce_direct(): lax.ppermute(send.astype(jnp.bfloat16), 'row', [(i, i ^ d) for i in range...  16.6 us
    ppermute x8, starting transfers between devices, step(): f = lax.ppermute(st['f'], 'col', self.fwd_pairs)  11.7 us
    ppermute x14, waiting for transfers between devices, reduce_level(): lax.ppermute(send.astype(jnp.bfloat16), 'row', [(i, i ^ d) for i in range...  8.39 us
    ppermute x14, starting transfers between devices, reduce_level(): lax.ppermute(send.astype(jnp.bfloat16), 'row', [(i, i ^ d) for i in range...  8.3 us
    reshape x7, other arithmetic, reduce_level(): (keep.astype(jnp.float32) + got.astype(jnp.float32)).reshape(-1, cur.shap...  5.19 us
  transfers between devices with their start and end apart: 31, of which 9 were waited for; matrix products, arithmetic and copies ran while one was open for 47% of the time, Pallas kernels for 0%

profile of v3, /device:TPU:0, one launch (start us, length us, event | category | flops | bytes accessed | tf_op | source)
XLA Modules:
  0.0 214.7 jit_solution(17381422035458293899)
XLA Ops:
  1.2 3.1 %collective-permute-start = (bf16[64,4096]{1,0:T(8,128)(2,1)S(1)}, bf16[64,4096]{1,0:T(8,128)(2,1)S(1)}, u32[]{:S(2)}, u32[]{:S(2)}) collective-permute-start(bf16[64,4096]{1,0:T(8,128)(2,1)S(1)} %slice.22), channel_id=1, source_target_pairs={{0,2},{2,4},{4,6},{6,7},{7,5},{5,3},{3,1},{1,0},{8,10},{10,12},{12... | collective-permute-start | bytes 1572872 | tf_op jit(solution)/shard_map/ppermute | solution.py:57
  10.2 1.6 fusion.60
  25.4 2.1 collective-permute-start.2
  27.6 11.3 %collective-permute-done.2 = bf16[64,4096]{1,0:T(8,128)(2,1)S(1)} collective-permute-done((bf16[64,4096]{1,0:T(8,128)(2,1)S(1)}, bf16[64,4096]{1,0:T(8,128)(2,1)S(1)}, u32[]{:S(2)}, u32[]{:S(2)}) %collective-permute-start.2) | collective-permute-done | bytes 524320 | tf_op jit(solution)/shard_map/ppermute | solution.py:57
  38.8 1.7 collective-permute-start.4
  41.0 10.4 %collective-permute-done.4 = bf16[64,4096]{1,0:T(8,128)(2,1)S(1)} collective-permute-done((bf16[64,4096]{1,0:T(8,128)(2,1)S(1)}, bf16[64,4096]{1,0:T(8,128)(2,1)S(1)}, u32[]{:S(2)}, u32[]{:S(2)}) %collective-permute-start.4) | collective-permute-done | bytes 524320 | tf_op jit(solution)/shard_map/ppermute | solution.py:57
  52.9 10.4 %collective-permute-done.6 = bf16[64,4096]{1,0:T(8,128)(2,1)S(1)} collective-permute-done((bf16[64,4096]{1,0:T(8,128)(2,1)S(1)}, bf16[64,4096]{1,0:T(8,128)(2,1)S(1)}, u32[]{:S(2)}, u32[]{:S(2)}) %collective-permute-start.6) | collective-permute-done | bytes 524320 | tf_op jit(solution)/shard_map/ppermute | solution.py:57
  63.4 1.5 collective-permute-start.8
  65.5 11.1 %fusion.20 = bf16[512,1664]{1,0:T(8,128)(2,1)S(1)} fusion(bf16[512,4096]{1,0:T(8,128)(2,1)S(1)} %bitcast.227, bf16[4096,3328]{1,0:T(8,128)(2,1)} %param.13), kind=kOutput, calls=%fused_computation.25 | convolution fusion | flops 6980173824 | bytes 19529728 | tf_op jit(solution)/shard_map/dot_general | solution.py:141
  79.5 11.1 %fusion.26 = bf16[512,1664]{1,0:T(8,128)(2,1)S(1)} fusion(bf16[512,4096]{1,0:T(8,128)(2,1)S(1)} %bitcast.228, bf16[4096,3328]{1,0:T(8,128)(2,1)} %param.13), kind=kOutput, calls=%fused_computation.27 | convolution fusion | flops 6980173824 | bytes 19529728 | tf_op jit(solution)/shard_map/dot_general | solution.py:141
  92.4 1.5 collective-permute-start.14
  94.6 11.1 %fusion.32 = bf16[512,1664]{1,0:T(8,128)(2,1)S(1)} fusion(bf16[512,4096]{1,0:T(8,128)(2,1)S(1)} %bitcast.229, bf16[4096,3328]{1,0:T(8,128)(2,1)} %param.14), kind=kOutput, calls=%fused_computation.29 | convolution fusion | flops 6980173824 | bytes 19529728 | tf_op jit(solution)/shard_map/dot_general | solution.py:141
  105.8 1.9 collective-permute-done.15
  109.4 11.1 %fusion.38 = bf16[512,1664]{1,0:T(8,128)(2,1)S(1)} fusion(bf16[512,4096]{1,0:T(8,128)(2,1)S(1)} %bitcast.230, bf16[4096,3328]{1,0:T(8,128)(2,1)} %param.14), kind=kOutput, calls=%fused_computation.31 | convolution fusion | flops 6980173824 | bytes 19529728 | tf_op jit(solution)/shard_map/dot_general | solution.py:141
  121.5 1.6 collective-permute-start.19
  123.2 11.1 %fusion.23 = bf16[512,1664]{1,0:T(8,128)(2,1)S(1)} fusion(bf16[512,4096]{1,0:T(8,128)(2,1)S(1)} %bitcast.223, bf16[4096,3328]{1,0:T(8,128)(2,1)} %param.13), kind=kOutput, calls=%fused_computation.26 | convolution fusion | flops 6980173824 | bytes 19529728 | tf_op jit(solution)/shard_map/dot_general | solution.py:141
  136.5 11.1 %fusion.29 = bf16[512,1664]{1,0:T(8,128)(2,1)S(1)} fusion(bf16[512,4096]{1,0:T(8,128)(2,1)S(1)} %bitcast.224, bf16[4096,3328]{1,0:T(8,128)(2,1)} %param.13), kind=kOutput, calls=%fused_computation.28 | convolution fusion | flops 6980173824 | bytes 19529728 | tf_op jit(solution)/shard_map/dot_general | solution.py:141
  150.5 11.3 %fusion.35 = bf16[512,1664]{1,0:T(8,128)(2,1)S(1)} fusion(bf16[512,4096]{1,0:T(8,128)(2,1)S(1)} %bitcast.225, bf16[4096,3328]{1,0:T(8,128)(2,1)} %param.14), kind=kOutput, calls=%fused_computation.30 | convolution fusion | flops 6980173824 | bytes 19529728 | tf_op jit(solution)/shard_map/dot_general | solution.py:141
  164.1 12.3 %fusion.41 = bf16[512,1664]{1,0:T(8,128)(2,1)} fusion(bf16[512,4096]{1,0:T(8,128)(2,1)S(1)} %bitcast.226, bf16[4096,3328]{1,0:T(8,128)(2,1)} %param.14), kind=kOutput, calls=%fused_computation.32 | convolution fusion | flops 6980173824 | bytes 19529728 | tf_op jit(solution)/shard_map/dot_general | solution.py:141
  179.6 1.5 dynamic-slice_bitcast_fusion.9
  183.3 8.1 %collective-permute-done.27 = bf16[1,128,1664]{2,1,0:T(8,128)(2,1)} collective-permute-done((bf16[1,128,1664]{2,1,0:T(8,128)(2,1)}, bf16[1,128,1664]{2,1,0:T(8,128)(2,1)}, u32[]{:S(2)}, u32[]{:S(2)}) %collective-permute-start.27) | collective-permute-done | bytes 426016 | tf_op jit(solution)/shard_map/ppermute | solution.py:77
  192.4 7.0 %collective-permute-done.30 = bf16[128,1664]{1,0:T(8,128)(2,1)S(1)} collective-permute-done((bf16[128,1664]{1,0:T(8,128)(2,1)S(1)}, bf16[128,1664]{1,0:T(8,128)(2,1)S(1)}, u32[]{:S(2)}, u32[]{:S(2)}) %collective-permute-start.30) | collective-permute-done | bytes 426016 | tf_op jit(solution)/shard_map/ppermute | solution.py:87
  199.4 9.6 %collective-permute-done.29 = bf16[128,1664]{1,0:T(8,128)(2,1)S(1)} collective-permute-done((bf16[128,1664]{1,0:T(8,128)(2,1)S(1)}, bf16[128,1664]{1,0:T(8,128)(2,1)S(1)}, u32[]{:S(2)}, u32[]{:S(2)}) %collective-permute-start.29) | collective-permute-done | bytes 426016 | tf_op jit(solution)/shard_map/ppermute | solution.py:87
  212.5 2.2 %fusion.16 = bf16[256,3328]{1,0:T(8,128)(2,1)} fusion(f32[2,2,64,3328]{3,2,0,1:T(8,128)S(1)} %pad_maximum_fusion.1, f32[2,2,64,3328]{3,2,0,1:T(8,128)S(1)} %pad_maximum_fusion), kind=kLoop, calls=%fused_computation.19 | loop fusion | flops 5111808 | bytes 8519680 | tf_op jit(solution)/shard_map/convert_element_type | solution.py:185
  (113 shorter events, 30.9 us)
Async XLA Ops:
  1.2 24.2 %collective-permute-start = (bf16[64,4096]{1,0:T(8,128)(2,1)S(1)}, bf16[64,4096]{1,0:T(8,128)(2,1)S(1)}, u32[]{:S(2)}, u32[]{:S(2)}) collective-permute-start(bf16[64,4096]{1,0:T(8,128)(2,1)S(1)} %slice.22), channel_id=1, source_target_pairs={{0,2},{2,4},{4,6},{6,7},{7,5},{5,3},{3,1},{1,0},{8,10},{10,12},{12... | collective-permute-start | bytes 1572872 | tf_op jit(solution)/shard_map/ppermute | solution.py:57
  4.3 23.2 %collective-permute-start.1 = (bf16[64,4096]{1,0:T(8,128)(2,1)S(1)}, bf16[64,4096]{1,0:T(8,128)(2,1)S(1)}, u32[]{:S(2)}, u32[]{:S(2)}) collective-permute-start(bf16[64,4096]{1,0:T(8,128)(2,1)S(1)} %slice.22), channel_id=1, source_target_pairs={{0,1},{2,0},{4,2},{6,4},{7,6},{5,7},{3,5},{1,3},{8,9},{10,8},{12,1... | collective-permute-start | bytes 1572872 | tf_op jit(solution)/shard_map/ppermute | solution.py:61
  25.4 13.4 %collective-permute-start.2 = (bf16[64,4096]{1,0:T(8,128)(2,1)S(1)}, bf16[64,4096]{1,0:T(8,128)(2,1)S(1)}, u32[]{:S(2)}, u32[]{:S(2)}) collective-permute-start(bf16[64,4096]{1,0:T(8,128)(2,1)S(1)} %collective-permute-done), channel_id=1, source_target_pairs={{0,2},{2,4},{4,6},{6,7},{7,5},{5,3},{3,1},{1,0},{8,10},{10,12},{12... | collective-permute-start | bytes 1572872 | tf_op jit(solution)/shard_map/ppermute | solution.py:57
  27.5 13.1 %collective-permute-start.3 = (bf16[64,4096]{1,0:T(8,128)(2,1)S(1)}, bf16[64,4096]{1,0:T(8,128)(2,1)S(1)}, u32[]{:S(2)}, u32[]{:S(2)}) collective-permute-start(bf16[64,4096]{1,0:T(8,128)(2,1)S(1)} %collective-permute-done.1), channel_id=1, source_target_pairs={{0,1},{2,0},{4,2},{6,4},{7,6},{5,7},{3,5},{1,3},{8,9},{10,8},{12,1... | collective-permute-start | bytes 1572872 | tf_op jit(solution)/shard_map/ppermute | solution.py:61
  38.8 12.5 %collective-permute-start.4 = (bf16[64,4096]{1,0:T(8,128)(2,1)S(1)}, bf16[64,4096]{1,0:T(8,128)(2,1)S(1)}, u32[]{:S(2)}, u32[]{:S(2)}) collective-permute-start(bf16[64,4096]{1,0:T(8,128)(2,1)S(1)} %collective-permute-done.2), channel_id=1, source_target_pairs={{0,2},{2,4},{4,6},{6,7},{7,5},{5,3},{3,1},{1,0},{8,10},{10,12},{12... | collective-permute-start | bytes 1572872 | tf_op jit(solution)/shard_map/ppermute | solution.py:57
  40.6 12.3 %collective-permute-start.5 = (bf16[64,4096]{1,0:T(8,128)(2,1)S(1)}, bf16[64,4096]{1,0:T(8,128)(2,1)S(1)}, u32[]{:S(2)}, u32[]{:S(2)}) collective-permute-start(bf16[64,4096]{1,0:T(8,128)(2,1)S(1)} %collective-permute-done.3), channel_id=1, source_target_pairs={{0,1},{2,0},{4,2},{6,4},{7,6},{5,7},{3,5},{1,3},{8,9},{10,8},{12,1... | collective-permute-start | bytes 1572872 | tf_op jit(solution)/shard_map/ppermute | solution.py:61
  63.4 13.7 %collective-permute-start.8 = (bf16[64,4096]{1,0:T(8,128)(2,1)S(1)}, bf16[64,4096]{1,0:T(8,128)(2,1)S(1)}, u32[]{:S(2)}, u32[]{:S(2)}) collective-permute-start(bf16[64,4096]{1,0:T(8,128)(2,1)S(1)} %slice.24), channel_id=1, source_target_pairs={{0,2},{2,4},{4,6},{6,7},{7,5},{5,3},{3,1},{1,0},{8,10},{10,12},{12... | collective-permute-start | bytes 1572872 | tf_op jit(solution)/shard_map/ppermute | solution.py:57
  77.2 13.4 %collective-permute-start.10 = (bf16[64,4096]{1,0:T(8,128)(2,1)S(1)}, bf16[64,4096]{1,0:T(8,128)(2,1)S(1)}, u32[]{:S(2)}, u32[]{:S(2)}) collective-permute-start(bf16[64,4096]{1,0:T(8,128)(2,1)S(1)} %collective-permute-done.7), channel_id=1, source_target_pairs={{0,1},{2,0},{4,2},{6,4},{7,6},{5,7},{3,5},{1,3},{8,9},{10,8},{12,1... | collective-permute-start | bytes 1572872 | tf_op jit(solution)/shard_map/ppermute | solution.py:61
  90.9 14.7 %collective-permute-start.12 = (bf16[1,128,1664]{2,1,0:T(8,128)(2,1)S(1)}, bf16[1,128,1664]{2,1,0:T(8,128)(2,1)S(1)}, u32[]{:S(2)}, u32[]{:S(2)}) collective-permute-start(bf16[1,128,1664]{2,1,0:T(8,128)(2,1)S(1)} %fusion.53), channel_id=1, source_target_pairs={{0,16},{8,24},{16,0},{24,8},{1,17},{9,25},{17,1},{25,9},{2,18},{10... | collective-permute-start | bytes 1277960 | tf_op jit(solution)/shard_map/ppermute | solution.py:77
  92.4 15.3 %collective-permute-start.14 = (bf16[64,4096]{1,0:T(8,128)(2,1)S(1)}, bf16[64,4096]{1,0:T(8,128)(2,1)S(1)}, u32[]{:S(2)}, u32[]{:S(2)}) collective-permute-start(bf16[64,4096]{1,0:T(8,128)(2,1)S(1)} %collective-permute-done.10), channel_id=1, source_target_pairs={{0,1},{2,0},{4,2},{6,4},{7,6},{5,7},{3,5},{1,3},{8,9},{10,8},{12,1... | collective-permute-start | bytes 1572872 | tf_op jit(solution)/shard_map/ppermute | solution.py:61
  93.9 13.8 %collective-permute-start.15 = (bf16[64,4096]{1,0:T(8,128)(2,1)S(1)}, bf16[64,4096]{1,0:T(8,128)(2,1)S(1)}, u32[]{:S(2)}, u32[]{:S(2)}) collective-permute-start(bf16[64,4096]{1,0:T(8,128)(2,1)S(1)} %collective-permute-done.11), channel_id=1, source_target_pairs={{0,2},{2,4},{4,6},{6,7},{7,5},{5,3},{3,1},{1,0},{8,10},{10,12},{12... | collective-permute-start | bytes 1572872 | tf_op jit(solution)/shard_map/ppermute | solution.py:57
  94.5 13.3 %collective-permute-start.13 = (bf16[2,128,1664]{2,1,0:T(8,128)(2,1)S(1)}, bf16[2,128,1664]{2,1,0:T(8,128)(2,1)S(1)}, u32[]{:S(2)}, u32[]{:S(2)}) collective-permute-start(bf16[2,128,1664]{2,1,0:T(8,128)(2,1)S(1)} %dynamic-slice_bitcast_fusion.5), channel_id=1, source_target_pairs={{0,8},{8,0},{16,24},{24,16},{1,9},{9,1},{17,25},{25,17},{2,10},{10... | collective-permute-start | bytes 2555912 | tf_op jit(solution)/shard_map/ppermute | solution.py:77
  108.0 12.5 %collective-permute-start.16 = (bf16[1,128,1664]{2,1,0:T(8,128)(2,1)S(1)}, bf16[1,128,1664]{2,1,0:T(8,128)(2,1)S(1)}, u32[]{:S(2)}, u32[]{:S(2)}) collective-permute-start(bf16[1,128,1664]{2,1,0:T(8,128)(2,1)S(1)} %fusion.54), channel_id=1, source_target_pairs={{0,16},{8,24},{16,0},{24,8},{1,17},{9,25},{17,1},{25,9},{2,18},{10... | collective-permute-start | bytes 1277960 | tf_op jit(solution)/shard_map/ppermute | solution.py:77
  108.6 12.6 %collective-permute-start.18 = (bf16[64,4096]{1,0:T(8,128)(2,1)S(1)}, bf16[64,4096]{1,0:T(8,128)(2,1)S(1)}, u32[]{:S(2)}, u32[]{:S(2)}) collective-permute-start(bf16[64,4096]{1,0:T(8,128)(2,1)S(1)} %collective-permute-done.15), channel_id=1, source_target_pairs={{0,2},{2,4},{4,6},{6,7},{7,5},{5,3},{3,1},{1,0},{8,10},{10,12},{12... | collective-permute-start | bytes 1572872 | tf_op jit(solution)/shard_map/ppermute | solution.py:57
  121.5 12.8 %collective-permute-start.19 = (bf16[1,128,1664]{2,1,0:T(8,128)(2,1)S(1)}, bf16[1,128,1664]{2,1,0:T(8,128)(2,1)S(1)}, u32[]{:S(2)}, u32[]{:S(2)}) collective-permute-start(bf16[1,128,1664]{2,1,0:T(8,128)(2,1)S(1)} %fusion.55), channel_id=1, source_target_pairs={{0,16},{8,24},{16,0},{24,8},{1,17},{9,25},{17,1},{25,9},{2,18},{10... | collective-permute-start | bytes 1277960 | tf_op jit(solution)/shard_map/ppermute | solution.py:77
  135.6 12.3 %collective-permute-start.21 = (bf16[1,128,1664]{2,1,0:T(8,128)(2,1)S(1)}, bf16[1,128,1664]{2,1,0:T(8,128)(2,1)S(1)}, u32[]{:S(2)}, u32[]{:S(2)}) collective-permute-start(bf16[1,128,1664]{2,1,0:T(8,128)(2,1)S(1)} %fusion.56), channel_id=1, source_target_pairs={{0,16},{8,24},{16,0},{24,8},{1,17},{9,25},{17,1},{25,9},{2,18},{10... | collective-permute-start | bytes 1277960 | tf_op jit(solution)/shard_map/ppermute | solution.py:77
  136.2 12.6 %collective-permute-start.22 = (bf16[2,128,1664]{2,1,0:T(8,128)(2,1)S(1)}, bf16[2,128,1664]{2,1,0:T(8,128)(2,1)S(1)}, u32[]{:S(2)}, u32[]{:S(2)}) collective-permute-start(bf16[2,128,1664]{2,1,0:T(8,128)(2,1)S(1)} %dynamic-slice_bitcast_fusion.2), channel_id=1, source_target_pairs={{0,8},{8,0},{16,24},{24,16},{1,9},{9,1},{17,25},{25,17},{2,10},{10... | collective-permute-start | bytes 2555912 | tf_op jit(solution)/shard_map/ppermute | solution.py:77
  149.1 12.8 %collective-permute-start.23 = (bf16[1,128,1664]{2,1,0:T(8,128)(2,1)S(1)}, bf16[1,128,1664]{2,1,0:T(8,128)(2,1)S(1)}, u32[]{:S(2)}, u32[]{:S(2)}) collective-permute-start(bf16[1,128,1664]{2,1,0:T(8,128)(2,1)S(1)} %fusion.57), channel_id=1, source_target_pairs={{0,16},{8,24},{16,0},{24,8},{1,17},{9,25},{17,1},{25,9},{2,18},{10... | collective-permute-start | bytes 1277960 | tf_op jit(solution)/shard_map/ppermute | solution.py:77
  150.4 12.4 %collective-permute-start.24 = (bf16[2,128,1664]{2,1,0:T(8,128)(2,1)S(1)}, bf16[2,128,1664]{2,1,0:T(8,128)(2,1)S(1)}, u32[]{:S(2)}, u32[]{:S(2)}) collective-permute-start(bf16[2,128,1664]{2,1,0:T(8,128)(2,1)S(1)} %dynamic-slice_bitcast_fusion.1), channel_id=1, source_target_pairs={{0,8},{8,0},{16,24},{24,16},{1,9},{9,1},{17,25},{25,17},{2,10},{10... | collective-permute-start | bytes 2555912 | tf_op jit(solution)/shard_map/ppermute | solution.py:77
  163.1 13.3 %collective-permute-start.25 = (bf16[1,128,1664]{2,1,0:T(8,128)(2,1)S(1)}, bf16[1,128,1664]{2,1,0:T(8,128)(2,1)S(1)}, u32[]{:S(2)}, u32[]{:S(2)}) collective-permute-start(bf16[1,128,1664]{2,1,0:T(8,128)(2,1)S(1)} %fusion.58), channel_id=1, source_target_pairs={{0,16},{8,24},{16,0},{24,8},{1,17},{9,25},{17,1},{25,9},{2,18},{10... | collective-permute-start | bytes 1277960 | tf_op jit(solution)/shard_map/ppermute | solution.py:77
  164.0 13.4 %collective-permute-start.26 = (bf16[2,128,1664]{2,1,0:T(8,128)(2,1)S(1)}, bf16[2,128,1664]{2,1,0:T(8,128)(2,1)S(1)}, u32[]{:S(2)}, u32[]{:S(2)}) collective-permute-start(bf16[2,128,1664]{2,1,0:T(8,128)(2,1)S(1)} %dynamic-slice_bitcast_fusion), channel_id=1, source_target_pairs={{0,8},{8,0},{16,24},{24,16},{1,9},{9,1},{17,25},{25,17},{2,10},{10... | collective-permute-start | bytes 2555912 | tf_op jit(solution)/shard_map/ppermute | solution.py:77
  178.3 13.0 %collective-permute-start.27 = (bf16[1,128,1664]{2,1,0:T(8,128)(2,1)}, bf16[1,128,1664]{2,1,0:T(8,128)(2,1)}, u32[]{:S(2)}, u32[]{:S(2)}) collective-permute-start(bf16[1,128,1664]{2,1,0:T(8,128)(2,1)} %fusion.59), channel_id=1, source_target_pairs={{0,16},{8,24},{16,0},{24,8},{1,17},{9,25},{17,1},{25,9},{2,18},{10... | collective-permute-start | bytes 1277960 | tf_op jit(solution)/shard_map/ppermute | solution.py:77
  181.3 18.1 %collective-permute-start.30 = (bf16[128,1664]{1,0:T(8,128)(2,1)S(1)}, bf16[128,1664]{1,0:T(8,128)(2,1)S(1)}, u32[]{:S(2)}, u32[]{:S(2)}) collective-permute-start(bf16[128,1664]{1,0:T(8,128)(2,1)S(1)} %get-tuple-element.128), channel_id=1, source_target_pairs={{0,24},{8,16},{16,8},{24,0},{1,25},{9,17},{17,9},{25,1},{2,26},{10... | collective-permute-start | bytes 1277960 | tf_op jit(solution)/shard_map/ppermute | solution.py:87
  182.0 27.0 %collective-permute-start.29 = (bf16[128,1664]{1,0:T(8,128)(2,1)S(1)}, bf16[128,1664]{1,0:T(8,128)(2,1)S(1)}, u32[]{:S(2)}, u32[]{:S(2)}) collective-permute-start(bf16[128,1664]{1,0:T(8,128)(2,1)S(1)} %get-tuple-element.129), channel_id=1, source_target_pairs={{0,16},{8,24},{16,0},{24,8},{1,17},{9,25},{17,1},{25,9},{2,18},{10... | collective-permute-start | bytes 1277960 | tf_op jit(solution)/shard_map/ppermute | solution.py:87
  (12 other events, 172.1 us)

commit v4 on v2

--- a/solution.py
+++ b/solution.py
@@ -5,7 +5,15 @@
 from jax.sharding import PartitionSpec as P
 
 HALVES = 2
-SPLIT_UNITS = 2
+
+
+def tile_widths(units, last):
+    half = units // 2
+    if not last:
+        return [half, units - half]
+    rest = units - half
+    small = max(128, (rest // 3) // 128 * 128)
+    return [half, rest - small, small]
 
 
 def ring_order(mesh):
@@ -91,18 +99,21 @@
         tc = local // HALVES
         group = n_col // n_row
         units = gate_weight.shape[1]
-        us = units // SPLIT_UNITS
 
         st = ring.init(tokens[:tc])
         for s in range(1, ring.steps + 1):
             st = ring.step(st, s)
         piece = ring.result(st)
+        piece, tokens = lax.optimization_barrier((piece, tokens))
 
         tiles = []
         for h in range(HALVES):
             for w in range(2):
-                for j in range(SPLIT_UNITS):
-                    tiles.append((h, w, j))
+                start = 0
+                for width in tile_widths(units, h == HALVES - 1 and w == 1):
+                    tiles.append((h, w, start, width))
+                    start += width
+        firsts = [i for i, tl in enumerate(tiles) if i == 0 or tl[0] != tiles[i - 1][0]]
 
         jobs = []
         done = {}
@@ -114,16 +125,15 @@
                 job[2] = reduce_level(job[2], levels[job[1]], n_row)
                 job[1] += 1
             if t < len(tiles):
-                h, w, j = tiles[t]
-                first_of_share = t % (2 * SPLIT_UNITS) == 0
-                if first_of_share and h + 1 < HALVES:
+                h, w, start, width = tiles[t]
+                if t in firsts and h + 1 < HALVES:
                     nxt = {"st": ring.init(tokens[(h + 1) * tc:(h + 2) * tc]), "s": 1}
                 if nxt is not None and nxt["s"] <= ring.steps:
                     nxt["st"] = ring.step(nxt["st"], nxt["s"])
                     nxt["s"] += 1
                 weight = gate_weight if w == 0 else up_weight
                 out = jnp.dot(
-                    piece, weight[:, j * us:(j + 1) * us], preferred_element_type=jnp.float32
+                    piece, weight[:, start:start + width], preferred_element_type=jnp.float32
                 ).astype(jnp.bfloat16)
                 new_job = [t, 0, out]
             else:
@@ -149,7 +159,7 @@
                 nxt["st"] = carry["nxt"]
             done = carry["done"]
             t += 1
-            if t < len(tiles) and t % (2 * SPLIT_UNITS) == 0 and nxt is not None:
+            if t < len(tiles) and t in firsts and nxt is not None:
                 while nxt["s"] <= ring.steps:
                     nxt["st"] = ring.step(nxt["st"], nxt["s"])
                     nxt["s"] += 1
@@ -159,8 +169,8 @@
         def assemble(w):
             parts = []
             for h in range(HALVES):
-                base = (h * 2 + w) * SPLIT_UNITS
-                parts.append(jnp.concatenate([done[base + j] for j in range(SPLIT_UNITS)], axis=1))
+                ids = [i for i, tl in enumerate(tiles) if tl[0] == h and tl[1] == w]
+                parts.append(jnp.concatenate([done[i] for i in ids], axis=1))
             x = jnp.stack(parts).reshape(HALVES, group, tc, units)
             return x.transpose(1, 0, 2, 3).reshape(group * HALVES * tc, units)
 

time: 204 us -> 203 us (level)
  local copies, waits for them, and re-layouts: 16.1 us -> 6.64 us
  waiting for transfers between devices: 47.7 us -> 56.2 us
    ppermute x8, waiting for transfers between devices: 26.7 us -> 34.6 us  [step(): f = lax.ppermute(st['f'], 'col', self.fwd_pairs)]
    dynamic_update_slice x8, local copies, waits for them, and re-layouts: 3.46 us -> 0.31 us  [step(): buf = lax.dynamic_update_slice(buf, f[None], (order_t[(p - s) % n], 0, 0))]
    dynamic_update_slice x6, local copies, waits for them, and re-layouts: 2.62 us -> 0.25 us  [step(): buf = lax.dynamic_update_slice(buf, b[None], (order_t[(p + s) % n], 0, 0))]
    slice x1, local copies, waits for them, and re-layouts: 2.37 us -> 0.04 us  [on_device(): nxt = {'st': ring.init(tokens[(h + 1) * tc:(h + 2) * tc]), 's': 1}]
    dot_general x8 -> x9, matrix products: 91.3 us -> 90.5 us  [on_device(): jnp.dot(piece, weight[:, start:start + width], preferred_element_type=jnp...]
    ppermute x16 -> x18, waiting for transfers between devices: 20.9 us -> 21.6 us  [reduce_level(): lax.ppermute(send.astype(jnp.bfloat16), 'row', [(i, i ^ d) for i in range...]
    ppermute x16 -> x18, starting transfers between devices: 9.95 us -> 9.74 us  [reduce_level(): lax.ppermute(send.astype(jnp.bfloat16), 'row', [(i, i ^ d) for i in range...]
  transfers between devices with their start and end apart: 30 -> 32, of which waited for: 8 -> 11; matrix products, arithmetic and copies ran while one was open for 45% -> 47% of each run, Pallas kernels for 0% -> 0%
where the time goes in v4:
time: 203 us
  matrix products  90.5 us (45%)
  waiting for transfers between devices  56.2 us (28%)
  starting transfers between devices  25.2 us (12%)
  between operations  18.5 us (9%)
  local copies, waits for them, and re-layouts  6.64 us (3%)
  other arithmetic  5.47 us (3%)
    dot_general x9, matrix products, on_device(): jnp.dot(piece, weight[:, start:start + width], preferred_element_type=jnp...  90.5 us
    ppermute x8, waiting for transfers between devices, step(): f = lax.ppermute(st['f'], 'col', self.fwd_pairs)  34.6 us
    ppermute x18, waiting for transfers between devices, reduce_level(): lax.ppermute(send.astype(jnp.bfloat16), 'row', [(i, i ^ d) for i in range...  21.6 us
    ppermute x8, starting transfers between devices, step(): f = lax.ppermute(st['f'], 'col', self.fwd_pairs)  11.7 us
    ppermute x18, starting transfers between devices, reduce_level(): lax.ppermute(send.astype(jnp.bfloat16), 'row', [(i, i ^ d) for i in range...  9.74 us
  transfers between devices with their start and end apart: 32, of which 11 were waited for; matrix products, arithmetic and copies ran while one was open for 47% of the time, Pallas kernels for 0%

profile of v4, /device:TPU:0, one launch (start us, length us, event | category | flops | bytes accessed | tf_op | source)
XLA Modules:
  0.0 202.6 jit_solution(1751561424389059460)
XLA Ops:
  1.2 3.1 %collective-permute-start = (bf16[64,4096]{1,0:T(8,128)(2,1)S(1)}, bf16[64,4096]{1,0:T(8,128)(2,1)S(1)}, u32[]{:S(2)}, u32[]{:S(2)}) collective-permute-start(bf16[64,4096]{1,0:T(8,128)(2,1)S(1)} %slice.27), channel_id=1, source_target_pairs={{0,2},{2,4},{4,6},{6,7},{7,5},{5,3},{3,1},{1,0},{8,10},{10,12},{12... | collective-permute-start | bytes 1572872 | tf_op jit(solution)/shard_map/ppermute | solution.py:65
  10.2 1.6 fusion.67
  25.5 2.1 %collective-permute-start.2 = (bf16[64,4096]{1,0:T(8,128)(2,1)S(1)}, bf16[64,4096]{1,0:T(8,128)(2,1)S(1)}, u32[]{:S(2)}, u32[]{:S(2)}) collective-permute-start(bf16[64,4096]{1,0:T(8,128)(2,1)S(1)} %collective-permute-done), channel_id=1, source_target_pairs={{0,2},{2,4},{4,6},{6,7},{7,5},{5,3},{3,1},{1,0},{8,10},{10,12},{12... | collective-permute-start | bytes 1572872 | tf_op jit(solution)/shard_map/ppermute | solution.py:65
  27.6 11.3 %collective-permute-done.2 = bf16[64,4096]{1,0:T(8,128)(2,1)S(1)} collective-permute-done((bf16[64,4096]{1,0:T(8,128)(2,1)S(1)}, bf16[64,4096]{1,0:T(8,128)(2,1)S(1)}, u32[]{:S(2)}, u32[]{:S(2)}) %collective-permute-start.2) | collective-permute-done | bytes 524320 | tf_op jit(solution)/shard_map/ppermute | solution.py:65
  38.9 1.7 collective-permute-start.4
  41.0 10.4 %collective-permute-done.4 = bf16[64,4096]{1,0:T(8,128)(2,1)S(1)} collective-permute-done((bf16[64,4096]{1,0:T(8,128)(2,1)S(1)}, bf16[64,4096]{1,0:T(8,128)(2,1)S(1)}, u32[]{:S(2)}, u32[]{:S(2)}) %collective-permute-start.4) | collective-permute-done | bytes 524320 | tf_op jit(solution)/shard_map/ppermute | solution.py:65
  53.0 10.4 %collective-permute-done.6 = bf16[64,4096]{1,0:T(8,128)(2,1)S(1)} collective-permute-done((bf16[64,4096]{1,0:T(8,128)(2,1)S(1)}, bf16[64,4096]{1,0:T(8,128)(2,1)S(1)}, u32[]{:S(2)}, u32[]{:S(2)}) %collective-permute-start.6) | collective-permute-done | bytes 524320 | tf_op jit(solution)/shard_map/ppermute | solution.py:65
  63.5 1.5 collective-permute-start.8
  65.6 11.1 %fusion.22 = bf16[512,1664]{1,0:T(8,128)(2,1)S(1)} fusion(bf16[512,4096]{1,0:T(8,128)(2,1)S(1)} %bitcast.249, bf16[4096,3328]{1,0:T(8,128)(2,1)} %param.13), kind=kOutput, calls=%fused_computation.27 | convolution fusion | flops 6980173824 | bytes 19529728 | tf_op jit(solution)/shard_map/dot_general | solution.py:135
  79.5 11.1 %fusion.28 = bf16[512,1664]{1,0:T(8,128)(2,1)S(1)} fusion(bf16[512,4096]{1,0:T(8,128)(2,1)S(1)} %bitcast.250, bf16[4096,3328]{1,0:T(8,128)(2,1)} %param.13), kind=kOutput, calls=%fused_computation.29 | convolution fusion | flops 6980173824 | bytes 19529728 | tf_op jit(solution)/shard_map/dot_general | solution.py:135
  94.6 11.1 %fusion.34 = bf16[512,1664]{1,0:T(8,128)(2,1)S(1)} fusion(bf16[512,4096]{1,0:T(8,128)(2,1)S(1)} %bitcast.251, bf16[4096,3328]{1,0:T(8,128)(2,1)} %param.14), kind=kOutput, calls=%fused_computation.31 | convolution fusion | flops 6980173824 | bytes 19529728 | tf_op jit(solution)/shard_map/dot_general | solution.py:135
  105.8 1.9 collective-permute-done.15
  109.4 11.1 %fusion.40 = bf16[512,1664]{1,0:T(8,128)(2,1)S(1)} fusion(bf16[512,4096]{1,0:T(8,128)(2,1)S(1)} %bitcast.252, bf16[4096,3328]{1,0:T(8,128)(2,1)} %param.14), kind=kOutput, calls=%fused_computation.33 | convolution fusion | flops 6980173824 | bytes 19529728 | tf_op jit(solution)/shard_map/dot_general | solution.py:135
  121.6 1.6 collective-permute-start.19
  123.3 11.1 %fusion.25 = bf16[512,1664]{1,0:T(8,128)(2,1)S(1)} fusion(bf16[512,4096]{1,0:T(8,128)(2,1)S(1)} %bitcast.244, bf16[4096,3328]{1,0:T(8,128)(2,1)} %param.13), kind=kOutput, calls=%fused_computation.28 | convolution fusion | flops 6980173824 | bytes 19529728 | tf_op jit(solution)/shard_map/dot_general | solution.py:135
  135.6 11.1 %fusion.31 = bf16[512,1664]{1,0:T(8,128)(2,1)S(1)} fusion(bf16[512,4096]{1,0:T(8,128)(2,1)S(1)} %bitcast.245, bf16[4096,3328]{1,0:T(8,128)(2,1)} %param.13), kind=kOutput, calls=%fused_computation.30 | convolution fusion | flops 6980173824 | bytes 19529728 | tf_op jit(solution)/shard_map/dot_general | solution.py:135
  148.8 11.3 %fusion.37 = bf16[512,1664]{1,0:T(8,128)(2,1)S(1)} fusion(bf16[512,4096]{1,0:T(8,128)(2,1)S(1)} %bitcast.246, bf16[4096,3328]{1,0:T(8,128)(2,1)} %param.14), kind=kOutput, calls=%fused_computation.32 | convolution fusion | flops 6980173824 | bytes 19529728 | tf_op jit(solution)/shard_map/dot_general | solution.py:135
  161.4 8.3 %fusion.43 = bf16[512,1152]{1,0:T(8,128)(2,1)S(1)} fusion(bf16[512,4096]{1,0:T(8,128)(2,1)S(1)} %bitcast.247, bf16[4096,3328]{1,0:T(8,128)(2,1)} %param.14), kind=kOutput, calls=%fused_computation.34 | convolution fusion | flops 4832428032 | bytes 14811136 | tf_op jit(solution)/shard_map/dot_general | solution.py:135
  169.7 2.8 %collective-permute-done.25 = bf16[1,128,1664]{2,1,0:T(8,128)(2,1)S(1)} collective-permute-done((bf16[1,128,1664]{2,1,0:T(8,128)(2,1)S(1)}, bf16[1,128,1664]{2,1,0:T(8,128)(2,1)S(1)}, u32[]{:S(2)}, u32[]{:S(2)}) %collective-permute-start.25) | collective-permute-done | bytes 426016 | tf_op jit(solution)/shard_map/ppermute | solution.py:85
  173.9 4.5 %fusion.46 = bf16[512,512]{1,0:T(8,128)(2,1)S(1)} fusion(bf16[512,4096]{1,0:T(8,128)(2,1)S(1)} %bitcast.248, bf16[4096,3328]{1,0:T(8,128)(2,1)} %param.14), kind=kOutput, calls=%fused_computation.46 | convolution fusion | flops 2147745792 | bytes 8912896 | tf_op jit(solution)/shard_map/dot_general | solution.py:135
  178.4 5.7 %collective-permute-done.27 = bf16[1,128,1664]{2,1,0:T(8,128)(2,1)S(1)} collective-permute-done((bf16[1,128,1664]{2,1,0:T(8,128)(2,1)S(1)}, bf16[1,128,1664]{2,1,0:T(8,128)(2,1)S(1)}, u32[]{:S(2)}, u32[]{:S(2)}) %collective-permute-start.27) | collective-permute-done | bytes 426016 | tf_op jit(solution)/shard_map/ppermute | solution.py:85
  186.0 7.9 %collective-permute-done.29 = bf16[1,128,1152]{2,1,0:T(8,128)(2,1)S(1)} collective-permute-done((bf16[1,128,1152]{2,1,0:T(8,128)(2,1)S(1)}, bf16[1,128,1152]{2,1,0:T(8,128)(2,1)S(1)}, u32[]{:S(2)}, u32[]{:S(2)}) %collective-permute-start.29) | collective-permute-done | bytes 294944 | tf_op jit(solution)/shard_map/ppermute | solution.py:85
  194.9 4.3 %collective-permute-done.31 = bf16[1,128,512]{2,1,0:T(8,128)(2,1)S(1)} collective-permute-done((bf16[1,128,512]{2,1,0:T(8,128)(2,1)S(1)}, bf16[1,128,512]{2,1,0:T(8,128)(2,1)S(1)}, u32[]{:S(2)}, u32[]{:S(2)}) %collective-permute-start.31) | collective-permute-done | bytes 131104 | tf_op jit(solution)/shard_map/ppermute | solution.py:85
  200.4 2.2 %fusion.18 = bf16[256,3328]{1,0:T(8,128)(2,1)} fusion(f32[2,2,64,3328]{3,2,0,1:T(8,128)S(1)} %pad_maximum_fusion.1, f32[2,2,64,3328]{3,2,0,1:T(8,128)S(1)} %pad_maximum_fusion), kind=kLoop, calls=%fused_computation.21 | loop fusion | flops 5111808 | bytes 8519680 | tf_op jit(solution)/shard_map/convert_element_type | solution.py:179
  (114 shorter events, 25.1 us)
Async XLA Ops:
  1.2 24.3 %collective-permute-start = (bf16[64,4096]{1,0:T(8,128)(2,1)S(1)}, bf16[64,4096]{1,0:T(8,128)(2,1)S(1)}, u32[]{:S(2)}, u32[]{:S(2)}) collective-permute-start(bf16[64,4096]{1,0:T(8,128)(2,1)S(1)} %slice.27), channel_id=1, source_target_pairs={{0,2},{2,4},{4,6},{6,7},{7,5},{5,3},{3,1},{1,0},{8,10},{10,12},{12... | collective-permute-start | bytes 1572872 | tf_op jit(solution)/shard_map/ppermute | solution.py:65
  4.3 23.3 %collective-permute-start.1 = (bf16[64,4096]{1,0:T(8,128)(2,1)S(1)}, bf16[64,4096]{1,0:T(8,128)(2,1)S(1)}, u32[]{:S(2)}, u32[]{:S(2)}) collective-permute-start(bf16[64,4096]{1,0:T(8,128)(2,1)S(1)} %slice.27), channel_id=1, source_target_pairs={{0,1},{2,0},{4,2},{6,4},{7,6},{5,7},{3,5},{1,3},{8,9},{10,8},{12,1... | collective-permute-start | bytes 1572872 | tf_op jit(solution)/shard_map/ppermute | solution.py:69
  25.5 13.4 %collective-permute-start.2 = (bf16[64,4096]{1,0:T(8,128)(2,1)S(1)}, bf16[64,4096]{1,0:T(8,128)(2,1)S(1)}, u32[]{:S(2)}, u32[]{:S(2)}) collective-permute-start(bf16[64,4096]{1,0:T(8,128)(2,1)S(1)} %collective-permute-done), channel_id=1, source_target_pairs={{0,2},{2,4},{4,6},{6,7},{7,5},{5,3},{3,1},{1,0},{8,10},{10,12},{12... | collective-permute-start | bytes 1572872 | tf_op jit(solution)/shard_map/ppermute | solution.py:65
  27.6 13.1 %collective-permute-start.3 = (bf16[64,4096]{1,0:T(8,128)(2,1)S(1)}, bf16[64,4096]{1,0:T(8,128)(2,1)S(1)}, u32[]{:S(2)}, u32[]{:S(2)}) collective-permute-start(bf16[64,4096]{1,0:T(8,128)(2,1)S(1)} %collective-permute-done.1), channel_id=1, source_target_pairs={{0,1},{2,0},{4,2},{6,4},{7,6},{5,7},{3,5},{1,3},{8,9},{10,8},{12,1... | collective-permute-start | bytes 1572872 | tf_op jit(solution)/shard_map/ppermute | solution.py:69
  38.9 12.5 %collective-permute-start.4 = (bf16[64,4096]{1,0:T(8,128)(2,1)S(1)}, bf16[64,4096]{1,0:T(8,128)(2,1)S(1)}, u32[]{:S(2)}, u32[]{:S(2)}) collective-permute-start(bf16[64,4096]{1,0:T(8,128)(2,1)S(1)} %collective-permute-done.2), channel_id=1, source_target_pairs={{0,2},{2,4},{4,6},{6,7},{7,5},{5,3},{3,1},{1,0},{8,10},{10,12},{12... | collective-permute-start | bytes 1572872 | tf_op jit(solution)/shard_map/ppermute | solution.py:65
  40.7 12.3 %collective-permute-start.5 = (bf16[64,4096]{1,0:T(8,128)(2,1)S(1)}, bf16[64,4096]{1,0:T(8,128)(2,1)S(1)}, u32[]{:S(2)}, u32[]{:S(2)}) collective-permute-start(bf16[64,4096]{1,0:T(8,128)(2,1)S(1)} %collective-permute-done.3), channel_id=1, source_target_pairs={{0,1},{2,0},{4,2},{6,4},{7,6},{5,7},{3,5},{1,3},{8,9},{10,8},{12,1... | collective-permute-start | bytes 1572872 | tf_op jit(solution)/shard_map/ppermute | solution.py:69
  51.4 12.0 %collective-permute-start.6 = (bf16[64,4096]{1,0:T(8,128)(2,1)S(1)}, bf16[64,4096]{1,0:T(8,128)(2,1)S(1)}, u32[]{:S(2)}, u32[]{:S(2)}) collective-permute-start(bf16[64,4096]{1,0:T(8,128)(2,1)S(1)} %collective-permute-done.4), channel_id=1, source_target_pairs={{0,2},{2,4},{4,6},{6,7},{7,5},{5,3},{3,1},{1,0},{8,10},{10,12},{12... | collective-permute-start | bytes 1572872 | tf_op jit(solution)/shard_map/ppermute | solution.py:65
  63.5 13.7 %collective-permute-start.8 = (bf16[64,4096]{1,0:T(8,128)(2,1)S(1)}, bf16[64,4096]{1,0:T(8,128)(2,1)S(1)}, u32[]{:S(2)}, u32[]{:S(2)}) collective-permute-start(bf16[64,4096]{1,0:T(8,128)(2,1)S(1)} %slice.29), channel_id=1, source_target_pairs={{0,2},{2,4},{4,6},{6,7},{7,5},{5,3},{3,1},{1,0},{8,10},{10,12},{12... | collective-permute-start | bytes 1572872 | tf_op jit(solution)/shard_map/ppermute | solution.py:65
  65.0 12.3 %collective-permute-start.7 = (bf16[64,4096]{1,0:T(8,128)(2,1)S(1)}, bf16[64,4096]{1,0:T(8,128)(2,1)S(1)}, u32[]{:S(2)}, u32[]{:S(2)}) collective-permute-start(bf16[64,4096]{1,0:T(8,128)(2,1)S(1)} %slice.29), channel_id=1, source_target_pairs={{0,1},{2,0},{4,2},{6,4},{7,6},{5,7},{3,5},{1,3},{8,9},{10,8},{12,1... | collective-permute-start | bytes 1572872 | tf_op jit(solution)/shard_map/ppermute | solution.py:69
  77.3 13.4 %collective-permute-start.10 = (bf16[64,4096]{1,0:T(8,128)(2,1)S(1)}, bf16[64,4096]{1,0:T(8,128)(2,1)S(1)}, u32[]{:S(2)}, u32[]{:S(2)}) collective-permute-start(bf16[64,4096]{1,0:T(8,128)(2,1)S(1)} %collective-permute-done.7), channel_id=1, source_target_pairs={{0,1},{2,0},{4,2},{6,4},{7,6},{5,7},{3,5},{1,3},{8,9},{10,8},{12,1... | collective-permute-start | bytes 1572872 | tf_op jit(solution)/shard_map/ppermute | solution.py:69
  78.7 11.9 %collective-permute-start.11 = (bf16[64,4096]{1,0:T(8,128)(2,1)S(1)}, bf16[64,4096]{1,0:T(8,128)(2,1)S(1)}, u32[]{:S(2)}, u32[]{:S(2)}) collective-permute-start(bf16[64,4096]{1,0:T(8,128)(2,1)S(1)} %collective-permute-done.8), channel_id=1, source_target_pairs={{0,2},{2,4},{4,6},{6,7},{7,5},{5,3},{3,1},{1,0},{8,10},{10,12},{12... | collective-permute-start | bytes 1572872 | tf_op jit(solution)/shard_map/ppermute | solution.py:65
  91.0 14.7 %collective-permute-start.12 = (bf16[1,128,1664]{2,1,0:T(8,128)(2,1)S(1)}, bf16[1,128,1664]{2,1,0:T(8,128)(2,1)S(1)}, u32[]{:S(2)}, u32[]{:S(2)}) collective-permute-start(bf16[1,128,1664]{2,1,0:T(8,128)(2,1)S(1)} %fusion.57), channel_id=1, source_target_pairs={{0,16},{8,24},{16,0},{24,8},{1,17},{9,25},{17,1},{25,9},{2,18},{10... | collective-permute-start | bytes 1277960 | tf_op jit(solution)/shard_map/ppermute | solution.py:85
  92.5 15.3 %collective-permute-start.14 = (bf16[64,4096]{1,0:T(8,128)(2,1)S(1)}, bf16[64,4096]{1,0:T(8,128)(2,1)S(1)}, u32[]{:S(2)}, u32[]{:S(2)}) collective-permute-start(bf16[64,4096]{1,0:T(8,128)(2,1)S(1)} %collective-permute-done.10), channel_id=1, source_target_pairs={{0,1},{2,0},{4,2},{6,4},{7,6},{5,7},{3,5},{1,3},{8,9},{10,8},{12,1... | collective-permute-start | bytes 1572872 | tf_op jit(solution)/shard_map/ppermute | solution.py:69
  93.9 13.8 %collective-permute-start.15 = (bf16[64,4096]{1,0:T(8,128)(2,1)S(1)}, bf16[64,4096]{1,0:T(8,128)(2,1)S(1)}, u32[]{:S(2)}, u32[]{:S(2)}) collective-permute-start(bf16[64,4096]{1,0:T(8,128)(2,1)S(1)} %collective-permute-done.11), channel_id=1, source_target_pairs={{0,2},{2,4},{4,6},{6,7},{7,5},{5,3},{3,1},{1,0},{8,10},{10,12},{12... | collective-permute-start | bytes 1572872 | tf_op jit(solution)/shard_map/ppermute | solution.py:65
  94.5 13.3 %collective-permute-start.13 = (bf16[2,128,1664]{2,1,0:T(8,128)(2,1)S(1)}, bf16[2,128,1664]{2,1,0:T(8,128)(2,1)S(1)}, u32[]{:S(2)}, u32[]{:S(2)}) collective-permute-start(bf16[2,128,1664]{2,1,0:T(8,128)(2,1)S(1)} %dynamic-slice_bitcast_fusion.5), channel_id=1, source_target_pairs={{0,8},{8,0},{16,24},{24,16},{1,9},{9,1},{17,25},{25,17},{2,10},{10... | collective-permute-start | bytes 2555912 | tf_op jit(solution)/shard_map/ppermute | solution.py:85
  108.1 12.5 %collective-permute-start.16 = (bf16[1,128,1664]{2,1,0:T(8,128)(2,1)S(1)}, bf16[1,128,1664]{2,1,0:T(8,128)(2,1)S(1)}, u32[]{:S(2)}, u32[]{:S(2)}) collective-permute-start(bf16[1,128,1664]{2,1,0:T(8,128)(2,1)S(1)} %fusion.58), channel_id=1, source_target_pairs={{0,16},{8,24},{16,0},{24,8},{1,17},{9,25},{17,1},{25,9},{2,18},{10... | collective-permute-start | bytes 1277960 | tf_op jit(solution)/shard_map/ppermute | solution.py:85
  108.6 12.6 %collective-permute-start.18 = (bf16[64,4096]{1,0:T(8,128)(2,1)S(1)}, bf16[64,4096]{1,0:T(8,128)(2,1)S(1)}, u32[]{:S(2)}, u32[]{:S(2)}) collective-permute-start(bf16[64,4096]{1,0:T(8,128)(2,1)S(1)} %collective-permute-done.15), channel_id=1, source_target_pairs={{0,2},{2,4},{4,6},{6,7},{7,5},{5,3},{3,1},{1,0},{8,10},{10,12},{12... | collective-permute-start | bytes 1572872 | tf_op jit(solution)/shard_map/ppermute | solution.py:65
  109.4 12.0 %collective-permute-start.17 = (bf16[2,128,1664]{2,1,0:T(8,128)(2,1)S(1)}, bf16[2,128,1664]{2,1,0:T(8,128)(2,1)S(1)}, u32[]{:S(2)}, u32[]{:S(2)}) collective-permute-start(bf16[2,128,1664]{2,1,0:T(8,128)(2,1)S(1)} %dynamic-slice_bitcast_fusion.4), channel_id=1, source_target_pairs={{0,8},{8,0},{16,24},{24,16},{1,9},{9,1},{17,25},{25,17},{2,10},{10... | collective-permute-start | bytes 2555912 | tf_op jit(solution)/shard_map/ppermute | solution.py:85
  121.6 12.8 %collective-permute-start.19 = (bf16[1,128,1664]{2,1,0:T(8,128)(2,1)S(1)}, bf16[1,128,1664]{2,1,0:T(8,128)(2,1)S(1)}, u32[]{:S(2)}, u32[]{:S(2)}) collective-permute-start(bf16[1,128,1664]{2,1,0:T(8,128)(2,1)S(1)} %fusion.59), channel_id=1, source_target_pairs={{0,16},{8,24},{16,0},{24,8},{1,17},{9,25},{17,1},{25,9},{2,18},{10... | collective-permute-start | bytes 1277960 | tf_op jit(solution)/shard_map/ppermute | solution.py:85
  134.7 12.3 %collective-permute-start.21 = (bf16[1,128,1664]{2,1,0:T(8,128)(2,1)S(1)}, bf16[1,128,1664]{2,1,0:T(8,128)(2,1)S(1)}, u32[]{:S(2)}, u32[]{:S(2)}) collective-permute-start(bf16[1,128,1664]{2,1,0:T(8,128)(2,1)S(1)} %fusion.60), channel_id=1, source_target_pairs={{0,16},{8,24},{16,0},{24,8},{1,17},{9,25},{17,1},{25,9},{2,18},{10... | collective-permute-start | bytes 1277960 | tf_op jit(solution)/shard_map/ppermute | solution.py:85
  135.4 11.7 %collective-permute-start.22 = (bf16[2,128,1664]{2,1,0:T(8,128)(2,1)S(1)}, bf16[2,128,1664]{2,1,0:T(8,128)(2,1)S(1)}, u32[]{:S(2)}, u32[]{:S(2)}) collective-permute-start(bf16[2,128,1664]{2,1,0:T(8,128)(2,1)S(1)} %dynamic-slice_bitcast_fusion.2), channel_id=1, source_target_pairs={{0,8},{8,0},{16,24},{24,16},{1,9},{9,1},{17,25},{25,17},{2,10},{10... | collective-permute-start | bytes 2555912 | tf_op jit(solution)/shard_map/ppermute | solution.py:85
  147.3 12.8 %collective-permute-start.23 = (bf16[1,128,1664]{2,1,0:T(8,128)(2,1)S(1)}, bf16[1,128,1664]{2,1,0:T(8,128)(2,1)S(1)}, u32[]{:S(2)}, u32[]{:S(2)}) collective-permute-start(bf16[1,128,1664]{2,1,0:T(8,128)(2,1)S(1)} %fusion.61), channel_id=1, source_target_pairs={{0,16},{8,24},{16,0},{24,8},{1,17},{9,25},{17,1},{25,9},{2,18},{10... | collective-permute-start | bytes 1277960 | tf_op jit(solution)/shard_map/ppermute | solution.py:85
  148.7 11.5 %collective-permute-start.24 = (bf16[2,128,1664]{2,1,0:T(8,128)(2,1)S(1)}, bf16[2,128,1664]{2,1,0:T(8,128)(2,1)S(1)}, u32[]{:S(2)}, u32[]{:S(2)}) collective-permute-start(bf16[2,128,1664]{2,1,0:T(8,128)(2,1)S(1)} %dynamic-slice_bitcast_fusion.1), channel_id=1, source_target_pairs={{0,8},{8,0},{16,24},{24,16},{1,9},{9,1},{17,25},{25,17},{2,10},{10... | collective-permute-start | bytes 2555912 | tf_op jit(solution)/shard_map/ppermute | solution.py:85
  160.5 12.1 %collective-permute-start.25 = (bf16[1,128,1664]{2,1,0:T(8,128)(2,1)S(1)}, bf16[1,128,1664]{2,1,0:T(8,128)(2,1)S(1)}, u32[]{:S(2)}, u32[]{:S(2)}) collective-permute-start(bf16[1,128,1664]{2,1,0:T(8,128)(2,1)S(1)} %fusion.62), channel_id=1, source_target_pairs={{0,16},{8,24},{16,0},{24,8},{1,17},{9,25},{17,1},{25,9},{2,18},{10... | collective-permute-start | bytes 1277960 | tf_op jit(solution)/shard_map/ppermute | solution.py:85
  (9 other events, 96.9 us)

commit v5 on v4

--- a/solution.py
+++ b/solution.py
@@ -62,9 +62,17 @@
         p = jnp.asarray(self.pos)[c]
         order_t = jnp.asarray(np.array(self.order, np.int32))
         buf = st["buf"]
+        b = st["b"]
+        if s == self.steps and self.back_steps < s and n > 2:
+            k2 = b.shape[1] // 2
+            f = lax.ppermute(st["f"][:, :k2], "col", self.fwd_pairs)
+            b = lax.ppermute(b[:, k2:], "col", self.bwd_pairs)
+            src = order_t[(p - s) % n]
+            buf = lax.dynamic_update_slice(buf, f[None], (src, 0, 0))
+            buf = lax.dynamic_update_slice(buf, b[None], (src, 0, k2))
+            return {"buf": buf, "f": f, "b": b}
         f = lax.ppermute(st["f"], "col", self.fwd_pairs)
         buf = lax.dynamic_update_slice(buf, f[None], (order_t[(p - s) % n], 0, 0))
-        b = st["b"]
         if s <= self.back_steps:
             b = lax.ppermute(b, "col", self.bwd_pairs)
             buf = lax.dynamic_update_slice(buf, b[None], (order_t[(p + s) % n], 0, 0))

time: 203 us -> 199 us (0.980)
  waiting for transfers between devices: 56.2 us -> 50.1 us
  starting transfers between devices: 25.2 us -> 27.9 us
    ppermute x8 -> x6, waiting for transfers between devices: 34.6 us -> 23.1 us  [step(): f = lax.ppermute(st['f'], 'col', self.fwd_pairs)]
    ppermute x0 -> x4, waiting for transfers between devices: none -> 5.69 us  [the longest x2 4.18 us: step(): f = lax.ppermute(st['f'][:, :k2], 'col', self.fwd_pairs)]
    ppermute x0 -> x4, starting transfers between devices: none -> 4.21 us  [the longest x2 2.61 us: step(): f = lax.ppermute(st['f'][:, :k2], 'col', self.fwd_pairs)]
    ppermute x8 -> x6, starting transfers between devices: 11.7 us -> 11.3 us  [step(): f = lax.ppermute(st['f'], 'col', self.fwd_pairs)]
  transfers between devices with their start and end apart: 32 -> 34, of which waited for: 11 -> 10; matrix products, arithmetic and copies ran while one was open for 47% -> 48% of each run, Pallas kernels for 0% -> 0%
where the time goes in v5:
time: 199 us
  matrix products  90.4 us (45%)
  waiting for transfers between devices  50.1 us (25%)
  starting transfers between devices  27.9 us (14%)
  between operations  18.5 us (9%)
  local copies, waits for them, and re-layouts  6.72 us (3%)
  other arithmetic  5.37 us (3%)
    dot_general x9, matrix products, on_device(): jnp.dot(piece, weight[:, start:start + width], preferred_element_type=jnp...  90.4 us
    ppermute x6, waiting for transfers between devices, step(): f = lax.ppermute(st['f'], 'col', self.fwd_pairs)  23.1 us
    ppermute x18, waiting for transfers between devices, reduce_level(): lax.ppermute(send.astype(jnp.bfloat16), 'row', [(i, i ^ d) for i in range...  21.4 us
    ppermute x6, starting transfers between devices, step(): f = lax.ppermute(st['f'], 'col', self.fwd_pairs)  11.3 us
    ppermute x18, starting transfers between devices, reduce_level(): lax.ppermute(send.astype(jnp.bfloat16), 'row', [(i, i ^ d) for i in range...  10.3 us
    ppermute x2, waiting for transfers between devices, step(): f = lax.ppermute(st['f'][:, :k2], 'col', self.fwd_pairs)  4.18 us
  transfers between devices with their start and end apart: 34, of which 10 were waited for; matrix products, arithmetic and copies ran while one was open for 48% of the time, Pallas kernels for 0%

profile of v5, /device:TPU:0, one launch (start us, length us, event | category | flops | bytes accessed | tf_op | source)
XLA Modules:
  0.0 198.9 jit_solution(5236610476127860658)
XLA Ops:
  1.2 3.1 %collective-permute-start = (bf16[64,4096]{1,0:T(8,128)(2,1)S(1)}, bf16[64,4096]{1,0:T(8,128)(2,1)S(1)}, u32[]{:S(2)}, u32[]{:S(2)}) collective-permute-start(bf16[64,4096]{1,0:T(8,128)(2,1)S(1)} %slice.39), channel_id=1, source_target_pairs={{0,2},{2,4},{4,6},{6,7},{7,5},{5,3},{3,1},{1,0},{8,10},{10,12},{12... | collective-permute-start | bytes 1572872 | tf_op jit(solution)/shard_map/ppermute | solution.py:74
  10.2 1.6 fusion.67
  25.4 2.1 %collective-permute-start.2 = (bf16[64,4096]{1,0:T(8,128)(2,1)S(1)}, bf16[64,4096]{1,0:T(8,128)(2,1)S(1)}, u32[]{:S(2)}, u32[]{:S(2)}) collective-permute-start(bf16[64,4096]{1,0:T(8,128)(2,1)S(1)} %collective-permute-done), channel_id=1, source_target_pairs={{0,2},{2,4},{4,6},{6,7},{7,5},{5,3},{3,1},{1,0},{8,10},{10,12},{12... | collective-permute-start | bytes 1572872 | tf_op jit(solution)/shard_map/ppermute | solution.py:74
  27.6 11.3 %collective-permute-done.2 = bf16[64,4096]{1,0:T(8,128)(2,1)S(1)} collective-permute-done((bf16[64,4096]{1,0:T(8,128)(2,1)S(1)}, bf16[64,4096]{1,0:T(8,128)(2,1)S(1)}, u32[]{:S(2)}, u32[]{:S(2)}) %collective-permute-start.2) | collective-permute-done | bytes 524320 | tf_op jit(solution)/shard_map/ppermute | solution.py:74
  38.8 1.7 collective-permute-start.4
  41.0 10.4 %collective-permute-done.4 = bf16[64,4096]{1,0:T(8,128)(2,1)S(1)} collective-permute-done((bf16[64,4096]{1,0:T(8,128)(2,1)S(1)}, bf16[64,4096]{1,0:T(8,128)(2,1)S(1)}, u32[]{:S(2)}, u32[]{:S(2)}) %collective-permute-start.4) | collective-permute-done | bytes 524320 | tf_op jit(solution)/shard_map/ppermute | solution.py:74
  53.6 4.2 %collective-permute-done.6 = bf16[64,2048]{1,0:T(8,128)(2,1)S(1)} collective-permute-done((bf16[64,2048]{1,0:T(8,128)(2,1)S(1)}, bf16[64,2048]{1,0:T(8,128)(2,1)S(1)}, u32[]{:S(2)}, u32[]{:S(2)}) %collective-permute-start.6) | collective-permute-done | bytes 262176 | tf_op jit(solution)/shard_map/ppermute | solution.py:68
  59.4 1.6 collective-permute-start.9
  61.5 11.1 %fusion.22 = bf16[512,1664]{1,0:T(8,128)(2,1)S(1)} fusion(bf16[512,4096]{1,0:T(8,128)(2,1)S(1)} %bitcast.253, bf16[4096,3328]{1,0:T(8,128)(2,1)} %param.13), kind=kOutput, calls=%fused_computation.27 | convolution fusion | flops 6980173824 | bytes 19529728 | tf_op jit(solution)/shard_map/dot_general | solution.py:143
  75.5 11.1 %fusion.28 = bf16[512,1664]{1,0:T(8,128)(2,1)S(1)} fusion(bf16[512,4096]{1,0:T(8,128)(2,1)S(1)} %bitcast.254, bf16[4096,3328]{1,0:T(8,128)(2,1)} %param.13), kind=kOutput, calls=%fused_computation.29 | convolution fusion | flops 6980173824 | bytes 19529728 | tf_op jit(solution)/shard_map/dot_general | solution.py:143
  86.9 1.6 collective-permute-start.13
  90.7 11.1 %fusion.34 = bf16[512,1664]{1,0:T(8,128)(2,1)S(1)} fusion(bf16[512,4096]{1,0:T(8,128)(2,1)S(1)} %bitcast.255, bf16[4096,3328]{1,0:T(8,128)(2,1)} %param.14), kind=kOutput, calls=%fused_computation.31 | convolution fusion | flops 6980173824 | bytes 19529728 | tf_op jit(solution)/shard_map/dot_general | solution.py:143
  106.3 11.1 %fusion.40 = bf16[512,1664]{1,0:T(8,128)(2,1)S(1)} fusion(bf16[512,4096]{1,0:T(8,128)(2,1)S(1)} %bitcast.256, bf16[4096,3328]{1,0:T(8,128)(2,1)} %param.14), kind=kOutput, calls=%fused_computation.33 | convolution fusion | flops 6980173824 | bytes 19529728 | tf_op jit(solution)/shard_map/dot_general | solution.py:143
  117.9 1.7 collective-permute-start.21
  120.0 11.1 %fusion.25 = bf16[512,1664]{1,0:T(8,128)(2,1)S(1)} fusion(bf16[512,4096]{1,0:T(8,128)(2,1)S(1)} %bitcast.248, bf16[4096,3328]{1,0:T(8,128)(2,1)} %param.13), kind=kOutput, calls=%fused_computation.28 | convolution fusion | flops 6980173824 | bytes 19529728 | tf_op jit(solution)/shard_map/dot_general | solution.py:143
  132.4 11.1 %fusion.31 = bf16[512,1664]{1,0:T(8,128)(2,1)S(1)} fusion(bf16[512,4096]{1,0:T(8,128)(2,1)S(1)} %bitcast.249, bf16[4096,3328]{1,0:T(8,128)(2,1)} %param.13), kind=kOutput, calls=%fused_computation.30 | convolution fusion | flops 6980173824 | bytes 19529728 | tf_op jit(solution)/shard_map/dot_general | solution.py:143
  145.5 11.1 %fusion.37 = bf16[512,1664]{1,0:T(8,128)(2,1)S(1)} fusion(bf16[512,4096]{1,0:T(8,128)(2,1)S(1)} %bitcast.250, bf16[4096,3328]{1,0:T(8,128)(2,1)} %param.14), kind=kOutput, calls=%fused_computation.32 | convolution fusion | flops 6980173824 | bytes 19529728 | tf_op jit(solution)/shard_map/dot_general | solution.py:143
  157.9 8.3 %fusion.43 = bf16[512,1152]{1,0:T(8,128)(2,1)S(1)} fusion(bf16[512,4096]{1,0:T(8,128)(2,1)S(1)} %bitcast.251, bf16[4096,3328]{1,0:T(8,128)(2,1)} %param.14), kind=kOutput, calls=%fused_computation.34 | convolution fusion | flops 4832428032 | bytes 14811136 | tf_op jit(solution)/shard_map/dot_general | solution.py:143
  166.2 2.8 %collective-permute-done.27 = bf16[1,128,1664]{2,1,0:T(8,128)(2,1)S(1)} collective-permute-done((bf16[1,128,1664]{2,1,0:T(8,128)(2,1)S(1)}, bf16[1,128,1664]{2,1,0:T(8,128)(2,1)S(1)}, u32[]{:S(2)}, u32[]{:S(2)}) %collective-permute-start.27) | collective-permute-done | bytes 426016 | tf_op jit(solution)/shard_map/ppermute | solution.py:93
  170.3 4.5 %fusion.46 = bf16[512,512]{1,0:T(8,128)(2,1)S(1)} fusion(bf16[512,4096]{1,0:T(8,128)(2,1)S(1)} %bitcast.252, bf16[4096,3328]{1,0:T(8,128)(2,1)} %param.14), kind=kOutput, calls=%fused_computation.46 | convolution fusion | flops 2147745792 | bytes 8912896 | tf_op jit(solution)/shard_map/dot_general | solution.py:143
  174.8 5.7 %collective-permute-done.29 = bf16[1,128,1664]{2,1,0:T(8,128)(2,1)S(1)} collective-permute-done((bf16[1,128,1664]{2,1,0:T(8,128)(2,1)S(1)}, bf16[1,128,1664]{2,1,0:T(8,128)(2,1)S(1)}, u32[]{:S(2)}, u32[]{:S(2)}) %collective-permute-start.29) | collective-permute-done | bytes 426016 | tf_op jit(solution)/shard_map/ppermute | solution.py:93
  182.5 7.9 %collective-permute-done.31 = bf16[1,128,1152]{2,1,0:T(8,128)(2,1)S(1)} collective-permute-done((bf16[1,128,1152]{2,1,0:T(8,128)(2,1)S(1)}, bf16[1,128,1152]{2,1,0:T(8,128)(2,1)S(1)}, u32[]{:S(2)}, u32[]{:S(2)}) %collective-permute-start.31) | collective-permute-done | bytes 294944 | tf_op jit(solution)/shard_map/ppermute | solution.py:93
  191.3 4.3 %collective-permute-done.33 = bf16[1,128,512]{2,1,0:T(8,128)(2,1)S(1)} collective-permute-done((bf16[1,128,512]{2,1,0:T(8,128)(2,1)S(1)}, bf16[1,128,512]{2,1,0:T(8,128)(2,1)S(1)}, u32[]{:S(2)}, u32[]{:S(2)}) %collective-permute-start.33) | collective-permute-done | bytes 131104 | tf_op jit(solution)/shard_map/ppermute | solution.py:93
  196.8 2.2 %fusion.18 = bf16[256,3328]{1,0:T(8,128)(2,1)} fusion(f32[2,2,64,3328]{3,2,0,1:T(8,128)S(1)} %pad_maximum_fusion.1, f32[2,2,64,3328]{3,2,0,1:T(8,128)S(1)} %pad_maximum_fusion), kind=kLoop, calls=%fused_computation.21 | loop fusion | flops 5111808 | bytes 8519680 | tf_op jit(solution)/shard_map/convert_element_type | solution.py:187
  (124 shorter events, 28.0 us)
Async XLA Ops:
  1.2 24.2 %collective-permute-start = (bf16[64,4096]{1,0:T(8,128)(2,1)S(1)}, bf16[64,4096]{1,0:T(8,128)(2,1)S(1)}, u32[]{:S(2)}, u32[]{:S(2)}) collective-permute-start(bf16[64,4096]{1,0:T(8,128)(2,1)S(1)} %slice.39), channel_id=1, source_target_pairs={{0,2},{2,4},{4,6},{6,7},{7,5},{5,3},{3,1},{1,0},{8,10},{10,12},{12... | collective-permute-start | bytes 1572872 | tf_op jit(solution)/shard_map/ppermute | solution.py:74
  4.3 23.2 %collective-permute-start.1 = (bf16[64,4096]{1,0:T(8,128)(2,1)S(1)}, bf16[64,4096]{1,0:T(8,128)(2,1)S(1)}, u32[]{:S(2)}, u32[]{:S(2)}) collective-permute-start(bf16[64,4096]{1,0:T(8,128)(2,1)S(1)} %slice.39), channel_id=1, source_target_pairs={{0,1},{2,0},{4,2},{6,4},{7,6},{5,7},{3,5},{1,3},{8,9},{10,8},{12,1... | collective-permute-start | bytes 1572872 | tf_op jit(solution)/shard_map/ppermute | solution.py:77
  25.4 13.4 %collective-permute-start.2 = (bf16[64,4096]{1,0:T(8,128)(2,1)S(1)}, bf16[64,4096]{1,0:T(8,128)(2,1)S(1)}, u32[]{:S(2)}, u32[]{:S(2)}) collective-permute-start(bf16[64,4096]{1,0:T(8,128)(2,1)S(1)} %collective-permute-done), channel_id=1, source_target_pairs={{0,2},{2,4},{4,6},{6,7},{7,5},{5,3},{3,1},{1,0},{8,10},{10,12},{12... | collective-permute-start | bytes 1572872 | tf_op jit(solution)/shard_map/ppermute | solution.py:74
  27.5 13.1 %collective-permute-start.3 = (bf16[64,4096]{1,0:T(8,128)(2,1)S(1)}, bf16[64,4096]{1,0:T(8,128)(2,1)S(1)}, u32[]{:S(2)}, u32[]{:S(2)}) collective-permute-start(bf16[64,4096]{1,0:T(8,128)(2,1)S(1)} %collective-permute-done.1), channel_id=1, source_target_pairs={{0,1},{2,0},{4,2},{6,4},{7,6},{5,7},{3,5},{1,3},{8,9},{10,8},{12,1... | collective-permute-start | bytes 1572872 | tf_op jit(solution)/shard_map/ppermute | solution.py:77
  38.8 12.5 %collective-permute-start.4 = (bf16[64,4096]{1,0:T(8,128)(2,1)S(1)}, bf16[64,4096]{1,0:T(8,128)(2,1)S(1)}, u32[]{:S(2)}, u32[]{:S(2)}) collective-permute-start(bf16[64,4096]{1,0:T(8,128)(2,1)S(1)} %collective-permute-done.2), channel_id=1, source_target_pairs={{0,2},{2,4},{4,6},{6,7},{7,5},{5,3},{3,1},{1,0},{8,10},{10,12},{12... | collective-permute-start | bytes 1572872 | tf_op jit(solution)/shard_map/ppermute | solution.py:74
  40.6 12.3 %collective-permute-start.5 = (bf16[64,4096]{1,0:T(8,128)(2,1)S(1)}, bf16[64,4096]{1,0:T(8,128)(2,1)S(1)}, u32[]{:S(2)}, u32[]{:S(2)}) collective-permute-start(bf16[64,4096]{1,0:T(8,128)(2,1)S(1)} %collective-permute-done.3), channel_id=1, source_target_pairs={{0,1},{2,0},{4,2},{6,4},{7,6},{5,7},{3,5},{1,3},{8,9},{10,8},{12,1... | collective-permute-start | bytes 1572872 | tf_op jit(solution)/shard_map/ppermute | solution.py:77
  59.4 13.7 %collective-permute-start.9 = (bf16[64,4096]{1,0:T(8,128)(2,1)S(1)}, bf16[64,4096]{1,0:T(8,128)(2,1)S(1)}, u32[]{:S(2)}, u32[]{:S(2)}) collective-permute-start(bf16[64,4096]{1,0:T(8,128)(2,1)S(1)} %slice.43), channel_id=1, source_target_pairs={{0,2},{2,4},{4,6},{6,7},{7,5},{5,3},{3,1},{1,0},{8,10},{10,12},{12... | collective-permute-start | bytes 1572872 | tf_op jit(solution)/shard_map/ppermute | solution.py:74
  61.1 12.1 %collective-permute-start.8 = (bf16[64,4096]{1,0:T(8,128)(2,1)S(1)}, bf16[64,4096]{1,0:T(8,128)(2,1)S(1)}, u32[]{:S(2)}, u32[]{:S(2)}) collective-permute-start(bf16[64,4096]{1,0:T(8,128)(2,1)S(1)} %slice.43), channel_id=1, source_target_pairs={{0,1},{2,0},{4,2},{6,4},{7,6},{5,7},{3,5},{1,3},{8,9},{10,8},{12,1... | collective-permute-start | bytes 1572872 | tf_op jit(solution)/shard_map/ppermute | solution.py:77
  73.3 13.4 %collective-permute-start.11 = (bf16[64,4096]{1,0:T(8,128)(2,1)S(1)}, bf16[64,4096]{1,0:T(8,128)(2,1)S(1)}, u32[]{:S(2)}, u32[]{:S(2)}) collective-permute-start(bf16[64,4096]{1,0:T(8,128)(2,1)S(1)} %collective-permute-done.8), channel_id=1, source_target_pairs={{0,1},{2,0},{4,2},{6,4},{7,6},{5,7},{3,5},{1,3},{8,9},{10,8},{12,1... | collective-permute-start | bytes 1572872 | tf_op jit(solution)/shard_map/ppermute | solution.py:77
  73.9 12.7 %collective-permute-start.12 = (bf16[64,4096]{1,0:T(8,128)(2,1)S(1)}, bf16[64,4096]{1,0:T(8,128)(2,1)S(1)}, u32[]{:S(2)}, u32[]{:S(2)}) collective-permute-start(bf16[64,4096]{1,0:T(8,128)(2,1)S(1)} %collective-permute-done.9), channel_id=1, source_target_pairs={{0,2},{2,4},{4,6},{6,7},{7,5},{5,3},{3,1},{1,0},{8,10},{10,12},{12... | collective-permute-start | bytes 1572872 | tf_op jit(solution)/shard_map/ppermute | solution.py:74
  86.9 14.8 %collective-permute-start.13 = (bf16[1,128,1664]{2,1,0:T(8,128)(2,1)S(1)}, bf16[1,128,1664]{2,1,0:T(8,128)(2,1)S(1)}, u32[]{:S(2)}, u32[]{:S(2)}) collective-permute-start(bf16[1,128,1664]{2,1,0:T(8,128)(2,1)S(1)} %fusion.57), channel_id=1, source_target_pairs={{0,16},{8,24},{16,0},{24,8},{1,17},{9,25},{17,1},{25,9},{2,18},{10... | collective-permute-start | bytes 1277960 | tf_op jit(solution)/shard_map/ppermute | solution.py:93
  88.5 14.8 %collective-permute-start.15 = (bf16[64,4096]{1,0:T(8,128)(2,1)S(1)}, bf16[64,4096]{1,0:T(8,128)(2,1)S(1)}, u32[]{:S(2)}, u32[]{:S(2)}) collective-permute-start(bf16[64,4096]{1,0:T(8,128)(2,1)S(1)} %collective-permute-done.11), channel_id=1, source_target_pairs={{0,1},{2,0},{4,2},{6,4},{7,6},{5,7},{3,5},{1,3},{8,9},{10,8},{12,1... | collective-permute-start | bytes 1572872 | tf_op jit(solution)/shard_map/ppermute | solution.py:77
  89.3 14.0 %collective-permute-start.16 = (bf16[64,4096]{1,0:T(8,128)(2,1)S(1)}, bf16[64,4096]{1,0:T(8,128)(2,1)S(1)}, u32[]{:S(2)}, u32[]{:S(2)}) collective-permute-start(bf16[64,4096]{1,0:T(8,128)(2,1)S(1)} %collective-permute-done.12), channel_id=1, source_target_pairs={{0,2},{2,4},{4,6},{6,7},{7,5},{5,3},{3,1},{1,0},{8,10},{10,12},{12... | collective-permute-start | bytes 1572872 | tf_op jit(solution)/shard_map/ppermute | solution.py:74
  90.6 12.7 %collective-permute-start.14 = (bf16[2,128,1664]{2,1,0:T(8,128)(2,1)S(1)}, bf16[2,128,1664]{2,1,0:T(8,128)(2,1)S(1)}, u32[]{:S(2)}, u32[]{:S(2)}) collective-permute-start(bf16[2,128,1664]{2,1,0:T(8,128)(2,1)S(1)} %dynamic-slice_bitcast_fusion.5), channel_id=1, source_target_pairs={{0,8},{8,0},{16,24},{24,16},{1,9},{9,1},{17,25},{25,17},{2,10},{10... | collective-permute-start | bytes 2555912 | tf_op jit(solution)/shard_map/ppermute | solution.py:93
  103.6 13.8 %collective-permute-start.20 = (bf16[64,2048]{1,0:T(8,128)(2,1)S(1)}, bf16[64,2048]{1,0:T(8,128)(2,1)S(1)}, u32[]{:S(2)}, u32[]{:S(2)}) collective-permute-start(bf16[64,2048]{1,0:T(8,128)(2,1)S(1)} %slice.48), channel_id=1, source_target_pairs={{0,2},{2,4},{4,6},{6,7},{7,5},{5,3},{3,1},{1,0},{8,10},{10,12},{12... | collective-permute-start | bytes 786440 | tf_op jit(solution)/shard_map/ppermute | solution.py:68
  104.7 12.8 %collective-permute-start.19 = (bf16[64,2048]{1,0:T(8,128)(2,1)S(1)}, bf16[64,2048]{1,0:T(8,128)(2,1)S(1)}, u32[]{:S(2)}, u32[]{:S(2)}) collective-permute-start(bf16[64,2048]{1,0:T(8,128)(2,1)S(1)} %slice.47), channel_id=1, source_target_pairs={{0,1},{2,0},{4,2},{6,4},{7,6},{5,7},{3,5},{1,3},{8,9},{10,8},{12,1... | collective-permute-start | bytes 786440 | tf_op jit(solution)/shard_map/ppermute | solution.py:69
  105.7 11.8 %collective-permute-start.17 = (bf16[1,128,1664]{2,1,0:T(8,128)(2,1)S(1)}, bf16[1,128,1664]{2,1,0:T(8,128)(2,1)S(1)}, u32[]{:S(2)}, u32[]{:S(2)}) collective-permute-start(bf16[1,128,1664]{2,1,0:T(8,128)(2,1)S(1)} %fusion.58), channel_id=1, source_target_pairs={{0,16},{8,24},{16,0},{24,8},{1,17},{9,25},{17,1},{25,9},{2,18},{10... | collective-permute-start | bytes 1277960 | tf_op jit(solution)/shard_map/ppermute | solution.py:93
  106.2 11.4 %collective-permute-start.18 = (bf16[2,128,1664]{2,1,0:T(8,128)(2,1)S(1)}, bf16[2,128,1664]{2,1,0:T(8,128)(2,1)S(1)}, u32[]{:S(2)}, u32[]{:S(2)}) collective-permute-start(bf16[2,128,1664]{2,1,0:T(8,128)(2,1)S(1)} %dynamic-slice_bitcast_fusion.4), channel_id=1, source_target_pairs={{0,8},{8,0},{16,24},{24,16},{1,9},{9,1},{17,25},{25,17},{2,10},{10... | collective-permute-start | bytes 2555912 | tf_op jit(solution)/shard_map/ppermute | solution.py:93
  117.9 13.2 %collective-permute-start.21 = (bf16[1,128,1664]{2,1,0:T(8,128)(2,1)S(1)}, bf16[1,128,1664]{2,1,0:T(8,128)(2,1)S(1)}, u32[]{:S(2)}, u32[]{:S(2)}) collective-permute-start(bf16[1,128,1664]{2,1,0:T(8,128)(2,1)S(1)} %fusion.59), channel_id=1, source_target_pairs={{0,16},{8,24},{16,0},{24,8},{1,17},{9,25},{17,1},{25,9},{2,18},{10... | collective-permute-start | bytes 1277960 | tf_op jit(solution)/shard_map/ppermute | solution.py:93
  119.7 11.4 %collective-permute-start.22 = (bf16[2,128,1664]{2,1,0:T(8,128)(2,1)S(1)}, bf16[2,128,1664]{2,1,0:T(8,128)(2,1)S(1)}, u32[]{:S(2)}, u32[]{:S(2)}) collective-permute-start(bf16[2,128,1664]{2,1,0:T(8,128)(2,1)S(1)} %dynamic-slice_bitcast_fusion.3), channel_id=1, source_target_pairs={{0,8},{8,0},{16,24},{24,16},{1,9},{9,1},{17,25},{25,17},{2,10},{10... | collective-permute-start | bytes 2555912 | tf_op jit(solution)/shard_map/ppermute | solution.py:93
  131.4 12.1 %collective-permute-start.23 = (bf16[1,128,1664]{2,1,0:T(8,128)(2,1)S(1)}, bf16[1,128,1664]{2,1,0:T(8,128)(2,1)S(1)}, u32[]{:S(2)}, u32[]{:S(2)}) collective-permute-start(bf16[1,128,1664]{2,1,0:T(8,128)(2,1)S(1)} %fusion.60), channel_id=1, source_target_pairs={{0,16},{8,24},{16,0},{24,8},{1,17},{9,25},{17,1},{25,9},{2,18},{10... | collective-permute-start | bytes 1277960 | tf_op jit(solution)/shard_map/ppermute | solution.py:93
  143.8 12.8 %collective-permute-start.25 = (bf16[1,128,1664]{2,1,0:T(8,128)(2,1)S(1)}, bf16[1,128,1664]{2,1,0:T(8,128)(2,1)S(1)}, u32[]{:S(2)}, u32[]{:S(2)}) collective-permute-start(bf16[1,128,1664]{2,1,0:T(8,128)(2,1)S(1)} %fusion.61), channel_id=1, source_target_pairs={{0,16},{8,24},{16,0},{24,8},{1,17},{9,25},{17,1},{25,9},{2,18},{10... | collective-permute-start | bytes 1277960 | tf_op jit(solution)/shard_map/ppermute | solution.py:93
  145.2 11.5 %collective-permute-start.26 = (bf16[2,128,1664]{2,1,0:T(8,128)(2,1)S(1)}, bf16[2,128,1664]{2,1,0:T(8,128)(2,1)S(1)}, u32[]{:S(2)}, u32[]{:S(2)}) collective-permute-start(bf16[2,128,1664]{2,1,0:T(8,128)(2,1)S(1)} %dynamic-slice_bitcast_fusion.1), channel_id=1, source_target_pairs={{0,8},{8,0},{16,24},{24,16},{1,9},{9,1},{17,25},{25,17},{2,10},{10... | collective-permute-start | bytes 2555912 | tf_op jit(solution)/shard_map/ppermute | solution.py:93
  156.9 12.1 %collective-permute-start.27 = (bf16[1,128,1664]{2,1,0:T(8,128)(2,1)S(1)}, bf16[1,128,1664]{2,1,0:T(8,128)(2,1)S(1)}, u32[]{:S(2)}, u32[]{:S(2)}) collective-permute-start(bf16[1,128,1664]{2,1,0:T(8,128)(2,1)S(1)} %fusion.62), channel_id=1, source_target_pairs={{0,16},{8,24},{16,0},{24,8},{1,17},{9,25},{17,1},{25,9},{2,18},{10... | collective-permute-start | bytes 1277960 | tf_op jit(solution)/shard_map/ppermute | solution.py:93
  (11 other events, 109.7 us)

commit v6 on v5

--- a/solution.py
+++ b/solution.py
@@ -159,7 +159,8 @@
             carry["jobs"] = [jb[2] for jb in jobs]
             carry["nxt"] = nxt["st"] if nxt is not None else None
             carry["done"] = done
-            carry = lax.optimization_barrier(carry)
+            if t + 1 < len(tiles):
+                carry = lax.optimization_barrier(carry)
             piece = carry["piece"]
             for jb, a in zip(jobs, carry["jobs"]):
                 jb[2] = a

time: 199 us -> 195 us (0.980)
  waiting for transfers between devices: 50.1 us -> 44.1 us
    ppermute x18, waiting for transfers between devices: 21.4 us -> 15.4 us  [reduce_level(): lax.ppermute(send.astype(jnp.bfloat16), 'row', [(i, i ^ d) for i in range...]
  transfers between devices with their start and end apart: 34 -> 34, of which waited for: 10 -> 9; matrix products, arithmetic and copies ran while one was open for 48% -> 50% of each run, Pallas kernels for 0% -> 0%
where the time goes in v6:
time: 195 us; the launch traced here: 194 us
  matrix products  90.4 us (46%)
  waiting for transfers between devices  44.1 us (23%)
  starting transfers between devices  28.9 us (15%)
  between operations  18.7 us (10%)
  local copies, waits for them, and re-layouts  6.73 us (3%)
  other arithmetic  5.39 us (3%)
    dot_general x9, matrix products, on_device(): jnp.dot(piece, weight[:, start:start + width], preferred_element_type=jnp...  90.4 us
    ppermute x6, waiting for transfers between devices, step(): f = lax.ppermute(st['f'], 'col', self.fwd_pairs)  23.1 us
    ppermute x18, waiting for transfers between devices, reduce_level(): lax.ppermute(send.astype(jnp.bfloat16), 'row', [(i, i ^ d) for i in range...  15.4 us
    ppermute x6, starting transfers between devices, step(): f = lax.ppermute(st['f'], 'col', self.fwd_pairs)  11.3 us
    ppermute x18, starting transfers between devices, reduce_level(): lax.ppermute(send.astype(jnp.bfloat16), 'row', [(i, i ^ d) for i in range...  11.3 us
    ppermute x2, waiting for transfers between devices, step(): f = lax.ppermute(st['f'][:, :k2], 'col', self.fwd_pairs)  4.18 us
  transfers between devices with their start and end apart: 34, of which 9 were waited for; matrix products, arithmetic and copies ran while one was open for 50% of the time, Pallas kernels for 0%

profile of v6, /device:TPU:0, one launch (start us, length us, event | category | flops | bytes accessed | tf_op | source)
XLA Modules:
  0.0 194.2 jit_solution(9932507031618778063)
XLA Ops:
  1.2 3.1 %collective-permute-start = (bf16[64,4096]{1,0:T(8,128)(2,1)S(1)}, bf16[64,4096]{1,0:T(8,128)(2,1)S(1)}, u32[]{:S(2)}, u32[]{:S(2)}) collective-permute-start(bf16[64,4096]{1,0:T(8,128)(2,1)S(1)} %slice.39), channel_id=1, source_target_pairs={{0,2},{2,4},{4,6},{6,7},{7,5},{5,3},{3,1},{1,0},{8,10},{10,12},{12... | collective-permute-start | bytes 1572872 | tf_op jit(solution)/shard_map/ppermute | solution.py:74
  10.2 1.6 fusion.62
  25.7 2.1 %collective-permute-start.2 = (bf16[64,4096]{1,0:T(8,128)(2,1)S(1)}, bf16[64,4096]{1,0:T(8,128)(2,1)S(1)}, u32[]{:S(2)}, u32[]{:S(2)}) collective-permute-start(bf16[64,4096]{1,0:T(8,128)(2,1)S(1)} %collective-permute-done), channel_id=1, source_target_pairs={{0,2},{2,4},{4,6},{6,7},{7,5},{5,3},{3,1},{1,0},{8,10},{10,12},{12... | collective-permute-start | bytes 1572872 | tf_op jit(solution)/shard_map/ppermute | solution.py:74
  27.9 11.3 %collective-permute-done.2 = bf16[64,4096]{1,0:T(8,128)(2,1)S(1)} collective-permute-done((bf16[64,4096]{1,0:T(8,128)(2,1)S(1)}, bf16[64,4096]{1,0:T(8,128)(2,1)S(1)}, u32[]{:S(2)}, u32[]{:S(2)}) %collective-permute-start.2) | collective-permute-done | bytes 524320 | tf_op jit(solution)/shard_map/ppermute | solution.py:74
  39.1 1.7 collective-permute-start.4
  41.3 10.4 %collective-permute-done.4 = bf16[64,4096]{1,0:T(8,128)(2,1)S(1)} collective-permute-done((bf16[64,4096]{1,0:T(8,128)(2,1)S(1)}, bf16[64,4096]{1,0:T(8,128)(2,1)S(1)}, u32[]{:S(2)}, u32[]{:S(2)}) %collective-permute-start.4) | collective-permute-done | bytes 524320 | tf_op jit(solution)/shard_map/ppermute | solution.py:74
  53.9 4.2 %collective-permute-done.6 = bf16[64,2048]{1,0:T(8,128)(2,1)S(1)} collective-permute-done((bf16[64,2048]{1,0:T(8,128)(2,1)S(1)}, bf16[64,2048]{1,0:T(8,128)(2,1)S(1)}, u32[]{:S(2)}, u32[]{:S(2)}) %collective-permute-start.6) | collective-permute-done | bytes 262176 | tf_op jit(solution)/shard_map/ppermute | solution.py:68
  58.1 1.5 collective-permute-done.7
  59.7 1.6 collective-permute-start.9
  61.8 11.1 %fusion.22 = bf16[512,1664]{1,0:T(8,128)(2,1)S(1)} fusion(bf16[512,4096]{1,0:T(8,128)(2,1)S(1)} %bitcast.234, bf16[4096,3328]{1,0:T(8,128)(2,1)} %param.13), kind=kOutput, calls=%fused_computation.27 | convolution fusion | flops 6980173824 | bytes 19529728 | tf_op jit(solution)/shard_map/dot_general | solution.py:143
  75.8 11.1 %fusion.28 = bf16[512,1664]{1,0:T(8,128)(2,1)S(1)} fusion(bf16[512,4096]{1,0:T(8,128)(2,1)S(1)} %bitcast.235, bf16[4096,3328]{1,0:T(8,128)(2,1)} %param.13), kind=kOutput, calls=%fused_computation.29 | convolution fusion | flops 6980173824 | bytes 19529728 | tf_op jit(solution)/shard_map/dot_general | solution.py:143
  87.2 1.6 collective-permute-start.13
  91.0 11.1 %fusion.34 = bf16[512,1664]{1,0:T(8,128)(2,1)S(1)} fusion(bf16[512,4096]{1,0:T(8,128)(2,1)S(1)} %bitcast.236, bf16[4096,3328]{1,0:T(8,128)(2,1)} %param.14), kind=kOutput, calls=%fused_computation.31 | convolution fusion | flops 6980173824 | bytes 19529728 | tf_op jit(solution)/shard_map/dot_general | solution.py:143
  106.6 11.1 %fusion.40 = bf16[512,1664]{1,0:T(8,128)(2,1)S(1)} fusion(bf16[512,4096]{1,0:T(8,128)(2,1)S(1)} %bitcast.237, bf16[4096,3328]{1,0:T(8,128)(2,1)} %param.14), kind=kOutput, calls=%fused_computation.33 | convolution fusion | flops 6980173824 | bytes 19529728 | tf_op jit(solution)/shard_map/dot_general | solution.py:143
  118.2 1.7 collective-permute-start.21
  120.3 11.1 %fusion.25 = bf16[512,1664]{1,0:T(8,128)(2,1)S(1)} fusion(bf16[512,4096]{1,0:T(8,128)(2,1)S(1)} %bitcast.229, bf16[4096,3328]{1,0:T(8,128)(2,1)} %param.13), kind=kOutput, calls=%fused_computation.28 | convolution fusion | flops 6980173824 | bytes 19529728 | tf_op jit(solution)/shard_map/dot_general | solution.py:143
  132.7 11.1 %fusion.31 = bf16[512,1664]{1,0:T(8,128)(2,1)S(1)} fusion(bf16[512,4096]{1,0:T(8,128)(2,1)S(1)} %bitcast.230, bf16[4096,3328]{1,0:T(8,128)(2,1)} %param.13), kind=kOutput, calls=%fused_computation.30 | convolution fusion | flops 6980173824 | bytes 19529728 | tf_op jit(solution)/shard_map/dot_general | solution.py:143
  145.8 11.1 %fusion.37 = bf16[512,1664]{1,0:T(8,128)(2,1)S(1)} fusion(bf16[512,4096]{1,0:T(8,128)(2,1)S(1)} %bitcast.231, bf16[4096,3328]{1,0:T(8,128)(2,1)} %param.14), kind=kOutput, calls=%fused_computation.32 | convolution fusion | flops 6980173824 | bytes 19529728 | tf_op jit(solution)/shard_map/dot_general | solution.py:143
  158.2 8.3 %fusion.43 = bf16[512,1152]{1,0:T(8,128)(2,1)S(1)} fusion(bf16[512,4096]{1,0:T(8,128)(2,1)S(1)} %bitcast.232, bf16[4096,3328]{1,0:T(8,128)(2,1)} %param.14), kind=kOutput, calls=%fused_computation.34 | convolution fusion | flops 4832428032 | bytes 14811136 | tf_op jit(solution)/shard_map/dot_general | solution.py:143
  166.5 2.8 %collective-permute-done.27 = bf16[1,128,1664]{2,1,0:T(8,128)(2,1)S(1)} collective-permute-done((bf16[1,128,1664]{2,1,0:T(8,128)(2,1)S(1)}, bf16[1,128,1664]{2,1,0:T(8,128)(2,1)S(1)}, u32[]{:S(2)}, u32[]{:S(2)}) %collective-permute-start.27) | collective-permute-done | bytes 426016 | tf_op jit(solution)/shard_map/ppermute | solution.py:93
  170.5 4.5 %fusion.46 = bf16[512,512]{1,0:T(8,128)(2,1)S(1)} fusion(bf16[512,4096]{1,0:T(8,128)(2,1)S(1)} %bitcast.233, bf16[4096,3328]{1,0:T(8,128)(2,1)} %param.14), kind=kOutput, calls=%fused_computation.45 | convolution fusion | flops 2147745792 | bytes 8912896 | tf_op jit(solution)/shard_map/dot_general | solution.py:143
  178.2 5.5 %collective-permute-done.33 = bf16[1,128,512]{2,1,0:T(8,128)(2,1)S(1)} collective-permute-done((bf16[1,128,512]{2,1,0:T(8,128)(2,1)S(1)}, bf16[1,128,512]{2,1,0:T(8,128)(2,1)S(1)}, u32[]{:S(2)}, u32[]{:S(2)}) %collective-permute-start.33) | collective-permute-done | bytes 131104 | tf_op jit(solution)/shard_map/ppermute | solution.py:93
  184.8 6.9 %collective-permute-done.31 = bf16[1,128,1152]{2,1,0:T(8,128)(2,1)S(1)} collective-permute-done((bf16[1,128,1152]{2,1,0:T(8,128)(2,1)S(1)}, bf16[1,128,1152]{2,1,0:T(8,128)(2,1)S(1)}, u32[]{:S(2)}, u32[]{:S(2)}) %collective-permute-start.31) | collective-permute-done | bytes 294944 | tf_op jit(solution)/shard_map/ppermute | solution.py:93
  192.0 2.2 %fusion.18 = bf16[256,3328]{1,0:T(8,128)(2,1)} fusion(f32[2,2,64,3328]{3,2,0,1:T(8,128)S(1)} %maximum_maximum_fusion, f32[2,2,64,3328]{3,2,0,1:T(8,128)S(1)} %pad_maximum_fusion), kind=kLoop, calls=%fused_computation.21 | loop fusion | flops 5111808 | bytes 8519680 | tf_op jit(solution)/shard_map/convert_element_type | solution.py:188
  (124 shorter events, 27.0 us)
Async XLA Ops:
  1.2 24.5 %collective-permute-start = (bf16[64,4096]{1,0:T(8,128)(2,1)S(1)}, bf16[64,4096]{1,0:T(8,128)(2,1)S(1)}, u32[]{:S(2)}, u32[]{:S(2)}) collective-permute-start(bf16[64,4096]{1,0:T(8,128)(2,1)S(1)} %slice.39), channel_id=1, source_target_pairs={{0,2},{2,4},{4,6},{6,7},{7,5},{5,3},{3,1},{1,0},{8,10},{10,12},{12... | collective-permute-start | bytes 1572872 | tf_op jit(solution)/shard_map/ppermute | solution.py:74
  4.3 23.5 %collective-permute-start.1 = (bf16[64,4096]{1,0:T(8,128)(2,1)S(1)}, bf16[64,4096]{1,0:T(8,128)(2,1)S(1)}, u32[]{:S(2)}, u32[]{:S(2)}) collective-permute-start(bf16[64,4096]{1,0:T(8,128)(2,1)S(1)} %slice.39), channel_id=1, source_target_pairs={{0,1},{2,0},{4,2},{6,4},{7,6},{5,7},{3,5},{1,3},{8,9},{10,8},{12,1... | collective-permute-start | bytes 1572872 | tf_op jit(solution)/shard_map/ppermute | solution.py:77
  25.7 13.4 %collective-permute-start.2 = (bf16[64,4096]{1,0:T(8,128)(2,1)S(1)}, bf16[64,4096]{1,0:T(8,128)(2,1)S(1)}, u32[]{:S(2)}, u32[]{:S(2)}) collective-permute-start(bf16[64,4096]{1,0:T(8,128)(2,1)S(1)} %collective-permute-done), channel_id=1, source_target_pairs={{0,2},{2,4},{4,6},{6,7},{7,5},{5,3},{3,1},{1,0},{8,10},{10,12},{12... | collective-permute-start | bytes 1572872 | tf_op jit(solution)/shard_map/ppermute | solution.py:74
  27.8 13.1 %collective-permute-start.3 = (bf16[64,4096]{1,0:T(8,128)(2,1)S(1)}, bf16[64,4096]{1,0:T(8,128)(2,1)S(1)}, u32[]{:S(2)}, u32[]{:S(2)}) collective-permute-start(bf16[64,4096]{1,0:T(8,128)(2,1)S(1)} %collective-permute-done.1), channel_id=1, source_target_pairs={{0,1},{2,0},{4,2},{6,4},{7,6},{5,7},{3,5},{1,3},{8,9},{10,8},{12,1... | collective-permute-start | bytes 1572872 | tf_op jit(solution)/shard_map/ppermute | solution.py:77
  39.1 12.5 %collective-permute-start.4 = (bf16[64,4096]{1,0:T(8,128)(2,1)S(1)}, bf16[64,4096]{1,0:T(8,128)(2,1)S(1)}, u32[]{:S(2)}, u32[]{:S(2)}) collective-permute-start(bf16[64,4096]{1,0:T(8,128)(2,1)S(1)} %collective-permute-done.2), channel_id=1, source_target_pairs={{0,2},{2,4},{4,6},{6,7},{7,5},{5,3},{3,1},{1,0},{8,10},{10,12},{12... | collective-permute-start | bytes 1572872 | tf_op jit(solution)/shard_map/ppermute | solution.py:74
  40.9 12.3 %collective-permute-start.5 = (bf16[64,4096]{1,0:T(8,128)(2,1)S(1)}, bf16[64,4096]{1,0:T(8,128)(2,1)S(1)}, u32[]{:S(2)}, u32[]{:S(2)}) collective-permute-start(bf16[64,4096]{1,0:T(8,128)(2,1)S(1)} %collective-permute-done.3), channel_id=1, source_target_pairs={{0,1},{2,0},{4,2},{6,4},{7,6},{5,7},{3,5},{1,3},{8,9},{10,8},{12,1... | collective-permute-start | bytes 1572872 | tf_op jit(solution)/shard_map/ppermute | solution.py:77
  59.7 13.7 %collective-permute-start.9 = (bf16[64,4096]{1,0:T(8,128)(2,1)S(1)}, bf16[64,4096]{1,0:T(8,128)(2,1)S(1)}, u32[]{:S(2)}, u32[]{:S(2)}) collective-permute-start(bf16[64,4096]{1,0:T(8,128)(2,1)S(1)} %slice.43), channel_id=1, source_target_pairs={{0,2},{2,4},{4,6},{6,7},{7,5},{5,3},{3,1},{1,0},{8,10},{10,12},{12... | collective-permute-start | bytes 1572872 | tf_op jit(solution)/shard_map/ppermute | solution.py:74
  61.4 12.1 %collective-permute-start.8 = (bf16[64,4096]{1,0:T(8,128)(2,1)S(1)}, bf16[64,4096]{1,0:T(8,128)(2,1)S(1)}, u32[]{:S(2)}, u32[]{:S(2)}) collective-permute-start(bf16[64,4096]{1,0:T(8,128)(2,1)S(1)} %slice.43), channel_id=1, source_target_pairs={{0,1},{2,0},{4,2},{6,4},{7,6},{5,7},{3,5},{1,3},{8,9},{10,8},{12,1... | collective-permute-start | bytes 1572872 | tf_op jit(solution)/shard_map/ppermute | solution.py:77
  73.5 13.4 %collective-permute-start.11 = (bf16[64,4096]{1,0:T(8,128)(2,1)S(1)}, bf16[64,4096]{1,0:T(8,128)(2,1)S(1)}, u32[]{:S(2)}, u32[]{:S(2)}) collective-permute-start(bf16[64,4096]{1,0:T(8,128)(2,1)S(1)} %collective-permute-done.8), channel_id=1, source_target_pairs={{0,1},{2,0},{4,2},{6,4},{7,6},{5,7},{3,5},{1,3},{8,9},{10,8},{12,1... | collective-permute-start | bytes 1572872 | tf_op jit(solution)/shard_map/ppermute | solution.py:77
  74.2 12.7 %collective-permute-start.12 = (bf16[64,4096]{1,0:T(8,128)(2,1)S(1)}, bf16[64,4096]{1,0:T(8,128)(2,1)S(1)}, u32[]{:S(2)}, u32[]{:S(2)}) collective-permute-start(bf16[64,4096]{1,0:T(8,128)(2,1)S(1)} %collective-permute-done.9), channel_id=1, source_target_pairs={{0,2},{2,4},{4,6},{6,7},{7,5},{5,3},{3,1},{1,0},{8,10},{10,12},{12... | collective-permute-start | bytes 1572872 | tf_op jit(solution)/shard_map/ppermute | solution.py:74
  87.2 14.8 %collective-permute-start.13 = (bf16[1,128,1664]{2,1,0:T(8,128)(2,1)S(1)}, bf16[1,128,1664]{2,1,0:T(8,128)(2,1)S(1)}, u32[]{:S(2)}, u32[]{:S(2)}) collective-permute-start(bf16[1,128,1664]{2,1,0:T(8,128)(2,1)S(1)} %fusion.55), channel_id=1, source_target_pairs={{0,16},{8,24},{16,0},{24,8},{1,17},{9,25},{17,1},{25,9},{2,18},{10... | collective-permute-start | bytes 1277960 | tf_op jit(solution)/shard_map/ppermute | solution.py:93
  88.8 14.8 %collective-permute-start.15 = (bf16[64,4096]{1,0:T(8,128)(2,1)S(1)}, bf16[64,4096]{1,0:T(8,128)(2,1)S(1)}, u32[]{:S(2)}, u32[]{:S(2)}) collective-permute-start(bf16[64,4096]{1,0:T(8,128)(2,1)S(1)} %collective-permute-done.11), channel_id=1, source_target_pairs={{0,1},{2,0},{4,2},{6,4},{7,6},{5,7},{3,5},{1,3},{8,9},{10,8},{12,1... | collective-permute-start | bytes 1572872 | tf_op jit(solution)/shard_map/ppermute | solution.py:77
  89.6 14.0 %collective-permute-start.16 = (bf16[64,4096]{1,0:T(8,128)(2,1)S(1)}, bf16[64,4096]{1,0:T(8,128)(2,1)S(1)}, u32[]{:S(2)}, u32[]{:S(2)}) collective-permute-start(bf16[64,4096]{1,0:T(8,128)(2,1)S(1)} %collective-permute-done.12), channel_id=1, source_target_pairs={{0,2},{2,4},{4,6},{6,7},{7,5},{5,3},{3,1},{1,0},{8,10},{10,12},{12... | collective-permute-start | bytes 1572872 | tf_op jit(solution)/shard_map/ppermute | solution.py:74
  90.9 12.7 %collective-permute-start.14 = (bf16[2,128,1664]{2,1,0:T(8,128)(2,1)S(1)}, bf16[2,128,1664]{2,1,0:T(8,128)(2,1)S(1)}, u32[]{:S(2)}, u32[]{:S(2)}) collective-permute-start(bf16[2,128,1664]{2,1,0:T(8,128)(2,1)S(1)} %dynamic-slice_bitcast_fusion.5), channel_id=1, source_target_pairs={{0,8},{8,0},{16,24},{24,16},{1,9},{9,1},{17,25},{25,17},{2,10},{10... | collective-permute-start | bytes 2555912 | tf_op jit(solution)/shard_map/ppermute | solution.py:93
  103.9 13.8 %collective-permute-start.20 = (bf16[64,2048]{1,0:T(8,128)(2,1)S(1)}, bf16[64,2048]{1,0:T(8,128)(2,1)S(1)}, u32[]{:S(2)}, u32[]{:S(2)}) collective-permute-start(bf16[64,2048]{1,0:T(8,128)(2,1)S(1)} %slice.48), channel_id=1, source_target_pairs={{0,2},{2,4},{4,6},{6,7},{7,5},{5,3},{3,1},{1,0},{8,10},{10,12},{12... | collective-permute-start | bytes 786440 | tf_op jit(solution)/shard_map/ppermute | solution.py:68
  105.0 12.8 %collective-permute-start.19 = (bf16[64,2048]{1,0:T(8,128)(2,1)S(1)}, bf16[64,2048]{1,0:T(8,128)(2,1)S(1)}, u32[]{:S(2)}, u32[]{:S(2)}) collective-permute-start(bf16[64,2048]{1,0:T(8,128)(2,1)S(1)} %slice.47), channel_id=1, source_target_pairs={{0,1},{2,0},{4,2},{6,4},{7,6},{5,7},{3,5},{1,3},{8,9},{10,8},{12,1... | collective-permute-start | bytes 786440 | tf_op jit(solution)/shard_map/ppermute | solution.py:69
  106.0 11.8 %collective-permute-start.17 = (bf16[1,128,1664]{2,1,0:T(8,128)(2,1)S(1)}, bf16[1,128,1664]{2,1,0:T(8,128)(2,1)S(1)}, u32[]{:S(2)}, u32[]{:S(2)}) collective-permute-start(bf16[1,128,1664]{2,1,0:T(8,128)(2,1)S(1)} %fusion.56), channel_id=1, source_target_pairs={{0,16},{8,24},{16,0},{24,8},{1,17},{9,25},{17,1},{25,9},{2,18},{10... | collective-permute-start | bytes 1277960 | tf_op jit(solution)/shard_map/ppermute | solution.py:93
  118.2 13.2 %collective-permute-start.21 = (bf16[1,128,1664]{2,1,0:T(8,128)(2,1)S(1)}, bf16[1,128,1664]{2,1,0:T(8,128)(2,1)S(1)}, u32[]{:S(2)}, u32[]{:S(2)}) collective-permute-start(bf16[1,128,1664]{2,1,0:T(8,128)(2,1)S(1)} %fusion.57), channel_id=1, source_target_pairs={{0,16},{8,24},{16,0},{24,8},{1,17},{9,25},{17,1},{25,9},{2,18},{10... | collective-permute-start | bytes 1277960 | tf_op jit(solution)/shard_map/ppermute | solution.py:93
  120.0 11.5 %collective-permute-start.22 = (bf16[2,128,1664]{2,1,0:T(8,128)(2,1)S(1)}, bf16[2,128,1664]{2,1,0:T(8,128)(2,1)S(1)}, u32[]{:S(2)}, u32[]{:S(2)}) collective-permute-start(bf16[2,128,1664]{2,1,0:T(8,128)(2,1)S(1)} %dynamic-slice_bitcast_fusion.3), channel_id=1, source_target_pairs={{0,8},{8,0},{16,24},{24,16},{1,9},{9,1},{17,25},{25,17},{2,10},{10... | collective-permute-start | bytes 2555912 | tf_op jit(solution)/shard_map/ppermute | solution.py:93
  131.7 12.1 %collective-permute-start.23 = (bf16[1,128,1664]{2,1,0:T(8,128)(2,1)S(1)}, bf16[1,128,1664]{2,1,0:T(8,128)(2,1)S(1)}, u32[]{:S(2)}, u32[]{:S(2)}) collective-permute-start(bf16[1,128,1664]{2,1,0:T(8,128)(2,1)S(1)} %fusion.58), channel_id=1, source_target_pairs={{0,16},{8,24},{16,0},{24,8},{1,17},{9,25},{17,1},{25,9},{2,18},{10... | collective-permute-start | bytes 1277960 | tf_op jit(solution)/shard_map/ppermute | solution.py:93
  144.1 12.8 %collective-permute-start.25 = (bf16[1,128,1664]{2,1,0:T(8,128)(2,1)S(1)}, bf16[1,128,1664]{2,1,0:T(8,128)(2,1)S(1)}, u32[]{:S(2)}, u32[]{:S(2)}) collective-permute-start(bf16[1,128,1664]{2,1,0:T(8,128)(2,1)S(1)} %fusion.59), channel_id=1, source_target_pairs={{0,16},{8,24},{16,0},{24,8},{1,17},{9,25},{17,1},{25,9},{2,18},{10... | collective-permute-start | bytes 1277960 | tf_op jit(solution)/shard_map/ppermute | solution.py:93
  145.5 11.5 %collective-permute-start.26 = (bf16[2,128,1664]{2,1,0:T(8,128)(2,1)S(1)}, bf16[2,128,1664]{2,1,0:T(8,128)(2,1)S(1)}, u32[]{:S(2)}, u32[]{:S(2)}) collective-permute-start(bf16[2,128,1664]{2,1,0:T(8,128)(2,1)S(1)} %dynamic-slice_bitcast_fusion.1), channel_id=1, source_target_pairs={{0,8},{8,0},{16,24},{24,16},{1,9},{9,1},{17,25},{25,17},{2,10},{10... | collective-permute-start | bytes 2555912 | tf_op jit(solution)/shard_map/ppermute | solution.py:93
  157.2 12.1 %collective-permute-start.27 = (bf16[1,128,1664]{2,1,0:T(8,128)(2,1)S(1)}, bf16[1,128,1664]{2,1,0:T(8,128)(2,1)S(1)}, u32[]{:S(2)}, u32[]{:S(2)}) collective-permute-start(bf16[1,128,1664]{2,1,0:T(8,128)(2,1)S(1)} %fusion.60), channel_id=1, source_target_pairs={{0,16},{8,24},{16,0},{24,8},{1,17},{9,25},{17,1},{25,9},{2,18},{10... | collective-permute-start | bytes 1277960 | tf_op jit(solution)/shard_map/ppermute | solution.py:93
  169.7 15.1 %collective-permute-start.29 = (bf16[1,128,1664]{2,1,0:T(8,128)(2,1)S(1)}, bf16[1,128,1664]{2,1,0:T(8,128)(2,1)S(1)}, u32[]{:S(2)}, u32[]{:S(2)}) collective-permute-start(bf16[1,128,1664]{2,1,0:T(8,128)(2,1)S(1)} %fusion.61), channel_id=1, source_target_pairs={{0,16},{8,24},{16,0},{24,8},{1,17},{9,25},{17,1},{25,9},{2,18},{10... | collective-permute-start | bytes 1277960 | tf_op jit(solution)/shard_map/ppermute | solution.py:93
  (11 other events, 108.5 us)

commit v7 on v6

--- a/solution.py
+++ b/solution.py
@@ -104,11 +104,13 @@
 
     def on_device(tokens, gate_weight, up_weight):
         local = tokens.shape[0]
-        tc = local // HALVES
+        first = (local * 7 // 16) // 8 * 8
+        sizes = [first, local - first]
+        offs = [0, first]
         group = n_col // n_row
         units = gate_weight.shape[1]
 
-        st = ring.init(tokens[:tc])
+        st = ring.init(tokens[:sizes[0]])
         for s in range(1, ring.steps + 1):
             st = ring.step(st, s)
         piece = ring.result(st)
@@ -135,7 +137,7 @@
             if t < len(tiles):
                 h, w, start, width = tiles[t]
                 if t in firsts and h + 1 < HALVES:
-                    nxt = {"st": ring.init(tokens[(h + 1) * tc:(h + 2) * tc]), "s": 1}
+                    nxt = {"st": ring.init(tokens[offs[h + 1]:offs[h + 1] + sizes[h + 1]]), "s": 1}
                 if nxt is not None and nxt["s"] <= ring.steps:
                     nxt["st"] = ring.step(nxt["st"], nxt["s"])
                     nxt["s"] += 1
@@ -180,8 +182,8 @@
             for h in range(HALVES):
                 ids = [i for i, tl in enumerate(tiles) if tl[0] == h and tl[1] == w]
                 parts.append(jnp.concatenate([done[i] for i in ids], axis=1))
-            x = jnp.stack(parts).reshape(HALVES, group, tc, units)
-            return x.transpose(1, 0, 2, 3).reshape(group * HALVES * tc, units)
+            parts = [x.reshape(group, sizes[h], units) for h, x in enumerate(parts)]
+            return jnp.concatenate(parts, axis=1).reshape(group * local, units)
 
         gate = assemble(0)
         up = assemble(1)

time: 195 us -> 204 us (1.046)
  matrix products: 90.4 us -> 99.7 us
  local copies, waits for them, and re-layouts: 6.73 us -> 13.7 us
  waiting for transfers between devices: 44.1 us -> 37.9 us
    dot_general x9, matrix products: 90.4 us -> 99.7 us  [on_device(): jnp.dot(piece, weight[:, start:start + width], preferred_element_type=jnp...]
    ppermute x6, waiting for transfers between devices: 23.1 us -> 16.7 us  [step(): f = lax.ppermute(st['f'], 'col', self.fwd_pairs)]
    broadcast_in_dim x0 -> x2, local copies, waits for them, and re-layouts: none -> 2.78 us  [init(): buf = jnp.zeros((n,) + x.shape, x.dtype)]
    ppermute x18, waiting for transfers between devices: 15.4 us -> 18.1 us  [reduce_level(): lax.ppermute(send.astype(jnp.bfloat16), 'row', [(i, i ^ d) for i in range...]
    dynamic_update_slice x6, local copies, waits for them, and re-layouts: 0.23 us -> 2.6 us  [step(): buf = lax.dynamic_update_slice(buf, f[None], (order_t[(p - s) % n], 0, 0))]
    dynamic_update_slice x6, local copies, waits for them, and re-layouts: 0.25 us -> 2.56 us  [step(): buf = lax.dynamic_update_slice(buf, b[None], (order_t[(p + s) % n], 0, 0))]
  transfers between devices with their start and end apart: 34 -> 34, of which waited for: 9 -> 9; matrix products, arithmetic and copies ran while one was open for 50% -> 55% of each run, Pallas kernels for 0% -> 0%
where the time goes in v7:
time: 204 us
  matrix products  99.7 us (49%)
  waiting for transfers between devices  37.9 us (19%)
  starting transfers between devices  28.6 us (14%)
  between operations  18.3 us (9%)
  local copies, waits for them, and re-layouts  13.7 us (7%)
  other arithmetic  5.17 us (3%)
    dot_general x9, matrix products, on_device(): jnp.dot(piece, weight[:, start:start + width], preferred_element_type=jnp...  99.7 us
    ppermute x18, waiting for transfers between devices, reduce_level(): lax.ppermute(send.astype(jnp.bfloat16), 'row', [(i, i ^ d) for i in range...  18.1 us
    ppermute x6, waiting for transfers between devices, step(): f = lax.ppermute(st['f'], 'col', self.fwd_pairs)  16.7 us
    ppermute x6, starting transfers between devices, step(): f = lax.ppermute(st['f'], 'col', self.fwd_pairs)  11.5 us
    ppermute x18, starting transfers between devices, reduce_level(): lax.ppermute(send.astype(jnp.bfloat16), 'row', [(i, i ^ d) for i in range...  11 us
  transfers between devices with their start and end apart: 34, of which 9 were waited for; matrix products, arithmetic and copies ran while one was open for 55% of the time, Pallas kernels for 0%

profile of v7, /device:TPU:0, one launch (start us, length us, event | category | flops | bytes accessed | tf_op | source)
XLA Modules:
  0.0 203.5 jit_solution(6449148206517168023)
XLA Ops:
  1.1 3.1 %collective-permute-start = (bf16[56,4096]{1,0:T(8,128)(2,1)S(1)}, bf16[56,4096]{1,0:T(8,128)(2,1)S(1)}, u32[]{:S(2)}, u32[]{:S(2)}) collective-permute-start(bf16[56,4096]{1,0:T(8,128)(2,1)S(1)} %slice.39), channel_id=1, source_target_pairs={{0,2},{2,4},{4,6},{6,7},{7,5},{5,3},{3,1},{1,0},{8,10},{10,12},{12... | collective-permute-start | bytes 1376264 | tf_op jit(solution)/shard_map/ppermute | solution.py:74
  4.3 2.2 %broadcast_in_dim.60 = bf16[8,56,4096]{2,1,0:T(8,128)(2,1)} broadcast(bf16[]{:T(256)} %constant.262.clone.1), dimensions={} | broadcast | bytes 3670018 | tf_op jit(solution)/shard_map/broadcast_in_dim | solution.py:55
  26.2 2.1 %collective-permute-start.2 = (bf16[56,4096]{1,0:T(8,128)(2,1)S(1)}, bf16[56,4096]{1,0:T(8,128)(2,1)S(1)}, u32[]{:S(2)}, u32[]{:S(2)}) collective-permute-start(bf16[56,4096]{1,0:T(8,128)(2,1)S(1)} %collective-permute-done), channel_id=1, source_target_pairs={{0,2},{2,4},{4,6},{6,7},{7,5},{5,3},{3,1},{1,0},{8,10},{10,12},{12... | collective-permute-start | bytes 1376264 | tf_op jit(solution)/shard_map/ppermute | solution.py:74
  29.9 8.3 %collective-permute-done.2 = bf16[56,4096]{1,0:T(8,128)(2,1)S(1)} collective-permute-done((bf16[56,4096]{1,0:T(8,128)(2,1)S(1)}, bf16[56,4096]{1,0:T(8,128)(2,1)S(1)}, u32[]{:S(2)}, u32[]{:S(2)}) %collective-permute-start.2) | collective-permute-done | bytes 458784 | tf_op jit(solution)/shard_map/ppermute | solution.py:74
  38.3 1.7 collective-permute-start.4
  41.9 7.5 %collective-permute-done.4 = bf16[56,4096]{1,0:T(8,128)(2,1)S(1)} collective-permute-done((bf16[56,4096]{1,0:T(8,128)(2,1)S(1)}, bf16[56,4096]{1,0:T(8,128)(2,1)S(1)}, u32[]{:S(2)}, u32[]{:S(2)}) %collective-permute-start.4) | collective-permute-done | bytes 458784 | tf_op jit(solution)/shard_map/ppermute | solution.py:74
  53.2 2.3 %collective-permute-done.6 = bf16[56,2048]{1,0:T(8,128)(2,1)S(1)} collective-permute-done((bf16[56,2048]{1,0:T(8,128)(2,1)S(1)}, bf16[56,2048]{1,0:T(8,128)(2,1)S(1)}, u32[]{:S(2)}, u32[]{:S(2)}) %collective-permute-start.6) | collective-permute-done | bytes 229408 | tf_op jit(solution)/shard_map/ppermute | solution.py:68
  57.8 1.6 collective-permute-start.9
  59.9 12.4 %fusion.34 = bf16[448,1664]{1,0:T(8,128)(2,1)S(1)} fusion(bf16[448,4096]{1,0:T(8,128)(2,1)} %bitcast.23, bf16[4096,3328]{1,0:T(8,128)(2,1)} %param.13), kind=kOutput, calls=%fused_computation.31 | convolution fusion | flops 6107652096 | bytes 18792448 | tf_op jit(solution)/shard_map/dot_general | solution.py:145
  75.3 12.4 %fusion.37 = bf16[448,1664]{1,0:T(8,128)(2,1)S(1)} fusion(bf16[448,4096]{1,0:T(8,128)(2,1)} %bitcast.23, bf16[4096,3328]{1,0:T(8,128)(2,1)} %param.13), kind=kOutput, calls=%fused_computation.32 | convolution fusion | flops 6107652096 | bytes 18792448 | tf_op jit(solution)/shard_map/dot_general | solution.py:145
  88.1 1.6 collective-permute-start.13
  91.9 12.5 %fusion.40 = bf16[448,1664]{1,0:T(8,128)(2,1)S(1)} fusion(bf16[448,4096]{1,0:T(8,128)(2,1)} %bitcast.23, bf16[4096,3328]{1,0:T(8,128)(2,1)} %param.14), kind=kOutput, calls=%fused_computation.33 | convolution fusion | flops 6107652096 | bytes 18792448 | tf_op jit(solution)/shard_map/dot_general | solution.py:145
  108.6 12.4 %fusion.43 = bf16[448,1664]{1,0:T(8,128)(2,1)S(1)} fusion(bf16[448,4096]{1,0:T(8,128)(2,1)} %bitcast.23, bf16[4096,3328]{1,0:T(8,128)(2,1)} %param.14), kind=kOutput, calls=%fused_computation.34 | convolution fusion | flops 6107652096 | bytes 18792448 | tf_op jit(solution)/shard_map/dot_general | solution.py:145
  121.5 1.6 collective-permute-start.21
  123.4 12.0 %fusion.25 = bf16[576,1664]{1,0:T(8,128)(2,1)S(1)} fusion(bf16[576,4096]{1,0:T(8,128)(2,1)S(1)} %bitcast.213, bf16[4096,3328]{1,0:T(8,128)(2,1)} %param.13), kind=kOutput, calls=%fused_computation.28 | convolution fusion | flops 7852695552 | bytes 20267008 | tf_op jit(solution)/shard_map/dot_general | solution.py:145
  136.5 12.0 %fusion.28 = bf16[576,1664]{1,0:T(8,128)(2,1)S(1)} fusion(bf16[576,4096]{1,0:T(8,128)(2,1)S(1)} %bitcast.214, bf16[4096,3328]{1,0:T(8,128)(2,1)} %param.13), kind=kOutput, calls=%fused_computation.29 | convolution fusion | flops 7852695552 | bytes 20267008 | tf_op jit(solution)/shard_map/dot_general | solution.py:145
  148.9 1.6 collective-permute-start.25
  150.8 12.0 %fusion.31 = bf16[576,1664]{1,0:T(8,128)(2,1)S(1)} fusion(bf16[576,4096]{1,0:T(8,128)(2,1)S(1)} %bitcast.215, bf16[4096,3328]{1,0:T(8,128)(2,1)} %param.14), kind=kOutput, calls=%fused_computation.30 | convolution fusion | flops 7852695552 | bytes 20267008 | tf_op jit(solution)/shard_map/dot_general | solution.py:145
  164.4 8.9 %fusion.22 = bf16[576,1152]{1,0:T(8,128)(2,1)S(1)} fusion(bf16[576,4096]{1,0:T(8,128)(2,1)S(1)} %bitcast.216, bf16[4096,3328]{1,0:T(8,128)(2,1)} %param.14), kind=kOutput, calls=%fused_computation.27 | convolution fusion | flops 5436481536 | bytes 15482880 | tf_op jit(solution)/shard_map/dot_general | solution.py:145
  173.4 3.1 %collective-permute-done.27 = bf16[1,144,1664]{2,1,0:T(8,128)(2,1)S(1)} collective-permute-done((bf16[1,144,1664]{2,1,0:T(8,128)(2,1)S(1)}, bf16[1,144,1664]{2,1,0:T(8,128)(2,1)S(1)}, u32[]{:S(2)}, u32[]{:S(2)}) %collective-permute-start.27) | collective-permute-done | bytes 479264 | tf_op jit(solution)/shard_map/ppermute | solution.py:93
  177.5 4.8 %fusion.46 = bf16[576,512]{1,0:T(8,128)(2,1)S(1)} fusion(bf16[576,4096]{1,0:T(8,128)(2,1)S(1)} %bitcast.217, bf16[4096,3328]{1,0:T(8,128)(2,1)} %param.14), kind=kOutput, calls=%fused_computation.46 | convolution fusion | flops 2416214016 | bytes 9502720 | tf_op jit(solution)/shard_map/dot_general | solution.py:145
  185.8 6.6 %collective-permute-done.33 = bf16[1,144,512]{2,1,0:T(8,128)(2,1)S(1)} collective-permute-done((bf16[1,144,512]{2,1,0:T(8,128)(2,1)S(1)}, bf16[1,144,512]{2,1,0:T(8,128)(2,1)S(1)}, u32[]{:S(2)}, u32[]{:S(2)}) %collective-permute-start.33) | collective-permute-done | bytes 147488 | tf_op jit(solution)/shard_map/ppermute | solution.py:93
  193.1 7.9 %collective-permute-done.31 = bf16[1,144,1152]{2,1,0:T(8,128)(2,1)S(1)} collective-permute-done((bf16[1,144,1152]{2,1,0:T(8,128)(2,1)S(1)}, bf16[1,144,1152]{2,1,0:T(8,128)(2,1)S(1)}, u32[]{:S(2)}, u32[]{:S(2)}) %collective-permute-start.31) | collective-permute-done | bytes 331808 | tf_op jit(solution)/shard_map/ppermute | solution.py:93
  201.3 2.2 %fusion.18 = bf16[256,3328]{1,0:T(8,128)(2,1)} fusion(f32[2,128,3328]{2,1,0:T(8,128)S(1)} %maximum_maximum_fusion, f32[2,128,3328]{2,1,0:T(8,128)S(1)} %pad_maximum_fusion), kind=kLoop, calls=%fused_computation.21 | loop fusion | flops 5111808 | bytes 8519680 | tf_op jit(solution)/shard_map/convert_element_type | solution.py:190
  (129 shorter events, 32.1 us)
Async XLA Ops:
  1.1 25.1 %collective-permute-start = (bf16[56,4096]{1,0:T(8,128)(2,1)S(1)}, bf16[56,4096]{1,0:T(8,128)(2,1)S(1)}, u32[]{:S(2)}, u32[]{:S(2)}) collective-permute-start(bf16[56,4096]{1,0:T(8,128)(2,1)S(1)} %slice.39), channel_id=1, source_target_pairs={{0,2},{2,4},{4,6},{6,7},{7,5},{5,3},{3,1},{1,0},{8,10},{10,12},{12... | collective-permute-start | bytes 1376264 | tf_op jit(solution)/shard_map/ppermute | solution.py:74
  4.3 24.1 %collective-permute-start.1 = (bf16[56,4096]{1,0:T(8,128)(2,1)S(1)}, bf16[56,4096]{1,0:T(8,128)(2,1)S(1)}, u32[]{:S(2)}, u32[]{:S(2)}) collective-permute-start(bf16[56,4096]{1,0:T(8,128)(2,1)S(1)} %slice.39), channel_id=1, source_target_pairs={{0,1},{2,0},{4,2},{6,4},{7,6},{5,7},{3,5},{1,3},{8,9},{10,8},{12,1... | collective-permute-start | bytes 1376264 | tf_op jit(solution)/shard_map/ppermute | solution.py:77
  57.8 15.2 %collective-permute-start.9 = (bf16[72,4096]{1,0:T(8,128)(2,1)S(1)}, bf16[72,4096]{1,0:T(8,128)(2,1)S(1)}, u32[]{:S(2)}, u32[]{:S(2)}) collective-permute-start(bf16[72,4096]{1,0:T(8,128)(2,1)S(1)} %slice.43), channel_id=1, source_target_pairs={{0,2},{2,4},{4,6},{6,7},{7,5},{5,3},{3,1},{1,0},{8,10},{10,12},{12... | collective-permute-start | bytes 1769480 | tf_op jit(solution)/shard_map/ppermute | solution.py:74
  59.4 13.6 %collective-permute-start.8 = (bf16[72,4096]{1,0:T(8,128)(2,1)S(1)}, bf16[72,4096]{1,0:T(8,128)(2,1)S(1)}, u32[]{:S(2)}, u32[]{:S(2)}) collective-permute-start(bf16[72,4096]{1,0:T(8,128)(2,1)S(1)} %slice.43), channel_id=1, source_target_pairs={{0,1},{2,0},{4,2},{6,4},{7,6},{5,7},{3,5},{1,3},{8,9},{10,8},{12,1... | collective-permute-start | bytes 1769480 | tf_op jit(solution)/shard_map/ppermute | solution.py:77
  73.1 14.7 %collective-permute-start.11 = (bf16[72,4096]{1,0:T(8,128)(2,1)S(1)}, bf16[72,4096]{1,0:T(8,128)(2,1)S(1)}, u32[]{:S(2)}, u32[]{:S(2)}) collective-permute-start(bf16[72,4096]{1,0:T(8,128)(2,1)S(1)} %collective-permute-done.8), channel_id=1, source_target_pairs={{0,1},{2,0},{4,2},{6,4},{7,6},{5,7},{3,5},{1,3},{8,9},{10,8},{12,1... | collective-permute-start | bytes 1769480 | tf_op jit(solution)/shard_map/ppermute | solution.py:77
  73.7 14.0 %collective-permute-start.12 = (bf16[72,4096]{1,0:T(8,128)(2,1)S(1)}, bf16[72,4096]{1,0:T(8,128)(2,1)S(1)}, u32[]{:S(2)}, u32[]{:S(2)}) collective-permute-start(bf16[72,4096]{1,0:T(8,128)(2,1)S(1)} %collective-permute-done.9), channel_id=1, source_target_pairs={{0,2},{2,4},{4,6},{6,7},{7,5},{5,3},{3,1},{1,0},{8,10},{10,12},{12... | collective-permute-start | bytes 1769480 | tf_op jit(solution)/shard_map/ppermute | solution.py:74
  75.2 12.7 %collective-permute-start.10 = (bf16[2,112,1664]{2,1,0:T(8,128)(2,1)S(1)}, bf16[2,112,1664]{2,1,0:T(8,128)(2,1)S(1)}, u32[]{:S(2)}, u32[]{:S(2)}) collective-permute-start(bf16[2,112,1664]{2,1,0:T(8,128)(2,1)S(1)} %dynamic-slice_bitcast_fusion.6), channel_id=1, source_target_pairs={{0,8},{8,0},{16,24},{24,16},{1,9},{9,1},{17,25},{25,17},{2,10},{10... | collective-permute-start | bytes 2236424 | tf_op jit(solution)/shard_map/ppermute | solution.py:93
  88.1 16.3 %collective-permute-start.13 = (bf16[1,112,1664]{2,1,0:T(8,128)(2,1)S(1)}, bf16[1,112,1664]{2,1,0:T(8,128)(2,1)S(1)}, u32[]{:S(2)}, u32[]{:S(2)}) collective-permute-start(bf16[1,112,1664]{2,1,0:T(8,128)(2,1)S(1)} %fusion.58), channel_id=1, source_target_pairs={{0,16},{8,24},{16,0},{24,8},{1,17},{9,25},{17,1},{25,9},{2,18},{10... | collective-permute-start | bytes 1118216 | tf_op jit(solution)/shard_map/ppermute | solution.py:93
  89.7 15.8 %collective-permute-start.15 = (bf16[72,4096]{1,0:T(8,128)(2,1)S(1)}, bf16[72,4096]{1,0:T(8,128)(2,1)S(1)}, u32[]{:S(2)}, u32[]{:S(2)}) collective-permute-start(bf16[72,4096]{1,0:T(8,128)(2,1)S(1)} %collective-permute-done.11), channel_id=1, source_target_pairs={{0,1},{2,0},{4,2},{6,4},{7,6},{5,7},{3,5},{1,3},{8,9},{10,8},{12,1... | collective-permute-start | bytes 1769480 | tf_op jit(solution)/shard_map/ppermute | solution.py:77
  90.3 15.1 %collective-permute-start.16 = (bf16[72,4096]{1,0:T(8,128)(2,1)S(1)}, bf16[72,4096]{1,0:T(8,128)(2,1)S(1)}, u32[]{:S(2)}, u32[]{:S(2)}) collective-permute-start(bf16[72,4096]{1,0:T(8,128)(2,1)S(1)} %collective-permute-done.12), channel_id=1, source_target_pairs={{0,2},{2,4},{4,6},{6,7},{7,5},{5,3},{3,1},{1,0},{8,10},{10,12},{12... | collective-permute-start | bytes 1769480 | tf_op jit(solution)/shard_map/ppermute | solution.py:74
  91.8 13.7 %collective-permute-start.14 = (bf16[2,112,1664]{2,1,0:T(8,128)(2,1)S(1)}, bf16[2,112,1664]{2,1,0:T(8,128)(2,1)S(1)}, u32[]{:S(2)}, u32[]{:S(2)}) collective-permute-start(bf16[2,112,1664]{2,1,0:T(8,128)(2,1)S(1)} %dynamic-slice_bitcast_fusion.5), channel_id=1, source_target_pairs={{0,8},{8,0},{16,24},{24,16},{1,9},{9,1},{17,25},{25,17},{2,10},{10... | collective-permute-start | bytes 2236424 | tf_op jit(solution)/shard_map/ppermute | solution.py:93
  105.8 15.3 %collective-permute-start.20 = (bf16[72,2048]{1,0:T(8,128)(2,1)S(1)}, bf16[72,2048]{1,0:T(8,128)(2,1)S(1)}, u32[]{:S(2)}, u32[]{:S(2)}) collective-permute-start(bf16[72,2048]{1,0:T(8,128)(2,1)S(1)} %slice.48), channel_id=1, source_target_pairs={{0,2},{2,4},{4,6},{6,7},{7,5},{5,3},{3,1},{1,0},{8,10},{10,12},{12... | collective-permute-start | bytes 884744 | tf_op jit(solution)/shard_map/ppermute | solution.py:68
  107.3 13.8 %collective-permute-start.19 = (bf16[72,2048]{1,0:T(8,128)(2,1)S(1)}, bf16[72,2048]{1,0:T(8,128)(2,1)S(1)}, u32[]{:S(2)}, u32[]{:S(2)}) collective-permute-start(bf16[72,2048]{1,0:T(8,128)(2,1)S(1)} %slice.47), channel_id=1, source_target_pairs={{0,1},{2,0},{4,2},{6,4},{7,6},{5,7},{3,5},{1,3},{8,9},{10,8},{12,1... | collective-permute-start | bytes 884744 | tf_op jit(solution)/shard_map/ppermute | solution.py:69
  107.9 13.3 %collective-permute-start.17 = (bf16[1,112,1664]{2,1,0:T(8,128)(2,1)S(1)}, bf16[1,112,1664]{2,1,0:T(8,128)(2,1)S(1)}, u32[]{:S(2)}, u32[]{:S(2)}) collective-permute-start(bf16[1,112,1664]{2,1,0:T(8,128)(2,1)S(1)} %fusion.59), channel_id=1, source_target_pairs={{0,16},{8,24},{16,0},{24,8},{1,17},{9,25},{17,1},{25,9},{2,18},{10... | collective-permute-start | bytes 1118216 | tf_op jit(solution)/shard_map/ppermute | solution.py:93
  108.5 12.7 %collective-permute-start.18 = (bf16[2,112,1664]{2,1,0:T(8,128)(2,1)S(1)}, bf16[2,112,1664]{2,1,0:T(8,128)(2,1)S(1)}, u32[]{:S(2)}, u32[]{:S(2)}) collective-permute-start(bf16[2,112,1664]{2,1,0:T(8,128)(2,1)S(1)} %dynamic-slice_bitcast_fusion.4), channel_id=1, source_target_pairs={{0,8},{8,0},{16,24},{24,16},{1,9},{9,1},{17,25},{25,17},{2,10},{10... | collective-permute-start | bytes 2236424 | tf_op jit(solution)/shard_map/ppermute | solution.py:93
  121.5 14.0 %collective-permute-start.21 = (bf16[1,112,1664]{2,1,0:T(8,128)(2,1)S(1)}, bf16[1,112,1664]{2,1,0:T(8,128)(2,1)S(1)}, u32[]{:S(2)}, u32[]{:S(2)}) collective-permute-start(bf16[1,112,1664]{2,1,0:T(8,128)(2,1)S(1)} %fusion.60), channel_id=1, source_target_pairs={{0,16},{8,24},{16,0},{24,8},{1,17},{9,25},{17,1},{25,9},{2,18},{10... | collective-permute-start | bytes 1118216 | tf_op jit(solution)/shard_map/ppermute | solution.py:93
  123.1 12.4 %collective-permute-start.22 = (bf16[2,112,1664]{2,1,0:T(8,128)(2,1)S(1)}, bf16[2,112,1664]{2,1,0:T(8,128)(2,1)S(1)}, u32[]{:S(2)}, u32[]{:S(2)}) collective-permute-start(bf16[2,112,1664]{2,1,0:T(8,128)(2,1)S(1)} %dynamic-slice_bitcast_fusion.3), channel_id=1, source_target_pairs={{0,8},{8,0},{16,24},{24,16},{1,9},{9,1},{17,25},{25,17},{2,10},{10... | collective-permute-start | bytes 2236424 | tf_op jit(solution)/shard_map/ppermute | solution.py:93
  135.7 12.8 %collective-permute-start.23 = (bf16[1,112,1664]{2,1,0:T(8,128)(2,1)S(1)}, bf16[1,112,1664]{2,1,0:T(8,128)(2,1)S(1)}, u32[]{:S(2)}, u32[]{:S(2)}) collective-permute-start(bf16[1,112,1664]{2,1,0:T(8,128)(2,1)S(1)} %fusion.61), channel_id=1, source_target_pairs={{0,16},{8,24},{16,0},{24,8},{1,17},{9,25},{17,1},{25,9},{2,18},{10... | collective-permute-start | bytes 1118216 | tf_op jit(solution)/shard_map/ppermute | solution.py:93
  136.4 12.2 %collective-permute-start.24 = (bf16[2,144,1664]{2,1,0:T(8,128)(2,1)S(1)}, bf16[2,144,1664]{2,1,0:T(8,128)(2,1)S(1)}, u32[]{:S(2)}, u32[]{:S(2)}) collective-permute-start(bf16[2,144,1664]{2,1,0:T(8,128)(2,1)S(1)} %dynamic-slice_bitcast_fusion.2), channel_id=1, source_target_pairs={{0,8},{8,0},{16,24},{24,16},{1,9},{9,1},{17,25},{25,17},{2,10},{10... | collective-permute-start | bytes 2875400 | tf_op jit(solution)/shard_map/ppermute | solution.py:93
  148.9 14.0 %collective-permute-start.25 = (bf16[1,144,1664]{2,1,0:T(8,128)(2,1)S(1)}, bf16[1,144,1664]{2,1,0:T(8,128)(2,1)S(1)}, u32[]{:S(2)}, u32[]{:S(2)}) collective-permute-start(bf16[1,144,1664]{2,1,0:T(8,128)(2,1)S(1)} %fusion.55), channel_id=1, source_target_pairs={{0,16},{8,24},{16,0},{24,8},{1,17},{9,25},{17,1},{25,9},{2,18},{10... | collective-permute-start | bytes 1437704 | tf_op jit(solution)/shard_map/ppermute | solution.py:93
  150.6 12.4 %collective-permute-start.26 = (bf16[2,144,1664]{2,1,0:T(8,128)(2,1)S(1)}, bf16[2,144,1664]{2,1,0:T(8,128)(2,1)S(1)}, u32[]{:S(2)}, u32[]{:S(2)}) collective-permute-start(bf16[2,144,1664]{2,1,0:T(8,128)(2,1)S(1)} %dynamic-slice_bitcast_fusion.1), channel_id=1, source_target_pairs={{0,8},{8,0},{16,24},{24,16},{1,9},{9,1},{17,25},{25,17},{2,10},{10... | collective-permute-start | bytes 2875400 | tf_op jit(solution)/shard_map/ppermute | solution.py:93
  163.3 13.2 %collective-permute-start.27 = (bf16[1,144,1664]{2,1,0:T(8,128)(2,1)S(1)}, bf16[1,144,1664]{2,1,0:T(8,128)(2,1)S(1)}, u32[]{:S(2)}, u32[]{:S(2)}) collective-permute-start(bf16[1,144,1664]{2,1,0:T(8,128)(2,1)S(1)} %fusion.56), channel_id=1, source_target_pairs={{0,16},{8,24},{16,0},{24,8},{1,17},{9,25},{17,1},{25,9},{2,18},{10... | collective-permute-start | bytes 1437704 | tf_op jit(solution)/shard_map/ppermute | solution.py:93
  164.4 12.2 %collective-permute-start.28 = (bf16[2,144,1664]{2,1,0:T(8,128)(2,1)S(1)}, bf16[2,144,1664]{2,1,0:T(8,128)(2,1)S(1)}, u32[]{:S(2)}, u32[]{:S(2)}) collective-permute-start(bf16[2,144,1664]{2,1,0:T(8,128)(2,1)S(1)} %dynamic-slice_bitcast_fusion), channel_id=1, source_target_pairs={{0,8},{8,0},{16,24},{24,16},{1,9},{9,1},{17,25},{25,17},{2,10},{10... | collective-permute-start | bytes 2875400 | tf_op jit(solution)/shard_map/ppermute | solution.py:93
  176.9 16.1 %collective-permute-start.29 = (bf16[1,144,1664]{2,1,0:T(8,128)(2,1)S(1)}, bf16[1,144,1664]{2,1,0:T(8,128)(2,1)S(1)}, u32[]{:S(2)}, u32[]{:S(2)}) collective-permute-start(bf16[1,144,1664]{2,1,0:T(8,128)(2,1)S(1)} %fusion.57), channel_id=1, source_target_pairs={{0,16},{8,24},{16,0},{24,8},{1,17},{9,25},{17,1},{25,9},{2,18},{10... | collective-permute-start | bytes 1437704 | tf_op jit(solution)/shard_map/ppermute | solution.py:93
  (13 other events, 112.4 us)

commit v8 on v7

--- a/solution.py
+++ b/solution.py
@@ -104,7 +104,7 @@
 
     def on_device(tokens, gate_weight, up_weight):
         local = tokens.shape[0]
-        first = (local * 7 // 16) // 8 * 8
+        first = (local * 9 // 16) // 8 * 8
         sizes = [first, local - first]
         offs = [0, first]
         group = n_col // n_row

time: 204 us -> 197 us (0.966)
  matrix products: 99.7 us -> 89 us
  waiting for transfers between devices: 37.9 us -> 47.8 us
  local copies, waits for them, and re-layouts: 13.7 us -> 6.81 us
    dot_general x9, matrix products: 99.7 us -> 89 us  [on_device(): jnp.dot(piece, weight[:, start:start + width], preferred_element_type=jnp...]
    ppermute x6, waiting for transfers between devices: 16.7 us -> 24.4 us  [step(): f = lax.ppermute(st['f'], 'col', self.fwd_pairs)]
    dynamic_update_slice x6, local copies, waits for them, and re-layouts: 2.6 us -> 0.26 us  [step(): buf = lax.dynamic_update_slice(buf, f[None], (order_t[(p - s) % n], 0, 0))]
    dynamic_update_slice x6, local copies, waits for them, and re-layouts: 2.56 us -> 0.27 us  [step(): buf = lax.dynamic_update_slice(buf, b[None], (order_t[(p + s) % n], 0, 0))]
    ppermute x2, waiting for transfers between devices: 2.3 us -> 4.53 us  [step(): f = lax.ppermute(st['f'][:, :k2], 'col', self.fwd_pairs)]
  transfers between devices with their start and end apart: 34 -> 34, of which waited for: 9 -> 10; matrix products, arithmetic and copies ran while one was open for 55% -> 49% of each run, Pallas kernels for 0% -> 0%
where the time goes in v8:
time: 197 us
  matrix products  89 us (45%)
  waiting for transfers between devices  47.8 us (24%)
  starting transfers between devices  29.4 us (15%)
  between operations  18.5 us (9%)
  local copies, waits for them, and re-layouts  6.81 us (3%)
  other arithmetic  5.15 us (3%)
    dot_general x9, matrix products, on_device(): jnp.dot(piece, weight[:, start:start + width], preferred_element_type=jnp...  89 us
    ppermute x6, waiting for transfers between devices, step(): f = lax.ppermute(st['f'], 'col', self.fwd_pairs)  24.4 us
    ppermute x18, waiting for transfers between devices, reduce_level(): lax.ppermute(send.astype(jnp.bfloat16), 'row', [(i, i ^ d) for i in range...  17.4 us
    ppermute x18, starting transfers between devices, reduce_level(): lax.ppermute(send.astype(jnp.bfloat16), 'row', [(i, i ^ d) for i in range...  11.8 us
    ppermute x6, starting transfers between devices, step(): f = lax.ppermute(st['f'], 'col', self.fwd_pairs)  11.5 us
    ppermute x2, waiting for transfers between devices, step(): f = lax.ppermute(st['f'][:, :k2], 'col', self.fwd_pairs)  4.53 us
  transfers between devices with their start and end apart: 34, of which 10 were waited for; matrix products, arithmetic and copies ran while one was open for 49% of the time, Pallas kernels for 0%

profile of v8, /device:TPU:0, one launch (start us, length us, event | category | flops | bytes accessed | tf_op | source)
XLA Modules:
  0.0 196.7 jit_solution(1360215024270311406)
XLA Ops:
  1.2 3.1 %collective-permute-start = (bf16[72,4096]{1,0:T(8,128)(2,1)S(1)}, bf16[72,4096]{1,0:T(8,128)(2,1)S(1)}, u32[]{:S(2)}, u32[]{:S(2)}) collective-permute-start(bf16[72,4096]{1,0:T(8,128)(2,1)S(1)} %slice.39), channel_id=1, source_target_pairs={{0,2},{2,4},{4,6},{6,7},{7,5},{5,3},{3,1},{1,0},{8,10},{10,12},{12... | collective-permute-start | bytes 1769480 | tf_op jit(solution)/shard_map/ppermute | solution.py:74
  10.2 1.6 fusion.62
  25.6 2.1 %collective-permute-start.2 = (bf16[72,4096]{1,0:T(8,128)(2,1)S(1)}, bf16[72,4096]{1,0:T(8,128)(2,1)S(1)}, u32[]{:S(2)}, u32[]{:S(2)}) collective-permute-start(bf16[72,4096]{1,0:T(8,128)(2,1)S(1)} %collective-permute-done), channel_id=1, source_target_pairs={{0,2},{2,4},{4,6},{6,7},{7,5},{5,3},{3,1},{1,0},{8,10},{10,12},{12... | collective-permute-start | bytes 1769480 | tf_op jit(solution)/shard_map/ppermute | solution.py:74
  27.8 12.6 %collective-permute-done.2 = bf16[72,4096]{1,0:T(8,128)(2,1)S(1)} collective-permute-done((bf16[72,4096]{1,0:T(8,128)(2,1)S(1)}, bf16[72,4096]{1,0:T(8,128)(2,1)S(1)}, u32[]{:S(2)}, u32[]{:S(2)}) %collective-permute-start.2) | collective-permute-done | bytes 589856 | tf_op jit(solution)/shard_map/ppermute | solution.py:74
  40.4 1.7 collective-permute-start.4
  42.6 11.8 %collective-permute-done.4 = bf16[72,4096]{1,0:T(8,128)(2,1)S(1)} collective-permute-done((bf16[72,4096]{1,0:T(8,128)(2,1)S(1)}, bf16[72,4096]{1,0:T(8,128)(2,1)S(1)}, u32[]{:S(2)}, u32[]{:S(2)}) %collective-permute-start.4) | collective-permute-done | bytes 589856 | tf_op jit(solution)/shard_map/ppermute | solution.py:74
  56.7 4.5 %collective-permute-done.6 = bf16[72,2048]{1,0:T(8,128)(2,1)S(1)} collective-permute-done((bf16[72,2048]{1,0:T(8,128)(2,1)S(1)}, bf16[72,2048]{1,0:T(8,128)(2,1)S(1)}, u32[]{:S(2)}, u32[]{:S(2)}) %collective-permute-start.6) | collective-permute-done | bytes 294944 | tf_op jit(solution)/shard_map/ppermute | solution.py:68
  62.8 1.6 collective-permute-start.9
  64.8 12.0 %fusion.22 = bf16[576,1664]{1,0:T(8,128)(2,1)S(1)} fusion(bf16[576,4096]{1,0:T(8,128)(2,1)S(1)} %bitcast.215, bf16[4096,3328]{1,0:T(8,128)(2,1)} %param.13), kind=kOutput, calls=%fused_computation.27 | convolution fusion | flops 7852695552 | bytes 20267008 | tf_op jit(solution)/shard_map/dot_general | solution.py:145
  79.7 12.0 %fusion.25 = bf16[576,1664]{1,0:T(8,128)(2,1)S(1)} fusion(bf16[576,4096]{1,0:T(8,128)(2,1)S(1)} %bitcast.216, bf16[4096,3328]{1,0:T(8,128)(2,1)} %param.13), kind=kOutput, calls=%fused_computation.28 | convolution fusion | flops 7852695552 | bytes 20267008 | tf_op jit(solution)/shard_map/dot_general | solution.py:145
  94.2 1.6 collective-permute-start.13
  95.9 12.0 %fusion.28 = bf16[576,1664]{1,0:T(8,128)(2,1)S(1)} fusion(bf16[576,4096]{1,0:T(8,128)(2,1)S(1)} %bitcast.217, bf16[4096,3328]{1,0:T(8,128)(2,1)} %param.14), kind=kOutput, calls=%fused_computation.29 | convolution fusion | flops 7852695552 | bytes 20267008 | tf_op jit(solution)/shard_map/dot_general | solution.py:145
  108.5 1.8 collective-permute-start.20
  111.4 12.1 %fusion.31 = bf16[576,1664]{1,0:T(8,128)(2,1)S(1)} fusion(bf16[576,4096]{1,0:T(8,128)(2,1)S(1)} %bitcast.218, bf16[4096,3328]{1,0:T(8,128)(2,1)} %param.14), kind=kOutput, calls=%fused_computation.30 | convolution fusion | flops 7852695552 | bytes 20267008 | tf_op jit(solution)/shard_map/dot_general | solution.py:145
  125.9 9.6 %fusion.34 = bf16[448,1664]{1,0:T(8,128)(2,1)S(1)} fusion(bf16[448,4096]{1,0:T(8,128)(2,1)S(1)} %bitcast.225, bf16[4096,3328]{1,0:T(8,128)(2,1)} %param.13), kind=kOutput, calls=%fused_computation.31 | convolution fusion | flops 6107652096 | bytes 18792448 | tf_op jit(solution)/shard_map/dot_general | solution.py:145
  135.6 1.9 collective-permute-done.21
  139.5 9.7 %fusion.37 = bf16[448,1664]{1,0:T(8,128)(2,1)S(1)} fusion(bf16[448,4096]{1,0:T(8,128)(2,1)S(1)} %bitcast.226, bf16[4096,3328]{1,0:T(8,128)(2,1)} %param.13), kind=kOutput, calls=%fused_computation.32 | convolution fusion | flops 6107652096 | bytes 18792448 | tf_op jit(solution)/shard_map/dot_general | solution.py:145
  152.4 9.7 %fusion.40 = bf16[448,1664]{1,0:T(8,128)(2,1)S(1)} fusion(bf16[448,4096]{1,0:T(8,128)(2,1)S(1)} %bitcast.227, bf16[4096,3328]{1,0:T(8,128)(2,1)} %param.14), kind=kOutput, calls=%fused_computation.33 | convolution fusion | flops 6107652096 | bytes 18792448 | tf_op jit(solution)/shard_map/dot_general | solution.py:145
  163.4 7.6 %fusion.43 = bf16[448,1152]{1,0:T(8,128)(2,1)S(1)} fusion(bf16[448,4096]{1,0:T(8,128)(2,1)S(1)} %bitcast.228, bf16[4096,3328]{1,0:T(8,128)(2,1)} %param.14), kind=kOutput, calls=%fused_computation.34 | convolution fusion | flops 4228374528 | bytes 14139392 | tf_op jit(solution)/shard_map/dot_general | solution.py:145
  171.0 2.5 %collective-permute-done.27 = bf16[1,112,1664]{2,1,0:T(8,128)(2,1)S(1)} collective-permute-done((bf16[1,112,1664]{2,1,0:T(8,128)(2,1)S(1)}, bf16[1,112,1664]{2,1,0:T(8,128)(2,1)S(1)}, u32[]{:S(2)}, u32[]{:S(2)}) %collective-permute-start.27) | collective-permute-done | bytes 372768 | tf_op jit(solution)/shard_map/ppermute | solution.py:93
  174.5 4.3 %fusion.46 = bf16[448,512]{1,0:T(8,128)(2,1)S(1)} fusion(bf16[448,4096]{1,0:T(8,128)(2,1)S(1)} %bitcast.229, bf16[4096,3328]{1,0:T(8,128)(2,1)} %param.14), kind=kOutput, calls=%fused_computation.45 | convolution fusion | flops 1879277568 | bytes 8323072 | tf_op jit(solution)/shard_map/dot_general | solution.py:145
  182.1 4.5 %collective-permute-done.33 = bf16[1,112,512]{2,1,0:T(8,128)(2,1)S(1)} collective-permute-done((bf16[1,112,512]{2,1,0:T(8,128)(2,1)S(1)}, bf16[1,112,512]{2,1,0:T(8,128)(2,1)S(1)}, u32[]{:S(2)}, u32[]{:S(2)}) %collective-permute-start.33) | collective-permute-done | bytes 114720 | tf_op jit(solution)/shard_map/ppermute | solution.py:93
  187.5 6.7 %collective-permute-done.31 = bf16[1,112,1152]{2,1,0:T(8,128)(2,1)S(1)} collective-permute-done((bf16[1,112,1152]{2,1,0:T(8,128)(2,1)S(1)}, bf16[1,112,1152]{2,1,0:T(8,128)(2,1)S(1)}, u32[]{:S(2)}, u32[]{:S(2)}) %collective-permute-start.31) | collective-permute-done | bytes 258080 | tf_op jit(solution)/shard_map/ppermute | solution.py:93
  194.6 2.2 %fusion.18 = bf16[256,3328]{1,0:T(8,128)(2,1)} fusion(f32[2,128,3328]{2,1,0:T(8,128)S(1)} %maximum_maximum_fusion, f32[2,128,3328]{2,1,0:T(8,128)S(1)} %pad_maximum_fusion), kind=kLoop, calls=%fused_computation.21 | loop fusion | flops 5111808 | bytes 8519680 | tf_op jit(solution)/shard_map/convert_element_type | solution.py:190
  (125 shorter events, 29.0 us)
Async XLA Ops:
  1.2 24.4 %collective-permute-start = (bf16[72,4096]{1,0:T(8,128)(2,1)S(1)}, bf16[72,4096]{1,0:T(8,128)(2,1)S(1)}, u32[]{:S(2)}, u32[]{:S(2)}) collective-permute-start(bf16[72,4096]{1,0:T(8,128)(2,1)S(1)} %slice.39), channel_id=1, source_target_pairs={{0,2},{2,4},{4,6},{6,7},{7,5},{5,3},{3,1},{1,0},{8,10},{10,12},{12... | collective-permute-start | bytes 1769480 | tf_op jit(solution)/shard_map/ppermute | solution.py:74
  4.3 23.4 %collective-permute-start.1 = (bf16[72,4096]{1,0:T(8,128)(2,1)S(1)}, bf16[72,4096]{1,0:T(8,128)(2,1)S(1)}, u32[]{:S(2)}, u32[]{:S(2)}) collective-permute-start(bf16[72,4096]{1,0:T(8,128)(2,1)S(1)} %slice.39), channel_id=1, source_target_pairs={{0,1},{2,0},{4,2},{6,4},{7,6},{5,7},{3,5},{1,3},{8,9},{10,8},{12,1... | collective-permute-start | bytes 1769480 | tf_op jit(solution)/shard_map/ppermute | solution.py:77
  25.6 14.8 %collective-permute-start.2 = (bf16[72,4096]{1,0:T(8,128)(2,1)S(1)}, bf16[72,4096]{1,0:T(8,128)(2,1)S(1)}, u32[]{:S(2)}, u32[]{:S(2)}) collective-permute-start(bf16[72,4096]{1,0:T(8,128)(2,1)S(1)} %collective-permute-done), channel_id=1, source_target_pairs={{0,2},{2,4},{4,6},{6,7},{7,5},{5,3},{3,1},{1,0},{8,10},{10,12},{12... | collective-permute-start | bytes 1769480 | tf_op jit(solution)/shard_map/ppermute | solution.py:74
  27.7 14.5 %collective-permute-start.3 = (bf16[72,4096]{1,0:T(8,128)(2,1)S(1)}, bf16[72,4096]{1,0:T(8,128)(2,1)S(1)}, u32[]{:S(2)}, u32[]{:S(2)}) collective-permute-start(bf16[72,4096]{1,0:T(8,128)(2,1)S(1)} %collective-permute-done.1), channel_id=1, source_target_pairs={{0,1},{2,0},{4,2},{6,4},{7,6},{5,7},{3,5},{1,3},{8,9},{10,8},{12,1... | collective-permute-start | bytes 1769480 | tf_op jit(solution)/shard_map/ppermute | solution.py:77
  40.4 13.9 %collective-permute-start.4 = (bf16[72,4096]{1,0:T(8,128)(2,1)S(1)}, bf16[72,4096]{1,0:T(8,128)(2,1)S(1)}, u32[]{:S(2)}, u32[]{:S(2)}) collective-permute-start(bf16[72,4096]{1,0:T(8,128)(2,1)S(1)} %collective-permute-done.2), channel_id=1, source_target_pairs={{0,2},{2,4},{4,6},{6,7},{7,5},{5,3},{3,1},{1,0},{8,10},{10,12},{12... | collective-permute-start | bytes 1769480 | tf_op jit(solution)/shard_map/ppermute | solution.py:74
  42.2 13.7 %collective-permute-start.5 = (bf16[72,4096]{1,0:T(8,128)(2,1)S(1)}, bf16[72,4096]{1,0:T(8,128)(2,1)S(1)}, u32[]{:S(2)}, u32[]{:S(2)}) collective-permute-start(bf16[72,4096]{1,0:T(8,128)(2,1)S(1)} %collective-permute-done.3), channel_id=1, source_target_pairs={{0,1},{2,0},{4,2},{6,4},{7,6},{5,7},{3,5},{1,3},{8,9},{10,8},{12,1... | collective-permute-start | bytes 1769480 | tf_op jit(solution)/shard_map/ppermute | solution.py:77
  62.8 14.6 %collective-permute-start.9 = (bf16[56,4096]{1,0:T(8,128)(2,1)S(1)}, bf16[56,4096]{1,0:T(8,128)(2,1)S(1)}, u32[]{:S(2)}, u32[]{:S(2)}) collective-permute-start(bf16[56,4096]{1,0:T(8,128)(2,1)S(1)} %slice.43), channel_id=1, source_target_pairs={{0,2},{2,4},{4,6},{6,7},{7,5},{5,3},{3,1},{1,0},{8,10},{10,12},{12... | collective-permute-start | bytes 1376264 | tf_op jit(solution)/shard_map/ppermute | solution.py:74
  64.4 13.0 %collective-permute-start.8 = (bf16[56,4096]{1,0:T(8,128)(2,1)S(1)}, bf16[56,4096]{1,0:T(8,128)(2,1)S(1)}, u32[]{:S(2)}, u32[]{:S(2)}) collective-permute-start(bf16[56,4096]{1,0:T(8,128)(2,1)S(1)} %slice.43), channel_id=1, source_target_pairs={{0,1},{2,0},{4,2},{6,4},{7,6},{5,7},{3,5},{1,3},{8,9},{10,8},{12,1... | collective-permute-start | bytes 1376264 | tf_op jit(solution)/shard_map/ppermute | solution.py:77
  77.5 14.3 %collective-permute-start.11 = (bf16[56,4096]{1,0:T(8,128)(2,1)S(1)}, bf16[56,4096]{1,0:T(8,128)(2,1)S(1)}, u32[]{:S(2)}, u32[]{:S(2)}) collective-permute-start(bf16[56,4096]{1,0:T(8,128)(2,1)S(1)} %collective-permute-done.8), channel_id=1, source_target_pairs={{0,1},{2,0},{4,2},{6,4},{7,6},{5,7},{3,5},{1,3},{8,9},{10,8},{12,1... | collective-permute-start | bytes 1376264 | tf_op jit(solution)/shard_map/ppermute | solution.py:77
  78.1 13.7 %collective-permute-start.12 = (bf16[56,4096]{1,0:T(8,128)(2,1)S(1)}, bf16[56,4096]{1,0:T(8,128)(2,1)S(1)}, u32[]{:S(2)}, u32[]{:S(2)}) collective-permute-start(bf16[56,4096]{1,0:T(8,128)(2,1)S(1)} %collective-permute-done.9), channel_id=1, source_target_pairs={{0,2},{2,4},{4,6},{6,7},{7,5},{5,3},{3,1},{1,0},{8,10},{10,12},{12... | collective-permute-start | bytes 1376264 | tf_op jit(solution)/shard_map/ppermute | solution.py:74
  79.6 12.2 %collective-permute-start.10 = (bf16[2,144,1664]{2,1,0:T(8,128)(2,1)S(1)}, bf16[2,144,1664]{2,1,0:T(8,128)(2,1)S(1)}, u32[]{:S(2)}, u32[]{:S(2)}) collective-permute-start(bf16[2,144,1664]{2,1,0:T(8,128)(2,1)S(1)} %dynamic-slice_bitcast_fusion.3), channel_id=1, source_target_pairs={{0,8},{8,0},{16,24},{24,16},{1,9},{9,1},{17,25},{25,17},{2,10},{10... | collective-permute-start | bytes 2875400 | tf_op jit(solution)/shard_map/ppermute | solution.py:93
  92.1 16.0 %collective-permute-start.15 = (bf16[56,4096]{1,0:T(8,128)(2,1)S(1)}, bf16[56,4096]{1,0:T(8,128)(2,1)S(1)}, u32[]{:S(2)}, u32[]{:S(2)}) collective-permute-start(bf16[56,4096]{1,0:T(8,128)(2,1)S(1)} %collective-permute-done.11), channel_id=1, source_target_pairs={{0,1},{2,0},{4,2},{6,4},{7,6},{5,7},{3,5},{1,3},{8,9},{10,8},{12,1... | collective-permute-start | bytes 1376264 | tf_op jit(solution)/shard_map/ppermute | solution.py:77
  92.7 15.3 %collective-permute-start.16 = (bf16[56,4096]{1,0:T(8,128)(2,1)S(1)}, bf16[56,4096]{1,0:T(8,128)(2,1)S(1)}, u32[]{:S(2)}, u32[]{:S(2)}) collective-permute-start(bf16[56,4096]{1,0:T(8,128)(2,1)S(1)} %collective-permute-done.12), channel_id=1, source_target_pairs={{0,2},{2,4},{4,6},{6,7},{7,5},{5,3},{3,1},{1,0},{8,10},{10,12},{12... | collective-permute-start | bytes 1376264 | tf_op jit(solution)/shard_map/ppermute | solution.py:74
  94.2 13.9 %collective-permute-start.13 = (bf16[1,144,1664]{2,1,0:T(8,128)(2,1)S(1)}, bf16[1,144,1664]{2,1,0:T(8,128)(2,1)S(1)}, u32[]{:S(2)}, u32[]{:S(2)}) collective-permute-start(bf16[1,144,1664]{2,1,0:T(8,128)(2,1)S(1)} %fusion.55), channel_id=1, source_target_pairs={{0,16},{8,24},{16,0},{24,8},{1,17},{9,25},{17,1},{25,9},{2,18},{10... | collective-permute-start | bytes 1437704 | tf_op jit(solution)/shard_map/ppermute | solution.py:93
  95.9 12.3 %collective-permute-start.14 = (bf16[2,144,1664]{2,1,0:T(8,128)(2,1)S(1)}, bf16[2,144,1664]{2,1,0:T(8,128)(2,1)S(1)}, u32[]{:S(2)}, u32[]{:S(2)}) collective-permute-start(bf16[2,144,1664]{2,1,0:T(8,128)(2,1)S(1)} %dynamic-slice_bitcast_fusion.2), channel_id=1, source_target_pairs={{0,8},{8,0},{16,24},{24,16},{1,9},{9,1},{17,25},{25,17},{2,10},{10... | collective-permute-start | bytes 2875400 | tf_op jit(solution)/shard_map/ppermute | solution.py:93
  108.5 15.0 %collective-permute-start.20 = (bf16[56,2048]{1,0:T(8,128)(2,1)S(1)}, bf16[56,2048]{1,0:T(8,128)(2,1)S(1)}, u32[]{:S(2)}, u32[]{:S(2)}) collective-permute-start(bf16[56,2048]{1,0:T(8,128)(2,1)S(1)} %slice.48), channel_id=1, source_target_pairs={{0,2},{2,4},{4,6},{6,7},{7,5},{5,3},{3,1},{1,0},{8,10},{10,12},{12... | collective-permute-start | bytes 688136 | tf_op jit(solution)/shard_map/ppermute | solution.py:68
  110.2 13.3 %collective-permute-start.19 = (bf16[56,2048]{1,0:T(8,128)(2,1)S(1)}, bf16[56,2048]{1,0:T(8,128)(2,1)S(1)}, u32[]{:S(2)}, u32[]{:S(2)}) collective-permute-start(bf16[56,2048]{1,0:T(8,128)(2,1)S(1)} %slice.47), channel_id=1, source_target_pairs={{0,1},{2,0},{4,2},{6,4},{7,6},{5,7},{3,5},{1,3},{8,9},{10,8},{12,1... | collective-permute-start | bytes 688136 | tf_op jit(solution)/shard_map/ppermute | solution.py:69
  110.6 13.0 %collective-permute-start.17 = (bf16[1,144,1664]{2,1,0:T(8,128)(2,1)S(1)}, bf16[1,144,1664]{2,1,0:T(8,128)(2,1)S(1)}, u32[]{:S(2)}, u32[]{:S(2)}) collective-permute-start(bf16[1,144,1664]{2,1,0:T(8,128)(2,1)S(1)} %fusion.56), channel_id=1, source_target_pairs={{0,16},{8,24},{16,0},{24,8},{1,17},{9,25},{17,1},{25,9},{2,18},{10... | collective-permute-start | bytes 1437704 | tf_op jit(solution)/shard_map/ppermute | solution.py:93
  111.3 12.4 %collective-permute-start.18 = (bf16[2,144,1664]{2,1,0:T(8,128)(2,1)S(1)}, bf16[2,144,1664]{2,1,0:T(8,128)(2,1)S(1)}, u32[]{:S(2)}, u32[]{:S(2)}) collective-permute-start(bf16[2,144,1664]{2,1,0:T(8,128)(2,1)S(1)} %dynamic-slice_bitcast_fusion.1), channel_id=1, source_target_pairs={{0,8},{8,0},{16,24},{24,16},{1,9},{9,1},{17,25},{25,17},{2,10},{10... | collective-permute-start | bytes 2875400 | tf_op jit(solution)/shard_map/ppermute | solution.py:93
  124.0 13.5 %collective-permute-start.21 = (bf16[1,144,1664]{2,1,0:T(8,128)(2,1)S(1)}, bf16[1,144,1664]{2,1,0:T(8,128)(2,1)S(1)}, u32[]{:S(2)}, u32[]{:S(2)}) collective-permute-start(bf16[1,144,1664]{2,1,0:T(8,128)(2,1)S(1)} %fusion.57), channel_id=1, source_target_pairs={{0,16},{8,24},{16,0},{24,8},{1,17},{9,25},{17,1},{25,9},{2,18},{10... | collective-permute-start | bytes 1437704 | tf_op jit(solution)/shard_map/ppermute | solution.py:93
  125.6 12.0 %collective-permute-start.22 = (bf16[2,144,1664]{2,1,0:T(8,128)(2,1)S(1)}, bf16[2,144,1664]{2,1,0:T(8,128)(2,1)S(1)}, u32[]{:S(2)}, u32[]{:S(2)}) collective-permute-start(bf16[2,144,1664]{2,1,0:T(8,128)(2,1)S(1)} %dynamic-slice_bitcast_fusion), channel_id=1, source_target_pairs={{0,8},{8,0},{16,24},{24,16},{1,9},{9,1},{17,25},{25,17},{2,10},{10... | collective-permute-start | bytes 2875400 | tf_op jit(solution)/shard_map/ppermute | solution.py:93
  137.9 12.6 %collective-permute-start.23 = (bf16[1,144,1664]{2,1,0:T(8,128)(2,1)S(1)}, bf16[1,144,1664]{2,1,0:T(8,128)(2,1)S(1)}, u32[]{:S(2)}, u32[]{:S(2)}) collective-permute-start(bf16[1,144,1664]{2,1,0:T(8,128)(2,1)S(1)} %fusion.58), channel_id=1, source_target_pairs={{0,16},{8,24},{16,0},{24,8},{1,17},{9,25},{17,1},{25,9},{2,18},{10... | collective-permute-start | bytes 1437704 | tf_op jit(solution)/shard_map/ppermute | solution.py:93
  150.8 11.3 %collective-permute-start.25 = (bf16[1,112,1664]{2,1,0:T(8,128)(2,1)S(1)}, bf16[1,112,1664]{2,1,0:T(8,128)(2,1)S(1)}, u32[]{:S(2)}, u32[]{:S(2)}) collective-permute-start(bf16[1,112,1664]{2,1,0:T(8,128)(2,1)S(1)} %fusion.59), channel_id=1, source_target_pairs={{0,16},{8,24},{16,0},{24,8},{1,17},{9,25},{17,1},{25,9},{2,18},{10... | collective-permute-start | bytes 1118216 | tf_op jit(solution)/shard_map/ppermute | solution.py:93
  173.8 13.6 %collective-permute-start.29 = (bf16[1,112,1664]{2,1,0:T(8,128)(2,1)S(1)}, bf16[1,112,1664]{2,1,0:T(8,128)(2,1)S(1)}, u32[]{:S(2)}, u32[]{:S(2)}) collective-permute-start(bf16[1,112,1664]{2,1,0:T(8,128)(2,1)S(1)} %fusion.61), channel_id=1, source_target_pairs={{0,16},{8,24},{16,0},{24,8},{1,17},{9,25},{17,1},{25,9},{2,18},{10... | collective-permute-start | bytes 1118216 | tf_op jit(solution)/shard_map/ppermute | solution.py:93
  (11 other events, 104.4 us)
